TPU v7x, 32 devices: a whole 2x2x4 slice. The times are simulated.
32 devices in a mesh: dp: 8 (over y, x, core), tensor: 4 (over z).
Axes of the slice: x: 2, y: 2, z: 4, core: 2. Of those that a mesh axis runs over, the one named last changes fastest.
Arguments:
- grad_out: bfloat16 [2048, 4096], P('dp'), may hold values from -1.5 to 1.5
- gate_input: bfloat16 [2048, 14336], P('dp', 'tensor'), may hold values from -6 to 6
- up_input: bfloat16 [2048, 14336], P('dp', 'tensor'), may hold values from -6 to 6
- next_hidden: bfloat16 [2048, 14336], P('dp', 'tensor'), may hold values from -6 to 6
- down_weight: bfloat16 [4096, 14336], P(None, 'tensor'), may hold values from -0.046875 to 0.046875
- first_moment: float32 [4096, 14336], P('dp', 'tensor'), may hold values from -48 to 48
- second_moment: float32 [4096, 14336], P('dp', 'tensor'), may hold values from 10 to 200
Outputs:
- gate_grad: bfloat16 [2048, 14336], P('dp', 'tensor')
- up_grad: bfloat16 [2048, 14336], P('dp', 'tensor')
- moment_one: float32 [4096, 14336], P('dp', 'tensor')
- moment_two: float32 [4096, 14336], P('dp', 'tensor')
- next_out: bfloat16 [2048, 4096], P('dp', 'tensor')
All inputs are finite; a program needn't handle non-finite values.
Results may differ from a plain program's by a relative error of at most 0.004.
The roundings to bfloat16 on the way count: a program that leaves them out, or rounds other values in their place, can miss the bound.
Values may be sent and summed in bfloat16 or wider, within the bound.
No kernel may reach another device: no remote copies, remote signals or barrier semaphores. Data moves between devices by JAX's collectives and lax.ppermute only.
A program may use at most 256 MiB of HBM per device.

v0:
```python
import jax
import jax.numpy as jnp
from jax import lax
from jax.sharding import PartitionSpec as P

STEP = 20


beta_one = 0.9
beta_two = 0.95
learn_rate = 0.001
decay_rate = 0.1
epsilon = 1e-08


def shards(grad_out, gate_input, up_input, next_hidden, down_weight, first_moment, second_moment):
    gate_value = gate_input.astype(jnp.float32)
    up_value = up_input.astype(jnp.float32)
    sigmoid_gate = jax.nn.sigmoid(gate_value)
    activated = gate_value * sigmoid_gate
    hidden = (activated * up_value).astype(jnp.bfloat16)
    owned_rows = first_moment.shape[0]
    weight_grad = lax.psum_scatter(
        lax.dot_general(
            grad_out, hidden, (((0,), (0,)), ((), ())), preferred_element_type=jnp.float32
        ).astype(jnp.bfloat16),
        "dp",
        scatter_dimension=0,
        tiled=True,
    ).astype(jnp.float32)
    grad_hidden = jnp.dot(grad_out, down_weight, preferred_element_type=jnp.float32)
    gate_grad = (
        grad_hidden * up_value * sigmoid_gate * (1.0 + gate_value * (1.0 - sigmoid_gate))
    ).astype(jnp.bfloat16)
    up_grad = (grad_hidden * activated).astype(jnp.bfloat16)
    moment_one = beta_one * first_moment + (1.0 - beta_one) * weight_grad
    moment_two = beta_two * second_moment + (1.0 - beta_two) * weight_grad * weight_grad
    corrected_one = moment_one / (1.0 - beta_one**STEP)
    corrected_two = moment_two / (1.0 - beta_two**STEP)
    old_shard = lax.dynamic_slice_in_dim(
        down_weight, lax.axis_index("dp") * owned_rows, owned_rows, 0
    ).astype(jnp.float32)
    new_shard = (
        old_shard
        - learn_rate
        * (corrected_one / (jnp.sqrt(corrected_two) + epsilon) + decay_rate * old_shard)
    ).astype(jnp.bfloat16)
    partial_out = lax.dot_general(
        next_hidden,
        lax.all_gather(new_shard, "dp", axis=0, tiled=True),
        (((1,), (1,)), ((), ())),
        preferred_element_type=jnp.float32,
    )
    next_out = lax.psum_scatter(partial_out, "tensor", scatter_dimension=1, tiled=True).astype(
        jnp.bfloat16
    )
    return (gate_grad, up_grad, moment_one, moment_two, next_out)


def solution(mesh):
    placed = (
        P("dp", None),
        P("dp", "tensor"),
        P("dp", "tensor"),
        P("dp", "tensor"),
        P(None, "tensor"),
        P("dp", "tensor"),
        P("dp", "tensor"),
    )
    return jax.shard_map(
        shards,
        mesh=mesh,
        in_specs=placed,
        out_specs=(
            P("dp", "tensor"),
            P("dp", "tensor"),
            P("dp", "tensor"),
            P("dp", "tensor"),
            P("dp", "tensor"),
        ),
        check_vma=False,
    )
```

profile of v0, /device:TPU:3, one launch (start us, length us, event | category | flops | bytes accessed | tf_op | source)
XLA Modules:
  0.0 469.8 jit_solution(2198838861264233746)
XLA Ops:
  7.2 0.0 copy-start
  7.2 0.0 reduce-scatter.3.cloned.1.call-start
  7.2 1.5 copy-done
  8.8 15.6 %fusion = bf16[4096,3584]{0,1:T(8,128)(2,1)} fusion(bf16[256,4096]{1,0:T(8,128)(2,1)S(1)} %copy-done, bf16[256,3584]{1,0:T(8,128)(2,1)} %param.9, bf16[256,3584]{1,0:T(8,128)(2,1)} %param.8), kind=kOutput, calls=%fused_computation.1 | convolution fusion | flops 7538212864 | bytes 35127296 | tf_op jit(solution)/shard_map/dot_general | solution.py:24
  24.4 0.0 reduce-scatter.3.cloned.1.call-update
  24.4 0.0 all-gather.2.cloned.1.call-start
  24.4 4.1 constant_dynamic-slice_fusion
  28.6 5.9 %copy.18 = bf16[512,3584]{0,1:T(8,128)(2,1)} copy(bf16[512,3584]{1,0:T(8,128)(2,1)} %constant_dynamic-slice_fusion) | data formatting | bytes 7340032
  34.5 9.3 %copy.12 = f32[512,3584]{0,1:T(8,128)} copy(f32[512,3584]{1,0:T(8,128)} %param.12) | data formatting | bytes 14680064 | tf_op args[5]
  43.8 9.4 %copy.13 = f32[512,3584]{0,1:T(8,128)} copy(f32[512,3584]{1,0:T(8,128)} %param.13) | data formatting | bytes 14680064 | tf_op args[6]
  53.2 151.1 %reduce-scatter.3.cloned.1.call-done = bf16[512,3584]{0,1:T(8,128)(2,1)} async-done(((bf16[4096,3584]{0,1:T(8,128)(2,1)}), bf16[512,3584]{0,1:T(8,128)(2,1)}) %reduce-scatter.3.cloned.1.call-update) | async-done | bytes 3670032 | tf_op jit(solution)/shard_map/reduce_scatter | solution.py:23
  204.3 14.8 %fusion.4 = (bf16[512,3584]{0,1:T(8,128)(2,1)}, f32[512,3584]{0,1:T(8,128)}, f32[512,3584]{0,1:T(8,128)}) fusion(bf16[512,3584]{0,1:T(8,128)(2,1)} %copy.18, bf16[512,3584]{0,1:T(8,128)(2,1)} %reduce-scatter.3.cloned.1.call-done, f32[512,3584]{0,1:T(8,128)} %copy.13, f32[512,3584]{0,1:T(8,128)} %copy.12), kind=kLoop, calls=%fused_computation.9 | loop fusion | flops 33030144 | bytes 40370176 | tf_op jit(solution)/shard_map/convert_element_type | solution.py:47
  219.1 0.0 all-gather.2.cloned.1.call-update
  219.2 0.2 reduce-scatter.5.cloned.1.call-start
  219.4 149.4 %all-gather.2.cloned.1.call-done = bf16[4096,3584]{0,1:T(8,128)(2,1)} async-done(((bf16[512,3584]{0,1:T(8,128)(2,1)}), bf16[4096,3584]{0,1:T(8,128)(2,1)}) %all-gather.2.cloned.1.call-update) | async-done | bytes 29360144 | tf_op jit(solution)/shard_map/all_gather | solution.py:50
  368.8 15.7 %convolution_bitcast_fusion = f32[256,4096]{0,1:T(8,128)} fusion(bf16[4096,3584]{0,1:T(8,128)(2,1)} %all-gather.2.cloned.1.call-done, bf16[256,3584]{1,0:T(8,128)(2,1)} %param.10), kind=kOutput, calls=%fused_computation.14 | convolution fusion | flops 7516192768 | bytes 35389440 | tf_op jit(solution)/shard_map/dot_general | solution.py:48
  384.4 0.0 reduce-scatter.5.cloned.1.call-update
  384.4 17.2 %multiply_convert_fusion = (bf16[256,3584]{1,0:T(8,128)(2,1)}, bf16[256,3584]{1,0:T(8,128)(2,1)}) fusion(bf16[256,3584]{1,0:T(8,128)(2,1)} %param.8, bf16[256,3584]{1,0:T(8,128)(2,1)} %param.9, bf16[256,4096]{1,0:T(8,128)(2,1)S(1)} %copy-done, bf16[4096,3584]{1,0:T(8,128)(2,1)} %param.11), kind=kOutput, calls=%fused_computation.25 | convolution fusion | flops 7529955328 | bytes 38797312 | tf_op jit(solution)/shard_map/dot_general | solution.py:31
  401.7 8.4 %copy.15 = f32[512,3584]{1,0:T(8,128)} copy(f32[512,3584]{0,1:T(8,128)} %get-tuple-element.12) | data formatting | bytes 14680064
  410.0 8.4 %copy.16 = f32[512,3584]{1,0:T(8,128)} copy(f32[512,3584]{0,1:T(8,128)} %get-tuple-element.11) | data formatting | bytes 14680064
  418.4 42.5 %reduce-scatter.5.cloned.1.call-done = f32[256,1024]{0,1:T(8,128)} async-done(((f32[256,4096]{0,1:T(8,128)}), f32[256,1024]{0,1:T(8,128)}) %reduce-scatter.5.cloned.1.call-update) | async-done | bytes 1048592 | tf_op jit(solution)/shard_map/reduce_scatter | solution.py:54
  461.0 1.3 convert_element_type.43
  462.2 1.0 copy.17
Async XLA Ops:
  7.2 1.6 copy-start
  7.2 197.2 %reduce-scatter.3.cloned.1.call-start = ((), (), s32[]{:S(2)}) async-start(), calls=%async_computation.2 | async-start | bytes 33030144 | tf_op jit(solution)/shard_map/reduce_scatter | solution.py:23
  24.4 344.4 %all-gather.2.cloned.1.call-start = ((), (), s32[]{:S(2)}) async-start(), calls=%async_computation.3 | async-start | bytes 33030144 | tf_op jit(solution)/shard_map/all_gather | solution.py:50
  219.2 241.8 %reduce-scatter.5.cloned.1.call-start = ((), (), s32[]{:S(2)}) async-start(), calls=%async_computation.4 | async-start | bytes 5242880 | tf_op jit(solution)/shard_map/reduce_scatter | solution.py:54
Sparse Core Ops, SparseCore 0:
  24.5 179.8 reduce-scatter.2
  219.3 149.4 all-gather.1
  384.6 76.3 reduce-scatter.4
where the time goes:
time: 472 us; the launch traced here: 470 us
  waiting for transfers between devices  343 us (73%)
  matrix products  48.5 us (10%)
  local copies, waits for them, and re-layouts  48.1 us (10%)
  other arithmetic  16.1 us (3%)
  between operations  13.8 us (3%)
    reduce_scatter x1, waiting for transfers between devices, shards(): lax.psum_scatter(lax.dot_general(grad_out, hidden, (((0,), (0,)), ((), ()...  151 us
    all_gather x1, waiting for transfers between devices, shards(): lax.all_gather(new_shard, 'dp', axis=0, tiled=True)  149 us
    unnamed x8, local copies, waits for them, and re-layouts  44 us
    reduce_scatter x1, waiting for transfers between devices, shards(): lax.psum_scatter(partial_out, 'tensor', scatter_dimension=1, tiled=True)  42.5 us
    dot_general x1, matrix products, shards(): jnp.dot(grad_out, down_weight, preferred_element_type=jnp.float32)  17.2 us
    dot_general x1, matrix products, shards(): lax.dot_general(next_hidden, lax.all_gather(new_shard, 'dp', axis=0, tile...  15.7 us
    dot_general x1, matrix products, shards(): lax.dot_general(grad_out, hidden, (((0,), (0,)), ((), ())), preferred_ele...  15.6 us
    convert_element_type x1, other arithmetic, shards(): new_shard = (old_shard - learn_rate * (corrected_one / (jnp.sqrt(correcte...  14.8 us
  transfers between devices with their start and end apart: 3, of which 3 were waited for; matrix products, arithmetic and copies ran while one was open for 13% of the time, Pallas kernels for 0%

commit v1 on v0

v1 whole, which is shorter than its diff:
```python
import jax
import jax.numpy as jnp
from jax import lax
from jax.sharding import PartitionSpec as P

STEP = 20


beta_one = 0.9
beta_two = 0.95
learn_rate = 0.001
decay_rate = 0.1
epsilon = 1e-08


def shards(grad_out, gate_input, up_input, next_hidden, down_weight, first_moment, second_moment):
    n_dp = lax.axis_size("dp")
    n_t = lax.axis_size("tensor")
    me = lax.axis_index("dp")
    col = lax.axis_index("tensor")
    tok = grad_out.shape[0]
    owned_rows = first_moment.shape[0]
    group = n_dp // n_t

    gate_value = gate_input.astype(jnp.float32)
    up_value = up_input.astype(jnp.float32)
    sigmoid_gate = jax.nn.sigmoid(gate_value)
    activated = gate_value * sigmoid_gate
    hidden = (activated * up_value).astype(jnp.bfloat16)

    hidden_all = lax.all_gather(hidden, "dp", axis=0, tiled=True)
    next_all = lax.all_gather(next_hidden, "dp", axis=0, tiled=True)
    grad_rows = lax.all_to_all(grad_out, "dp", 1, 0, tiled=True)

    grad_hidden = jnp.dot(grad_out, down_weight, preferred_element_type=jnp.float32)
    gate_grad = (
        grad_hidden * up_value * sigmoid_gate * (1.0 + gate_value * (1.0 - sigmoid_gate))
    ).astype(jnp.bfloat16)
    up_grad = (grad_hidden * activated).astype(jnp.bfloat16)

    weight_grad = jnp.zeros((owned_rows, hidden.shape[1]), jnp.float32)
    for b in range(n_dp):
        block = lax.dot_general(
            grad_rows[b * tok : (b + 1) * tok],
            hidden_all[b * tok : (b + 1) * tok],
            (((0,), (0,)), ((), ())),
            preferred_element_type=jnp.float32,
        ).astype(jnp.bfloat16)
        weight_grad = weight_grad + block.astype(jnp.float32)

    moment_one = beta_one * first_moment + (1.0 - beta_one) * weight_grad
    moment_two = beta_two * second_moment + (1.0 - beta_two) * weight_grad * weight_grad
    corrected_one = moment_one / (1.0 - beta_one**STEP)
    corrected_two = moment_two / (1.0 - beta_two**STEP)
    old_shard = lax.dynamic_slice_in_dim(down_weight, me * owned_rows, owned_rows, 0).astype(
        jnp.float32
    )
    new_shard = (
        old_shard
        - learn_rate
        * (corrected_one / (jnp.sqrt(corrected_two) + epsilon) + decay_rate * old_shard)
    ).astype(jnp.bfloat16)

    partial_out = lax.dot_general(
        next_all, new_shard, (((1,), (1,)), ((), ())), preferred_element_type=jnp.float32
    )
    summed = lax.psum_scatter(partial_out, "tensor", scatter_dimension=0, tiled=True).astype(
        jnp.bfloat16
    )
    sub = me % group
    pieces = []
    for k in range(group):
        s = (sub + k) % group
        piece = lax.dynamic_slice_in_dim(summed, s * tok, tok, 0)
        perm = []
        for i in range(n_dp):
            for j in range(n_t):
                si = (i % group + k) % group
                dst = (group * j + si) * n_t + i // group
                perm.append((i * n_t + j, dst))
        pieces.append(lax.ppermute(piece, ("dp", "tensor"), perm))
    ordered = []
    for r in range(group):
        chosen = pieces[0]
        for k in range(1, group):
            chosen = jnp.where((sub - k) % group == r, pieces[k], chosen)
        ordered.append(chosen)
    next_out = jnp.concatenate(ordered, axis=1)
    return (gate_grad, up_grad, moment_one, moment_two, next_out)


def solution(mesh):
    n_dp = mesh.shape["dp"]
    n_t = mesh.shape["tensor"]
    if n_dp % n_t:
        raise ValueError("bad mesh")
    placed = (
        P("dp", None),
        P("dp", "tensor"),
        P("dp", "tensor"),
        P("dp", "tensor"),
        P(None, "tensor"),
        P("dp", "tensor"),
        P("dp", "tensor"),
    )
    return jax.shard_map(
        shards,
        mesh=mesh,
        in_specs=placed,
        out_specs=(
            P("dp", "tensor"),
            P("dp", "tensor"),
            P("dp", "tensor"),
            P("dp", "tensor"),
            P("dp", "tensor"),
        ),
        check_vma=False,
    )
```

time: 472 us -> 364 us (0.77)
  waiting for transfers between devices: 343 us -> 198 us
  matrix products: 48.5 us -> 92 us
  other arithmetic: 16.1 us -> 1.37 us
  starting transfers between devices: 0.3 us -> 9.51 us
    reduce_scatter x2 -> x1, waiting for transfers between devices: 194 us -> 76.5 us  [shards(): lax.psum_scatter(partial_out, 'tensor', scatter_dimension=0, tiled=True)]
    all_gather x1 -> x2, waiting for transfers between devices: 149 us -> 89.7 us  [the longest x1 52.1 us: shards(): hidden_all = lax.all_gather(hidden, 'dp', axis=0, tiled=True)]
    dot_general x2 -> x9, matrix products: 31.2 us -> 70.6 us  [the longest x8 45.3 us: shards(): lax.dot_general(grad_rows[b * tok:(b + 1) * tok], hidden_all[b * tok:(b +...]
    ppermute x0 -> x2, waiting for transfers between devices: none -> 16.2 us  [shards(): pieces.append(lax.ppermute(piece, ('dp', 'tensor'), perm))]
    all_to_all x0 -> x1, waiting for transfers between devices: none -> 15.2 us  [shards(): grad_rows = lax.all_to_all(grad_out, 'dp', 1, 0, tiled=True)]
    convert_element_type x2 -> x1, other arithmetic: 16.1 us -> 1.29 us  [shards(): lax.psum_scatter(partial_out, 'tensor', scatter_dimension=0, tiled=True)]
    ppermute x0 -> x2, starting transfers between devices: none -> 4.86 us  [shards(): pieces.append(lax.ppermute(piece, ('dp', 'tensor'), perm))]
    unnamed x8 -> x11, local copies, waits for them, and re-layouts: 44 us -> 44.2 us
  transfers between devices with their start and end apart: 3 -> 6, of which waited for: 3 -> 6; matrix products, arithmetic and copies ran while one was open for 13% -> 25% of each run, Pallas kernels for 0% -> 0%
where the time goes in v1:
time: 364 us; the launch traced here: 363 us
  waiting for transfers between devices  198 us (54%)
  matrix products  92 us (25%)
  local copies, waits for them, and re-layouts  48.3 us (13%)
  between operations  13.8 us (4%)
  starting transfers between devices  9.51 us (3%)
    reduce_scatter x1, waiting for transfers between devices, shards(): lax.psum_scatter(partial_out, 'tensor', scatter_dimension=0, tiled=True)  76.5 us
    all_gather x1, waiting for transfers between devices, shards(): hidden_all = lax.all_gather(hidden, 'dp', axis=0, tiled=True)  52.1 us
    dot_general x8, matrix products, shards(): lax.dot_general(grad_rows[b * tok:(b + 1) * tok], hidden_all[b * tok:(b +...  45.3 us
    unnamed x11, local copies, waits for them, and re-layouts  44.2 us
    all_gather x1, waiting for transfers between devices, shards(): next_all = lax.all_gather(next_hidden, 'dp', axis=0, tiled=True)  37.6 us
    dot_general x1, matrix products, shards(): lax.dot_general(next_all, new_shard, (((1,), (1,)), ((), ())), preferred_...  25.4 us
    dot_general x1, matrix products, shards(): jnp.dot(grad_out, down_weight, preferred_element_type=jnp.float32)  21.4 us
    ppermute x2, waiting for transfers between devices, shards(): pieces.append(lax.ppermute(piece, ('dp', 'tensor'), perm))  16.2 us
  transfers between devices with their start and end apart: 6, of which 6 were waited for; matrix products, arithmetic and copies ran while one was open for 25% of the time, Pallas kernels for 0%

profile of v1, /device:TPU:3, one launch (start us, length us, event | category | flops | bytes accessed | tf_op | source)
XLA Modules:
  0.0 363.5 jit_solution(1527206523269003042)
XLA Ops:
  7.2 21.4 %multiply_convert_fusion = (bf16[256,3584]{1,0:T(8,128)(2,1)}, bf16[256,3584]{1,0:T(8,128)(2,1)}, bf16[256,3584]{1,0:T(8,128)(2,1)}) fusion(bf16[256,3584]{1,0:T(8,128)(2,1)} %param.8, bf16[256,3584]{1,0:T(8,128)(2,1)} %param.9, bf16[256,4096]{1,0:T(8,128)(2,1)} %param.7, bf16[4096,3584]{1,0:T(8,128)(2,1)} %param.11), kind=kOutput, calls=%fused_computation.31 | convolution fusion | flops 7531790336 | bytes 40632320 | tf_op jit(solution)/shard_map/dot_general | solution.py:35
  32.6 4.6 %all-to-all-start = ((bf16[256,8,512]{0,2,1:T(8,128)(2,1)}), bf16[256,8,512]{0,2,1:T(8,128)(2,1)S(1)}, u32[]{:S(2)}, u32[]{:S(2)}) async-start(bf16[256,8,512]{0,2,1:T(8,128)(2,1)} %bitcast.54), calls=%async_computation | async-start | bytes 4194304 | tf_op jit(solution)/shard_map/all_to_all | solution.py:33
  37.2 8.9 %copy.34 = f32[512,3584]{0,1:T(8,128)} copy(f32[512,3584]{1,0:T(8,128)} %param.13) | data formatting | bytes 14680064 | tf_op args[6]
  46.1 8.4 %copy.24 = f32[512,3584]{0,1:T(8,128)} copy(f32[512,3584]{1,0:T(8,128)} %param.12) | data formatting | bytes 14680064 | tf_op args[5]
  54.4 4.0 %constant_dynamic-slice_fusion.2 = bf16[512,3584]{1,0:T(8,128)(2,1)} fusion(bf16[4096,3584]{1,0:T(8,128)(2,1)} %param.11, s32[]{:T(128)S(6)} %select_n.47), kind=kLoop, calls=%fused_computation.55 | loop fusion | bytes 7340036 | tf_op jit(solution)/shard_map/dynamic_slice | solution.py:55
  58.5 6.0 %copy.39 = bf16[512,3584]{0,1:T(8,128)(2,1)} copy(bf16[512,3584]{1,0:T(8,128)(2,1)} %constant_dynamic-slice_fusion.2) | data formatting | bytes 7340032
  64.5 15.2 %all-to-all-done = bf16[256,8,512]{0,2,1:T(8,128)(2,1)S(1)} async-done(((bf16[256,8,512]{0,2,1:T(8,128)(2,1)}), bf16[256,8,512]{0,2,1:T(8,128)(2,1)S(1)}, u32[]{:S(2)}, u32[]{:S(2)}) %all-to-all-start) | async-done | bytes 2097184 | tf_op jit(solution)/shard_map/all_to_all | solution.py:33
  79.7 52.1 %all-gather.3.cloned.1.call-done = bf16[2048,3584]{1,0:T(8,128)(2,1)} async-done(((bf16[256,3584]{1,0:T(8,128)(2,1)}), bf16[2048,3584]{1,0:T(8,128)(2,1)}) %all-gather.3.cloned.1.call-update) | async-done | bytes 14680080 | tf_op jit(solution)/shard_map/all_gather | solution.py:31
  131.8 4.7 %convolution_convert_fusion = bf16[3584,512]{1,0:T(8,128)(2,1)} fusion(bf16[2048,3584]{1,0:T(8,128)(2,1)} %all-gather.3.cloned.1.call-done, bf16[8,256,512]{1,2,0:T(8,128)(2,1)S(1)} %bitcast.46), kind=kOutput, calls=%fused_computation.10 | convolution fusion | flops 941359104 | bytes 5767168 | tf_op jit(solution)/shard_map/dot_general | solution.py:43
  136.5 5.4 %convolution_convert_fusion.1 = bf16[3584,512]{1,0:T(8,128)(2,1)} fusion(bf16[2048,3584]{1,0:T(8,128)(2,1)} %all-gather.3.cloned.1.call-done, bf16[8,256,512]{1,2,0:T(8,128)(2,1)S(1)} %bitcast.47), kind=kOutput, calls=%fused_computation.11 | convolution fusion | flops 941359104 | bytes 5767168 | tf_op jit(solution)/shard_map/dot_general | solution.py:43
  141.9 3.0 convolution_convert_fusion.2
  144.9 3.1 convolution_convert_fusion.3
  147.9 3.0 convolution_convert_fusion.4
  150.9 2.9 convolution_convert_fusion.5
  153.9 3.0 convolution_convert_fusion.6
  156.9 20.2 %fusion.3 = (f32[512,3584]{0,1:T(8,128)}, f32[512,3584]{0,1:T(8,128)}) fusion(f32[512,3584]{0,1:T(8,128)} %copy.34, f32[512,3584]{0,1:T(8,128)} %copy.24, bf16[3584,512]{1,0:T(8,128)(2,1)} %convolution_convert_fusion, bf16[3584,512]{1,0:T(8,128)(2,1)} %convolution_convert_fusion.1, bf16[3584,512]{1,0:T(8,128)(2,1)} %convolution_convert_fusion.2, ...), kind=kOutput, calls=%fused_computation.6 | convolution fusion | flops 981729280 | bytes 57147392 | tf_op jit(solution)/shard_map/dot_general | solution.py:43
  177.1 37.6 %all-gather.5.cloned.1.call-done = bf16[2048,3584]{1,0:T(8,128)(2,1)} async-done(((bf16[256,3584]{1,0:T(8,128)(2,1)}), bf16[2048,3584]{1,0:T(8,128)(2,1)}) %all-gather.5.cloned.1.call-update) | async-done | bytes 14680080 | tf_op jit(solution)/shard_map/all_gather | solution.py:32
  214.7 25.4 %fusion.15 = f32[2048,512]{0,1:T(8,128)} fusion(bf16[2048,3584]{1,0:T(8,128)(2,1)} %all-gather.5.cloned.1.call-done, bf16[512,3584]{0,1:T(8,128)(2,1)} %copy.39, f32[512,3584]{0,1:T(8,128)} %get-tuple-element.20, f32[512,3584]{0,1:T(8,128)} %get-tuple-element.21), kind=kOutput, calls=%fused_computation.33 | convolution fusion | flops 7534542848 | bytes 37224448 | tf_op jit(solution)/shard_map/dot_general | solution.py:64
  240.1 76.5 %reduce-scatter.2.cloned.1.call-done = f32[512,512]{0,1:T(8,128)} async-done(((f32[2048,512]{0,1:T(8,128)}), f32[512,512]{0,1:T(8,128)}) %reduce-scatter.2.cloned.1.call-update) | async-done | bytes 1048592 | tf_op jit(solution)/shard_map/reduce_scatter | solution.py:67
  319.8 3.1 collective-permute-start.1
  322.9 8.4 %copy.36 = f32[512,3584]{1,0:T(8,128)} copy(f32[512,3584]{0,1:T(8,128)} %get-tuple-element.21) | data formatting | bytes 14680064
  331.2 8.4 %copy.37 = f32[512,3584]{1,0:T(8,128)} copy(f32[512,3584]{0,1:T(8,128)} %get-tuple-element.20) | data formatting | bytes 14680064
  339.6 10.6 %collective-permute-done = bf16[256,512]{0,1:T(8,128)(2,1)S(1)} collective-permute-done((bf16[256,512]{0,1:T(8,128)(2,1)S(1)}, bf16[256,512]{0,1:T(8,128)(2,1)S(1)}, u32[]{:S(2)}, u32[]{:S(2)}) %collective-permute-start) | collective-permute-done | bytes 262176 | tf_op jit(solution)/shard_map/ppermute | solution.py:81
  350.2 5.6 %collective-permute-done.1 = bf16[256,512]{0,1:T(8,128)(2,1)S(1)} collective-permute-done((bf16[256,512]{0,1:T(8,128)(2,1)S(1)}, bf16[256,512]{0,1:T(8,128)(2,1)S(1)}, u32[]{:S(2)}, u32[]{:S(2)}) %collective-permute-start.1) | collective-permute-done | bytes 262176 | tf_op jit(solution)/shard_map/ppermute | solution.py:81
  (17 shorter events, 8.3 us)
Async XLA Ops:
  7.2 124.6 %all-gather.3.cloned.1.call-start = ((), (), s32[]{:S(2)}) async-start(), calls=%async_computation.2 | async-start | bytes 16515072 | tf_op jit(solution)/shard_map/all_gather | solution.py:31
  28.6 1.6 copy-start.1
  28.6 186.1 %all-gather.5.cloned.1.call-start = ((), (), s32[]{:S(2)}) async-start(), calls=%async_computation.3 | async-start | bytes 16515072 | tf_op jit(solution)/shard_map/all_gather | solution.py:32
  32.6 47.1 %all-to-all-start = ((bf16[256,8,512]{0,2,1:T(8,128)(2,1)}), bf16[256,8,512]{0,2,1:T(8,128)(2,1)S(1)}, u32[]{:S(2)}, u32[]{:S(2)}) async-start(bf16[256,8,512]{0,2,1:T(8,128)(2,1)} %bitcast.54), calls=%async_computation | async-start | bytes 4194304 | tf_op jit(solution)/shard_map/all_to_all | solution.py:33
  37.2 279.4 %reduce-scatter.2.cloned.1.call-start = ((), (), s32[]{:S(2)}) async-start(), calls=%async_computation.4 | async-start | bytes 5242880 | tf_op jit(solution)/shard_map/reduce_scatter | solution.py:67
  131.8 10.1 %copy-start = (bf16[2048,3584]{1,0:T(8,128)(2,1)S(1)}, bf16[2048,3584]{1,0:T(8,128)(2,1)}, u32[]{:S(2)}) copy-start(bf16[2048,3584]{1,0:T(8,128)(2,1)} %all-gather.3.cloned.1.call-done) | copy-start | bytes 44040196
  318.0 32.2 %collective-permute-start = (bf16[256,512]{0,1:T(8,128)(2,1)S(1)}, bf16[256,512]{0,1:T(8,128)(2,1)S(1)}, u32[]{:S(2)}, u32[]{:S(2)}) collective-permute-start(bf16[256,512]{0,1:T(8,128)(2,1)S(1)} %get-tuple-element.28), channel_id=1, source_target_pairs={{0,4},{1,12},{2,20},{3,28},{4,0},{5,8},{6,16},{7,24},{8,5},{9,13},... | collective-permute-start | bytes 786440 | tf_op jit(solution)/shard_map/ppermute | solution.py:81
  319.8 36.1 %collective-permute-start.1 = (bf16[256,512]{0,1:T(8,128)(2,1)S(1)}, bf16[256,512]{0,1:T(8,128)(2,1)S(1)}, u32[]{:S(2)}, u32[]{:S(2)}) collective-permute-start(bf16[256,512]{0,1:T(8,128)(2,1)S(1)} %get-tuple-element.27), channel_id=1, source_target_pairs={{0,0},{1,8},{2,16},{3,24},{4,4},{5,12},{6,20},{7,28},{8,1},{9,9},{... | collective-permute-start | bytes 786440 | tf_op jit(solution)/shard_map/ppermute | solution.py:81
Sparse Core Ops, SparseCore 0:
  28.7 103.0 all-gather.2
  133.7 80.9 all-gather.4
  240.2 76.3 reduce-scatter.1

commit v2 on v1

--- a/solution.py
+++ b/solution.py
@@ -30,7 +30,7 @@
 
     hidden_all = lax.all_gather(hidden, "dp", axis=0, tiled=True)
     next_all = lax.all_gather(next_hidden, "dp", axis=0, tiled=True)
-    grad_rows = lax.all_to_all(grad_out, "dp", 1, 0, tiled=True)
+    grad_rows = lax.all_to_all(grad_out.T, "dp", 0, 1, tiled=True)
 
     grad_hidden = jnp.dot(grad_out, down_weight, preferred_element_type=jnp.float32)
     gate_grad = (
@@ -40,10 +40,9 @@
 
     weight_grad = jnp.zeros((owned_rows, hidden.shape[1]), jnp.float32)
     for b in range(n_dp):
-        block = lax.dot_general(
-            grad_rows[b * tok : (b + 1) * tok],
+        block = jnp.dot(
+            grad_rows[:, b * tok : (b + 1) * tok],
             hidden_all[b * tok : (b + 1) * tok],
-            (((0,), (0,)), ((), ())),
             preferred_element_type=jnp.float32,
         ).astype(jnp.bfloat16)
         weight_grad = weight_grad + block.astype(jnp.float32)
@@ -62,10 +61,12 @@
     ).astype(jnp.bfloat16)
 
     partial_out = lax.dot_general(
-        next_all, new_shard, (((1,), (1,)), ((), ())), preferred_element_type=jnp.float32
+        new_shard, next_all, (((1,), (1,)), ((), ())), preferred_element_type=jnp.float32
     )
-    summed = lax.psum_scatter(partial_out, "tensor", scatter_dimension=0, tiled=True).astype(
-        jnp.bfloat16
+    summed = (
+        lax.psum_scatter(partial_out, "tensor", scatter_dimension=1, tiled=True)
+        .astype(jnp.bfloat16)
+        .T
     )
     sub = me % group
     pieces = []

time: 364 us -> 364 us (level)
    unnamed x11 -> x13, local copies, waits for them, and re-layouts: 44.2 us -> 44.3 us
  transfers between devices with their start and end apart: 6 -> 6, of which waited for: 6 -> 6; matrix products, arithmetic and copies ran while one was open for 25% -> 26% of each run, Pallas kernels for 0% -> 0%
where the time goes in v2:
time: 364 us; the launch traced here: 363 us
  waiting for transfers between devices  196 us (54%)
  matrix products  91.7 us (25%)
  local copies, waits for them, and re-layouts  50.8 us (14%)
  between operations  13.9 us (4%)
  starting transfers between devices  9.51 us (3%)
    reduce_scatter x1, waiting for transfers between devices, shards(): lax.psum_scatter(partial_out, 'tensor', scatter_dimension=1, tiled=True)  76.5 us
    all_gather x1, waiting for transfers between devices, shards(): hidden_all = lax.all_gather(hidden, 'dp', axis=0, tiled=True)  49.7 us
    dot_general x8, matrix products, shards(): jnp.dot(grad_rows[:, b * tok:(b + 1) * tok], hidden_all[b * tok:(b + 1) *...  44.9 us
    unnamed x13, local copies, waits for them, and re-layouts  44.3 us
    all_gather x1, waiting for transfers between devices, shards(): next_all = lax.all_gather(next_hidden, 'dp', axis=0, tiled=True)  38 us
    dot_general x1, matrix products, shards(): lax.dot_general(new_shard, next_all, (((1,), (1,)), ((), ())), preferred_...  25.4 us
    dot_general x1, matrix products, shards(): jnp.dot(grad_out, down_weight, preferred_element_type=jnp.float32)  21.4 us
    ppermute x2, waiting for transfers between devices, shards(): pieces.append(lax.ppermute(piece, ('dp', 'tensor'), perm))  16.2 us
  transfers between devices with their start and end apart: 6, of which 6 were waited for; matrix products, arithmetic and copies ran while one was open for 26% of the time, Pallas kernels for 0%

profile of v2, /device:TPU:3, one launch (start us, length us, event | category | flops | bytes accessed | tf_op | source)
XLA Modules:
  0.0 363.5 jit_solution(1253085345670090751)
XLA Ops:
  7.2 21.4 %multiply_convert_fusion = (bf16[256,3584]{1,0:T(8,128)(2,1)}, bf16[256,3584]{1,0:T(8,128)(2,1)}, bf16[256,3584]{1,0:T(8,128)(2,1)}) fusion(bf16[256,3584]{1,0:T(8,128)(2,1)} %param.8, bf16[256,3584]{1,0:T(8,128)(2,1)} %param.9, bf16[256,4096]{1,0:T(8,128)(2,1)} %param.7, bf16[4096,3584]{1,0:T(8,128)(2,1)} %param.11), kind=kOutput, calls=%fused_computation.31 | convolution fusion | flops 7531790336 | bytes 40632320 | tf_op jit(solution)/shard_map/dot_general | solution.py:35
  32.7 4.6 %all-to-all-start = ((bf16[8,512,256]{2,1,0:T(8,128)(2,1)}), bf16[8,512,256]{2,1,0:T(8,128)(2,1)S(1)}, u32[]{:S(2)}, u32[]{:S(2)}) async-start(bf16[8,512,256]{2,1,0:T(8,128)(2,1)} %bitcast.18), calls=%async_computation | async-start | bytes 4194304 | tf_op jit(solution)/shard_map/all_to_all | solution.py:33
  37.2 8.9 %copy.27 = f32[512,3584]{0,1:T(8,128)} copy(f32[512,3584]{1,0:T(8,128)} %param.13) | data formatting | bytes 14680064 | tf_op args[6]
  46.1 8.4 %copy.24 = f32[512,3584]{0,1:T(8,128)} copy(f32[512,3584]{1,0:T(8,128)} %param.12) | data formatting | bytes 14680064 | tf_op args[5]
  54.5 4.1 %constant_dynamic-slice_fusion = bf16[512,3584]{1,0:T(8,128)(2,1)} fusion(bf16[4096,3584]{1,0:T(8,128)(2,1)} %param.11, s32[]{:T(128)S(6)} %select_n.47), kind=kLoop, calls=%fused_computation.54 | loop fusion | bytes 7340036 | tf_op jit(solution)/shard_map/dynamic_slice | solution.py:54
  58.5 6.0 %copy.32 = bf16[512,3584]{0,1:T(8,128)(2,1)} copy(bf16[512,3584]{1,0:T(8,128)(2,1)} %constant_dynamic-slice_fusion) | data formatting | bytes 7340032
  64.5 15.2 %all-to-all-done = bf16[8,512,256]{2,1,0:T(8,128)(2,1)S(1)} async-done(((bf16[8,512,256]{2,1,0:T(8,128)(2,1)}), bf16[8,512,256]{2,1,0:T(8,128)(2,1)S(1)}, u32[]{:S(2)}, u32[]{:S(2)}) %all-to-all-start) | async-done | bytes 2097184 | tf_op jit(solution)/shard_map/all_to_all | solution.py:33
  82.1 49.7 %all-gather.3.cloned.1.call-done = bf16[2048,3584]{1,0:T(8,128)(2,1)} async-done(((bf16[256,3584]{1,0:T(8,128)(2,1)}), bf16[2048,3584]{1,0:T(8,128)(2,1)}) %all-gather.3.cloned.1.call-update) | async-done | bytes 14680080 | tf_op jit(solution)/shard_map/all_gather | solution.py:31
  131.8 4.7 %convolution_convert_fusion = bf16[3584,512]{1,0:T(8,128)(2,1)} fusion(bf16[2048,3584]{1,0:T(8,128)(2,1)} %all-gather.3.cloned.1.call-done, bf16[512,2048]{0,1:T(8,128)(2,1)} %bitcast.19), kind=kOutput, calls=%fused_computation.10 | convolution fusion | flops 941359104 | bytes 5767168 | tf_op jit(solution)/shard_map/dot_general | solution.py:43
  136.5 5.3 %convolution_convert_fusion.1 = bf16[3584,512]{1,0:T(8,128)(2,1)} fusion(bf16[2048,3584]{1,0:T(8,128)(2,1)} %all-gather.3.cloned.1.call-done, bf16[512,2048]{0,1:T(8,128)(2,1)S(1)} %bitcast.20), kind=kOutput, calls=%fused_computation.11 | convolution fusion | flops 941359104 | bytes 5767168 | tf_op jit(solution)/shard_map/dot_general | solution.py:43
  141.8 2.9 convolution_convert_fusion.2
  144.8 3.1 convolution_convert_fusion.3
  147.8 3.0 convolution_convert_fusion.4
  150.8 2.9 convolution_convert_fusion.5
  153.8 3.0 convolution_convert_fusion.6
  156.7 20.0 %fusion.3 = (f32[512,3584]{0,1:T(8,128)}, f32[512,3584]{0,1:T(8,128)}) fusion(f32[512,3584]{0,1:T(8,128)} %copy.27, f32[512,3584]{0,1:T(8,128)} %copy.24, bf16[3584,512]{1,0:T(8,128)(2,1)} %convolution_convert_fusion, bf16[3584,512]{1,0:T(8,128)(2,1)} %convolution_convert_fusion.1, bf16[3584,512]{1,0:T(8,128)(2,1)} %convolution_convert_fusion.2, ...), kind=kOutput, calls=%fused_computation.6 | convolution fusion | flops 981729280 | bytes 57147392 | tf_op jit(solution)/shard_map/dot_general | solution.py:43
  176.8 38.0 %all-gather.5.cloned.1.call-done = bf16[2048,3584]{1,0:T(8,128)(2,1)} async-done(((bf16[256,3584]{1,0:T(8,128)(2,1)}), bf16[2048,3584]{1,0:T(8,128)(2,1)}) %all-gather.5.cloned.1.call-update) | async-done | bytes 14680080 | tf_op jit(solution)/shard_map/all_gather | solution.py:32
  214.7 25.4 %fusion.13 = f32[512,2048]{1,0:T(8,128)} fusion(bf16[2048,3584]{1,0:T(8,128)(2,1)} %all-gather.5.cloned.1.call-done, bf16[512,3584]{0,1:T(8,128)(2,1)} %copy.32, f32[512,3584]{0,1:T(8,128)} %get-tuple-element.20, f32[512,3584]{0,1:T(8,128)} %get-tuple-element.21), kind=kOutput, calls=%fused_computation.32 | convolution fusion | flops 7534542848 | bytes 37224448 | tf_op jit(solution)/shard_map/dot_general | solution.py:63
  240.2 76.5 %reduce-scatter.2.cloned.1.call-done = f32[512,512]{1,0:T(8,128)} async-done(((f32[512,2048]{1,0:T(8,128)}), f32[512,512]{1,0:T(8,128)}) %reduce-scatter.2.cloned.1.call-update) | async-done | bytes 1048592 | tf_op jit(solution)/shard_map/reduce_scatter | solution.py:67
  319.8 3.1 collective-permute-start.1
  322.9 8.4 %copy.29 = f32[512,3584]{1,0:T(8,128)} copy(f32[512,3584]{0,1:T(8,128)} %get-tuple-element.21) | data formatting | bytes 14680064
  331.3 8.4 %copy.30 = f32[512,3584]{1,0:T(8,128)} copy(f32[512,3584]{0,1:T(8,128)} %get-tuple-element.20) | data formatting | bytes 14680064
  339.6 10.6 %collective-permute-done = bf16[256,512]{0,1:T(8,128)(2,1)S(1)} collective-permute-done((bf16[256,512]{0,1:T(8,128)(2,1)S(1)}, bf16[256,512]{0,1:T(8,128)(2,1)S(1)}, u32[]{:S(2)}, u32[]{:S(2)}) %collective-permute-start) | collective-permute-done | bytes 262176 | tf_op jit(solution)/shard_map/ppermute | solution.py:82
  350.2 5.6 %collective-permute-done.1 = bf16[256,512]{0,1:T(8,128)(2,1)S(1)} collective-permute-done((bf16[256,512]{0,1:T(8,128)(2,1)S(1)}, bf16[256,512]{0,1:T(8,128)(2,1)S(1)}, u32[]{:S(2)}, u32[]{:S(2)}) %collective-permute-start.1) | collective-permute-done | bytes 262176 | tf_op jit(solution)/shard_map/ppermute | solution.py:82
  (20 shorter events, 10.8 us)
Async XLA Ops:
  7.2 124.7 %all-gather.3.cloned.1.call-start = ((), (), s32[]{:S(2)}) async-start(), calls=%async_computation.2 | async-start | bytes 16515072 | tf_op jit(solution)/shard_map/all_gather | solution.py:31
  28.6 1.6 copy-start.1
  28.6 186.1 %all-gather.5.cloned.1.call-start = ((), (), s32[]{:S(2)}) async-start(), calls=%async_computation.3 | async-start | bytes 16515072 | tf_op jit(solution)/shard_map/all_gather | solution.py:32
  32.7 47.1 %all-to-all-start = ((bf16[8,512,256]{2,1,0:T(8,128)(2,1)}), bf16[8,512,256]{2,1,0:T(8,128)(2,1)S(1)}, u32[]{:S(2)}, u32[]{:S(2)}) async-start(bf16[8,512,256]{2,1,0:T(8,128)(2,1)} %bitcast.18), calls=%async_computation | async-start | bytes 4194304 | tf_op jit(solution)/shard_map/all_to_all | solution.py:33
  37.2 279.4 %reduce-scatter.2.cloned.1.call-start = ((), (), s32[]{:S(2)}) async-start(), calls=%async_computation.4 | async-start | bytes 5242880 | tf_op jit(solution)/shard_map/reduce_scatter | solution.py:67
  131.8 4.7 %copy-start = (bf16[512,8,256]{0,2,1:T(8,128)(2,1)S(1)}, bf16[512,8,256]{0,2,1:T(8,128)(2,1)}, u32[]{:S(2)}) copy-start(bf16[512,8,256]{0,2,1:T(8,128)(2,1)} %copy.26) | copy-start | bytes 6291460
  131.8 10.0 %copy-start.2 = (bf16[2048,3584]{1,0:T(8,128)(2,1)S(1)}, bf16[2048,3584]{1,0:T(8,128)(2,1)}, u32[]{:S(2)}) copy-start(bf16[2048,3584]{1,0:T(8,128)(2,1)} %all-gather.3.cloned.1.call-done) | copy-start | bytes 44040196
  318.0 32.2 %collective-permute-start = (bf16[256,512]{0,1:T(8,128)(2,1)S(1)}, bf16[256,512]{0,1:T(8,128)(2,1)S(1)}, u32[]{:S(2)}, u32[]{:S(2)}) collective-permute-start(bf16[256,512]{0,1:T(8,128)(2,1)S(1)} %get-tuple-element.28), channel_id=1, source_target_pairs={{0,4},{1,12},{2,20},{3,28},{4,0},{5,8},{6,16},{7,24},{8,5},{9,13},... | collective-permute-start | bytes 786440 | tf_op jit(solution)/shard_map/ppermute | solution.py:82
  319.8 36.1 %collective-permute-start.1 = (bf16[256,512]{0,1:T(8,128)(2,1)S(1)}, bf16[256,512]{0,1:T(8,128)(2,1)S(1)}, u32[]{:S(2)}, u32[]{:S(2)}) collective-permute-start(bf16[256,512]{0,1:T(8,128)(2,1)S(1)} %get-tuple-element.27), channel_id=1, source_target_pairs={{0,0},{1,8},{2,16},{3,24},{4,4},{5,12},{6,20},{7,28},{8,1},{9,9},{... | collective-permute-start | bytes 786440 | tf_op jit(solution)/shard_map/ppermute | solution.py:82
Sparse Core Ops, SparseCore 0:
  28.7 103.0 all-gather.2
  133.7 80.9 all-gather.4
  240.2 76.3 reduce-scatter.1

commit v3 on v2

--- a/solution.py
+++ b/solution.py
@@ -1,6 +1,10 @@
+import functools
+
 import jax
 import jax.numpy as jnp
 from jax import lax
+from jax.experimental import pallas as pl
+from jax.experimental.pallas import tpu as pltpu
 from jax.sharding import PartitionSpec as P
 
 STEP = 20
@@ -11,6 +15,62 @@
 learn_rate = 0.001
 decay_rate = 0.1
 epsilon = 1e-08
+
+
+def adam_kernel(me_ref, g_ref, h_ref, m1_ref, m2_ref, w_ref, m1_out, m2_out, w_out, *, blocks, tok):
+    acc = jnp.zeros(m1_ref.shape, jnp.float32)
+    for b in range(blocks):
+        part = jnp.dot(
+            g_ref[:, b * tok : (b + 1) * tok],
+            h_ref[b * tok : (b + 1) * tok, :],
+            preferred_element_type=jnp.float32,
+        )
+        acc = acc + part.astype(jnp.bfloat16).astype(jnp.float32)
+    moment_one = beta_one * m1_ref[...] + (1.0 - beta_one) * acc
+    moment_two = beta_two * m2_ref[...] + (1.0 - beta_two) * acc * acc
+    corrected_one = moment_one / (1.0 - beta_one**STEP)
+    corrected_two = moment_two / (1.0 - beta_two**STEP)
+    old = w_ref[...].astype(jnp.float32)
+    w_out[...] = (
+        old - learn_rate * (corrected_one / (jnp.sqrt(corrected_two) + epsilon) + decay_rate * old)
+    ).astype(jnp.bfloat16)
+    m1_out[...] = moment_one
+    m2_out[...] = moment_two
+
+
+def owner_update(me, grad_rows, hidden_all, first_moment, second_moment, down_weight, tok):
+    rows, width = first_moment.shape
+    tokens = hidden_all.shape[0]
+    tn = 512 if width % 512 == 0 else 256
+    grid_spec = pltpu.PrefetchScalarGridSpec(
+        num_scalar_prefetch=1,
+        grid=(width // tn,),
+        in_specs=[
+            pl.BlockSpec((rows, tokens), lambda n, me: (0, 0)),
+            pl.BlockSpec((tokens, tn), lambda n, me: (0, n)),
+            pl.BlockSpec((rows, tn), lambda n, me: (0, n)),
+            pl.BlockSpec((rows, tn), lambda n, me: (0, n)),
+            pl.BlockSpec((rows, tn), lambda n, me: (me[0], n)),
+        ],
+        out_specs=[
+            pl.BlockSpec((rows, tn), lambda n, me: (0, n)),
+            pl.BlockSpec((rows, tn), lambda n, me: (0, n)),
+            pl.BlockSpec((rows, tn), lambda n, me: (0, n)),
+        ],
+    )
+    flops = 2 * rows * tokens * width
+    nbytes = 2 * rows * tokens + 2 * tokens * width + 16 * rows * width + 4 * rows * width
+    return pl.pallas_call(
+        functools.partial(adam_kernel, blocks=tokens // tok, tok=tok),
+        grid_spec=grid_spec,
+        out_shape=[
+            jax.ShapeDtypeStruct((rows, width), jnp.float32),
+            jax.ShapeDtypeStruct((rows, width), jnp.float32),
+            jax.ShapeDtypeStruct((rows, width), jnp.bfloat16),
+        ],
+        compiler_params=pltpu.CompilerParams(vmem_limit_bytes=48 * 1024 * 1024),
+        cost_estimate=pl.CostEstimate(flops=flops, transcendentals=rows * width, bytes_accessed=nbytes),
+    )(jnp.reshape(me, (1,)).astype(jnp.int32), grad_rows, hidden_all, first_moment, second_moment, down_weight)
 
 
 def shards(grad_out, gate_input, up_input, next_hidden, down_weight, first_moment, second_moment):
@@ -27,6 +87,11 @@
     sigmoid_gate = jax.nn.sigmoid(gate_value)
     activated = gate_value * sigmoid_gate
     hidden = (activated * up_value).astype(jnp.bfloat16)
+    hidden, gate_input, up_input = lax.optimization_barrier((hidden, gate_input, up_input))
+    gate_value = gate_input.astype(jnp.float32)
+    up_value = up_input.astype(jnp.float32)
+    sigmoid_gate = jax.nn.sigmoid(gate_value)
+    activated = gate_value * sigmoid_gate
 
     hidden_all = lax.all_gather(hidden, "dp", axis=0, tiled=True)
     next_all = lax.all_gather(next_hidden, "dp", axis=0, tiled=True)
@@ -38,27 +103,9 @@
     ).astype(jnp.bfloat16)
     up_grad = (grad_hidden * activated).astype(jnp.bfloat16)
 
-    weight_grad = jnp.zeros((owned_rows, hidden.shape[1]), jnp.float32)
-    for b in range(n_dp):
-        block = jnp.dot(
-            grad_rows[:, b * tok : (b + 1) * tok],
-            hidden_all[b * tok : (b + 1) * tok],
-            preferred_element_type=jnp.float32,
-        ).astype(jnp.bfloat16)
-        weight_grad = weight_grad + block.astype(jnp.float32)
-
-    moment_one = beta_one * first_moment + (1.0 - beta_one) * weight_grad
-    moment_two = beta_two * second_moment + (1.0 - beta_two) * weight_grad * weight_grad
-    corrected_one = moment_one / (1.0 - beta_one**STEP)
-    corrected_two = moment_two / (1.0 - beta_two**STEP)
-    old_shard = lax.dynamic_slice_in_dim(down_weight, me * owned_rows, owned_rows, 0).astype(
-        jnp.float32
+    moment_one, moment_two, new_shard = owner_update(
+        me, grad_rows, hidden_all, first_moment, second_moment, down_weight, tok
     )
-    new_shard = (
-        old_shard
-        - learn_rate
-        * (corrected_one / (jnp.sqrt(corrected_two) + epsilon) + decay_rate * old_shard)
-    ).astype(jnp.bfloat16)
 
     partial_out = lax.dot_general(
         new_shard, next_all, (((1,), (1,)), ((), ())), preferred_element_type=jnp.float32

time: 364 us -> 334 us (0.918)
  matrix products: 91.7 us -> 29.5 us
  waiting for transfers between devices: 196 us -> 245 us
  local copies, waits for them, and re-layouts: 50.8 us -> 8.55 us
  Pallas kernels: 0 us -> 22.2 us
  other arithmetic: 1.37 us -> 5.88 us
    dot_general x8 -> x0, matrix products: 44.9 us -> none  [shards(): jnp.dot(grad_rows[:, b * tok:(b + 1) * tok], hidden_all[b * tok:(b + 1) *...]
    unnamed x13 -> x9, local copies, waits for them, and re-layouts: 44.3 us -> 4.19 us
    all_to_all x1, waiting for transfers between devices: 15.2 us -> 42 us  [shards(): grad_rows = lax.all_to_all(grad_out.T, 'dp', 0, 1, tiled=True)]
    pallas_call x0 -> x1, Pallas kernels: none -> 22.2 us  [owner_update(): pl.pallas_call(functools.partial(adam_kernel, blocks=tokens // tok, tok=t...]
    all_gather x1, waiting for transfers between devices: 38 us -> 58.9 us  [shards(): next_all = lax.all_gather(next_hidden, 'dp', axis=0, tiled=True)]
    dot_general x1, matrix products: 25.4 us -> 13.5 us  [shards(): lax.dot_general(new_shard, next_all, (((1,), (1,)), ((), ())), preferred_...]
    dot_general x1, matrix products: 21.4 us -> 16 us  [shards(): jnp.dot(grad_out, down_weight, preferred_element_type=jnp.float32)]
    convert_element_type x0 -> x1, other arithmetic: none -> 4.51 us  [shards(): hidden = (activated * up_value).astype(jnp.bfloat16)]
  transfers between devices with their start and end apart: 6 -> 6, of which waited for: 6 -> 6; matrix products, arithmetic and copies ran while one was open for 26% -> 6% of each run, Pallas kernels for 0% -> 7%
where the time goes in v3:
time: 334 us
  waiting for transfers between devices  245 us (73%)
  matrix products  29.5 us (9%)
  Pallas kernels  22.2 us (7%)
  between operations  13.8 us (4%)
  starting transfers between devices  9.51 us (3%)
  local copies, waits for them, and re-layouts  8.55 us (3%)
  other arithmetic  5.88 us (2%)
    reduce_scatter x1, waiting for transfers between devices, shards(): lax.psum_scatter(partial_out, 'tensor', scatter_dimension=1, tiled=True)  76.5 us
    all_gather x1, waiting for transfers between devices, shards(): next_all = lax.all_gather(next_hidden, 'dp', axis=0, tiled=True)  58.9 us
    all_gather x1, waiting for transfers between devices, shards(): hidden_all = lax.all_gather(hidden, 'dp', axis=0, tiled=True)  49.4 us
    all_to_all x1, waiting for transfers between devices, shards(): grad_rows = lax.all_to_all(grad_out.T, 'dp', 0, 1, tiled=True)  42 us
    pallas_call x1, Pallas kernels, owner_update(): pl.pallas_call(functools.partial(adam_kernel, blocks=tokens // tok, tok=t...  22.2 us
    ppermute x2, waiting for transfers between devices, shards(): pieces.append(lax.ppermute(piece, ('dp', 'tensor'), perm))  17 us
    dot_general x1, matrix products, shards(): jnp.dot(grad_out, down_weight, preferred_element_type=jnp.float32)  16 us
    dot_general x1, matrix products, shards(): lax.dot_general(new_shard, next_all, (((1,), (1,)), ((), ())), preferred_...  13.5 us
  transfers between devices with their start and end apart: 6, of which 6 were waited for; matrix products, arithmetic and copies ran while one was open for 6% of the time, Pallas kernels for 7%

profile of v3, /device:TPU:3, one launch (start us, length us, event | category | flops | bytes accessed | tf_op | source)
XLA Modules:
  0.0 333.9 jit_solution(7478503569391600480)
XLA Ops:
  7.2 0.0 all-gather.3.cloned.1.call-start
  7.2 4.5 %fusion.12 = bf16[256,3584]{1,0:T(8,128)(2,1)} fusion(bf16[256,3584]{1,0:T(8,128)(2,1)} %param.9, bf16[256,3584]{1,0:T(8,128)(2,1)} %param.8), kind=kLoop, calls=%fused_computation.17 | loop fusion | flops 7340032 | bytes 5505024 | tf_op jit(solution)/shard_map/convert_element_type | solution.py:89
  11.7 0.0 all-gather.3.cloned.1.call-update
  11.8 0.0 all-gather.5.cloned.1.call-start
  11.8 0.7 all-gather.5.cloned.1.call-update
  12.5 2.5 copy.14
  15.0 4.6 %all-to-all-start = ((bf16[8,512,256]{2,1,0:T(8,128)(2,1)}), bf16[8,512,256]{2,1,0:T(8,128)(2,1)S(1)}, u32[]{:S(2)}, u32[]{:S(2)}) async-start(bf16[8,512,256]{2,1,0:T(8,128)(2,1)} %bitcast.16), calls=%async_computation | async-start | bytes 4194304 | tf_op jit(solution)/shard_map/all_to_all | solution.py:98
  19.6 42.0 %all-to-all-done = bf16[8,512,256]{2,1,0:T(8,128)(2,1)S(1)} async-done(((bf16[8,512,256]{2,1,0:T(8,128)(2,1)}), bf16[8,512,256]{2,1,0:T(8,128)(2,1)S(1)}, u32[]{:S(2)}, u32[]{:S(2)}) %all-to-all-start) | async-done | bytes 2097184 | tf_op jit(solution)/shard_map/all_to_all | solution.py:98
  61.6 1.3 copy-done.1
  62.9 1.9 copy.17
  64.8 49.4 %all-gather.3.cloned.1.call-done.h_ref = bf16[2048,3584]{1,0:T(8,128)(2,1)} async-done(((bf16[256,3584]{1,0:T(8,128)(2,1)}), bf16[2048,3584]{1,0:T(8,128)(2,1)}) %all-gather.3.cloned.1.call-update) | async-done | bytes 14680080 | tf_op jit(solution)/shard_map/all_gather | solution.py:96
  114.1 22.2 %shard_map.110 = (f32[512,3584]{1,0:T(8,128)}, f32[512,3584]{1,0:T(8,128)}, bf16[512,3584]{1,0:T(8,128)(2,1)S(1)}) custom-call(s32[1]{0:T(128)} %bitcast.me_ref, bf16[512,2048]{1,0:T(8,128)(2,1)S(1)} %bitcast.14, bf16[2048,3584]{1,0:T(8,128)(2,1)} %all-gather.3.cloned.1.call-done.h_ref, f32[512,3584]{1,0:T(8,128)} %m1_ref.1, f32[512,3584]{1,0:T(8,128)} %m2_ref.1, ...), custom_call_target="tpu_custom_call" | custom-call | flops 7516192768 | bytes 53477376 | tf_op jit(solution)/shard_map/pallas_call | solution.py:63
  136.3 1.9 copy-done
  138.2 58.9 %all-gather.5.cloned.1.call-done = bf16[2048,3584]{1,0:T(8,128)(2,1)} async-done(((bf16[256,3584]{1,0:T(8,128)(2,1)}), bf16[2048,3584]{1,0:T(8,128)(2,1)}) %all-gather.5.cloned.1.call-update) | async-done | bytes 14680080 | tf_op jit(solution)/shard_map/all_gather | solution.py:97
  197.1 13.5 %fusion.13 = f32[512,2048]{1,0:T(8,128)} fusion(bf16[512,3584]{1,0:T(8,128)(2,1)} %copy-done, bf16[2048,3584]{1,0:T(8,128)(2,1)} %all-gather.5.cloned.1.call-done), kind=kOutput, calls=%fused_computation.23 | convolution fusion | flops 7516192768 | bytes 22544384 | tf_op jit(solution)/shard_map/dot_general | solution.py:110
  210.6 0.0 reduce-scatter.2.cloned.1.call-update
  210.6 76.5 %reduce-scatter.2.cloned.1.call-done = f32[512,512]{1,0:T(8,128)} async-done(((f32[512,2048]{1,0:T(8,128)}), f32[512,512]{1,0:T(8,128)}) %reduce-scatter.2.cloned.1.call-update) | async-done | bytes 1048592 | tf_op jit(solution)/shard_map/reduce_scatter | solution.py:114
  287.1 1.3 convert_element_type.31
  288.5 1.8 collective-permute-start
  290.3 3.1 collective-permute-start.1
  293.3 16.0 %fusion.11 = (bf16[256,3584]{1,0:T(8,128)(2,1)}, bf16[256,3584]{1,0:T(8,128)(2,1)}) fusion(bf16[256,3584]{1,0:T(8,128)(2,1)} %param.8, bf16[256,3584]{1,0:T(8,128)(2,1)} %param.9, bf16[256,4096]{1,0:T(8,128)(2,1)S(1)} %copy-done.3, bf16[4096,3584]{1,0:T(8,128)(2,1)} %w_ref.1), kind=kOutput, calls=%fused_computation.16 | convolution fusion | flops 7529955328 | bytes 38797312 | tf_op jit(solution)/shard_map/dot_general | solution.py:100
  309.3 11.4 %collective-permute-done = bf16[256,512]{0,1:T(8,128)(2,1)S(1)} collective-permute-done((bf16[256,512]{0,1:T(8,128)(2,1)S(1)}, bf16[256,512]{0,1:T(8,128)(2,1)S(1)}, u32[]{:S(2)}, u32[]{:S(2)}) %collective-permute-start) | collective-permute-done | bytes 262176 | tf_op jit(solution)/shard_map/ppermute | solution.py:129
  320.7 5.6 %collective-permute-done.1 = bf16[256,512]{0,1:T(8,128)(2,1)S(1)} collective-permute-done((bf16[256,512]{0,1:T(8,128)(2,1)S(1)}, bf16[256,512]{0,1:T(8,128)(2,1)S(1)}, u32[]{:S(2)}, u32[]{:S(2)}) %collective-permute-start.1) | collective-permute-done | bytes 262176 | tf_op jit(solution)/shard_map/ppermute | solution.py:129
  326.4 1.0 copy.16
  (10 shorter events, 0.1 us)
Async XLA Ops:
  7.2 5.4 %copy-start.2 = (bf16[256,4096]{1,0:T(8,128)(2,1)S(1)}, bf16[256,4096]{1,0:T(8,128)(2,1)}, u32[]{:S(2)}) copy-start(bf16[256,4096]{1,0:T(8,128)(2,1)} %param.7) | copy-start | bytes 6291460
  7.2 107.0 %all-gather.3.cloned.1.call-start = ((), (), s32[]{:S(2)}) async-start(), calls=%async_computation.2 | async-start | bytes 16515072 | tf_op jit(solution)/shard_map/all_gather | solution.py:96
  11.8 185.3 %all-gather.5.cloned.1.call-start = ((), (), s32[]{:S(2)}) async-start(), calls=%async_computation.3 | async-start | bytes 16515072 | tf_op jit(solution)/shard_map/all_gather | solution.py:97
  15.0 46.6 %all-to-all-start = ((bf16[8,512,256]{2,1,0:T(8,128)(2,1)}), bf16[8,512,256]{2,1,0:T(8,128)(2,1)S(1)}, u32[]{:S(2)}, u32[]{:S(2)}) async-start(bf16[8,512,256]{2,1,0:T(8,128)(2,1)} %bitcast.16), calls=%async_computation | async-start | bytes 4194304 | tf_op jit(solution)/shard_map/all_to_all | solution.py:98
  19.6 267.6 %reduce-scatter.2.cloned.1.call-start = ((), (), s32[]{:S(2)}) async-start(), calls=%async_computation.4 | async-start | bytes 5242880 | tf_op jit(solution)/shard_map/reduce_scatter | solution.py:114
  61.6 1.3 copy-start.1
  136.3 1.9 copy-start
  210.6 82.8 %copy-start.3 = (bf16[256,4096]{1,0:T(8,128)(2,1)S(1)}, bf16[256,4096]{1,0:T(8,128)(2,1)}, u32[]{:S(2)}) copy-start(bf16[256,4096]{1,0:T(8,128)(2,1)} %param.7) | copy-start | bytes 6291460
  288.5 32.3 %collective-permute-start = (bf16[256,512]{0,1:T(8,128)(2,1)S(1)}, bf16[256,512]{0,1:T(8,128)(2,1)S(1)}, u32[]{:S(2)}, u32[]{:S(2)}) collective-permute-start(bf16[256,512]{0,1:T(8,128)(2,1)S(1)} %get-tuple-element.32), channel_id=1, source_target_pairs={{0,4},{1,12},{2,20},{3,28},{4,0},{5,8},{6,16},{7,24},{8,5},{9,13},... | collective-permute-start | bytes 786440 | tf_op jit(solution)/shard_map/ppermute | solution.py:129
  290.3 36.1 %collective-permute-start.1 = (bf16[256,512]{0,1:T(8,128)(2,1)S(1)}, bf16[256,512]{0,1:T(8,128)(2,1)S(1)}, u32[]{:S(2)}, u32[]{:S(2)}) collective-permute-start(bf16[256,512]{0,1:T(8,128)(2,1)S(1)} %get-tuple-element.31), channel_id=1, source_target_pairs={{0,0},{1,8},{2,16},{3,24},{4,4},{5,12},{6,20},{7,28},{8,1},{9,9},{... | collective-permute-start | bytes 786440 | tf_op jit(solution)/shard_map/ppermute | solution.py:129
Sparse Core Ops, SparseCore 0:
  11.9 102.2 all-gather.2
  116.0 80.9 all-gather.4
  210.7 76.3 reduce-scatter.1

commit v4 on v3

--- a/solution.py
+++ b/solution.py
@@ -93,8 +93,10 @@
     sigmoid_gate = jax.nn.sigmoid(gate_value)
     activated = gate_value * sigmoid_gate
 
+    half = tok // 2
     hidden_all = lax.all_gather(hidden, "dp", axis=0, tiled=True)
-    next_all = lax.all_gather(next_hidden, "dp", axis=0, tiled=True)
+    first_own, hidden_all = lax.optimization_barrier((next_hidden[:half], hidden_all))
+    first_next = lax.all_gather(first_own, "dp", axis=0, tiled=True)
     grad_rows = lax.all_to_all(grad_out.T, "dp", 0, 1, tiled=True)
 
     grad_hidden = jnp.dot(grad_out, down_weight, preferred_element_type=jnp.float32)
@@ -106,34 +108,47 @@
     moment_one, moment_two, new_shard = owner_update(
         me, grad_rows, hidden_all, first_moment, second_moment, down_weight, tok
     )
+    gate_grad, up_grad, new_shard = lax.optimization_barrier((gate_grad, up_grad, new_shard))
 
-    partial_out = lax.dot_general(
-        new_shard, next_all, (((1,), (1,)), ((), ())), preferred_element_type=jnp.float32
-    )
-    summed = (
-        lax.psum_scatter(partial_out, "tensor", scatter_dimension=1, tiled=True)
-        .astype(jnp.bfloat16)
-        .T
-    )
+    width = n_dp * half // n_t
+    summed_parts = []
+    next_part = first_next
+    for c in range(2):
+        partial_out = lax.dot_general(
+            new_shard, next_part, (((1,), (1,)), ((), ())), preferred_element_type=jnp.float32
+        )
+        if c == 0:
+            second_own, partial_out = lax.optimization_barrier((next_hidden[half:], partial_out))
+            next_part = lax.all_gather(second_own, "dp", axis=0, tiled=True)
+            blocks = lax.all_to_all(partial_out, "tensor", 1, 0, tiled=True)
+            blocks, next_part = lax.optimization_barrier((blocks, next_part))
+            total = jnp.sum(jnp.reshape(blocks, (n_t,) + partial_out.shape[:1] + (width,)), axis=0)
+        else:
+            total = lax.psum_scatter(partial_out, "tensor", scatter_dimension=1, tiled=True)
+        summed_parts.append(total.astype(jnp.bfloat16).T)
+
     sub = me % group
-    pieces = []
-    for k in range(group):
-        s = (sub + k) % group
-        piece = lax.dynamic_slice_in_dim(summed, s * tok, tok, 0)
-        perm = []
-        for i in range(n_dp):
-            for j in range(n_t):
-                si = (i % group + k) % group
-                dst = (group * j + si) * n_t + i // group
-                perm.append((i * n_t + j, dst))
-        pieces.append(lax.ppermute(piece, ("dp", "tensor"), perm))
-    ordered = []
-    for r in range(group):
-        chosen = pieces[0]
-        for k in range(1, group):
-            chosen = jnp.where((sub - k) % group == r, pieces[k], chosen)
-        ordered.append(chosen)
-    next_out = jnp.concatenate(ordered, axis=1)
+    halves = []
+    for c in range(2):
+        pieces = []
+        for k in range(group):
+            s = (sub + k) % group
+            piece = lax.dynamic_slice_in_dim(summed_parts[c], s * half, half, 0)
+            perm = []
+            for i in range(n_dp):
+                for j in range(n_t):
+                    si = (i % group + k) % group
+                    dst = (group * j + si) * n_t + i // group
+                    perm.append((i * n_t + j, dst))
+            pieces.append(lax.ppermute(piece, ("dp", "tensor"), perm))
+        ordered = []
+        for r in range(group):
+            chosen = pieces[0]
+            for k in range(1, group):
+                chosen = jnp.where((sub - k) % group == r, pieces[k], chosen)
+            ordered.append(chosen)
+        halves.append(jnp.concatenate(ordered, axis=1))
+    next_out = jnp.concatenate(halves, axis=0)
     return (gate_grad, up_grad, moment_one, moment_two, next_out)
 
 

time: 334 us -> 316 us (0.946)
  waiting for transfers between devices: 245 us -> 155 us
  blocking collectives: 0 us -> 51.9 us
  starting transfers between devices: 9.51 us -> 23.7 us
  matrix products: 29.5 us -> 34.4 us
    all_gather x1 -> x2, waiting for transfers between devices: 58.9 us -> 3.81 us  [the longest x1 3.81 us: shards(): first_next = lax.all_gather(first_own, 'dp', axis=0, tiled=True)]
    all_to_all x0 -> x1, blocking collectives: none -> 51.9 us  [shards(): blocks = lax.all_to_all(partial_out, 'tensor', 1, 0, tiled=True)]
    reduce_scatter x1, waiting for transfers between devices: 76.5 us -> 39.9 us  [shards(): lax.psum_scatter(partial_out, 'tensor', scatter_dimension=1, tiled=True)]
    all_gather x1, waiting for transfers between devices: 49.4 us -> 79.8 us  [shards(): hidden_all = lax.all_gather(hidden, 'dp', axis=0, tiled=True)]
    all_to_all x1, waiting for transfers between devices: 42 us -> 17.5 us  [shards(): grad_rows = lax.all_to_all(grad_out.T, 'dp', 0, 1, tiled=True)]
    ppermute x2 -> x4, starting transfers between devices: 4.86 us -> 19.6 us  [shards(): pieces.append(lax.ppermute(piece, ('dp', 'tensor'), perm))]
    dot_general x1 -> x2, matrix products: 13.5 us -> 16.9 us  [shards(): lax.dot_general(new_shard, next_part, (((1,), (1,)), ((), ())), preferred...]
    ppermute x2 -> x4, waiting for transfers between devices: 17 us -> 14 us  [shards(): pieces.append(lax.ppermute(piece, ('dp', 'tensor'), perm))]
  transfers between devices with their start and end apart: 6 -> 9, of which waited for: 6 -> 6; matrix products, arithmetic and copies ran while one was open for 6% -> 8% of each run, Pallas kernels for 7% -> 7%
where the time goes in v4:
time: 316 us
  waiting for transfers between devices  155 us (49%)
  blocking collectives  51.9 us (16%)
  matrix products  34.4 us (11%)
  starting transfers between devices  23.7 us (8%)
  Pallas kernels  22.3 us (7%)
  between operations  13.9 us (4%)
  local copies, waits for them, and re-layouts  8.84 us (3%)
  other arithmetic  5.69 us (2%)
    all_gather x1, waiting for transfers between devices, shards(): hidden_all = lax.all_gather(hidden, 'dp', axis=0, tiled=True)  79.8 us
    all_to_all x1, blocking collectives, shards(): blocks = lax.all_to_all(partial_out, 'tensor', 1, 0, tiled=True)  51.9 us
    reduce_scatter x1, waiting for transfers between devices, shards(): lax.psum_scatter(partial_out, 'tensor', scatter_dimension=1, tiled=True)  39.9 us
    pallas_call x1, Pallas kernels, owner_update(): pl.pallas_call(functools.partial(adam_kernel, blocks=tokens // tok, tok=t...  22.3 us
    ppermute x4, starting transfers between devices, shards(): pieces.append(lax.ppermute(piece, ('dp', 'tensor'), perm))  19.6 us
    all_to_all x1, waiting for transfers between devices, shards(): grad_rows = lax.all_to_all(grad_out.T, 'dp', 0, 1, tiled=True)  17.5 us
    dot_general x1, matrix products, shards(): jnp.dot(grad_out, down_weight, preferred_element_type=jnp.float32)  17.4 us
    dot_general x2, matrix products, shards(): lax.dot_general(new_shard, next_part, (((1,), (1,)), ((), ())), preferred...  16.9 us
  transfers between devices with their start and end apart: 9, of which 6 were waited for; matrix products, arithmetic and copies ran while one was open for 8% of the time, Pallas kernels for 7%

profile of v4, /device:TPU:3, one launch (start us, length us, event | category | flops | bytes accessed | tf_op | source)
XLA Modules:
  0.0 315.7 jit_solution(5432606212935495337)
XLA Ops:
  7.2 4.4 %fusion.12 = bf16[256,3584]{1,0:T(8,128)(2,1)} fusion(bf16[256,3584]{1,0:T(8,128)(2,1)} %param.9, bf16[256,3584]{1,0:T(8,128)(2,1)} %param.8), kind=kLoop, calls=%fused_computation.17 | loop fusion | flops 7340032 | bytes 5505024 | tf_op jit(solution)/shard_map/convert_element_type | solution.py:89
  11.7 3.0 fusion.13
  14.6 79.8 %all-gather.4.cloned.1.call-done.h_ref = bf16[2048,3584]{1,0:T(8,128)(2,1)} async-done(((bf16[256,3584]{1,0:T(8,128)(2,1)}), bf16[2048,3584]{1,0:T(8,128)(2,1)}) %all-gather.4.cloned.1.call-update) | async-done | bytes 14680080 | tf_op jit(solution)/shard_map/all_gather | solution.py:97
  94.4 2.5 copy.17
  96.9 4.0 %all-to-all-start = ((bf16[8,512,256]{2,1,0:T(8,128)(2,1)}), bf16[8,512,256]{2,1,0:T(8,128)(2,1)S(1)}, u32[]{:S(2)}, u32[]{:S(2)}) async-start(bf16[8,512,256]{2,1,0:T(8,128)(2,1)} %bitcast.31), calls=%async_computation | async-start | bytes 4194304 | tf_op jit(solution)/shard_map/all_to_all | solution.py:100
  100.9 17.4 %fusion.11 = (bf16[256,3584]{1,0:T(8,128)(2,1)}, bf16[256,3584]{1,0:T(8,128)(2,1)}) fusion(bf16[256,3584]{1,0:T(8,128)(2,1)} %param.8, bf16[256,3584]{1,0:T(8,128)(2,1)} %param.9, bf16[256,4096]{1,0:T(8,128)(2,1)} %param.7, bf16[4096,3584]{1,0:T(8,128)(2,1)} %w_ref.1), kind=kOutput, calls=%fused_computation.16 | convolution fusion | flops 7529955328 | bytes 38797312 | tf_op jit(solution)/shard_map/dot_general | solution.py:102
  118.3 17.5 %all-to-all-done = bf16[8,512,256]{2,1,0:T(8,128)(2,1)S(1)} async-done(((bf16[8,512,256]{2,1,0:T(8,128)(2,1)}), bf16[8,512,256]{2,1,0:T(8,128)(2,1)S(1)}, u32[]{:S(2)}, u32[]{:S(2)}) %all-to-all-start) | async-done | bytes 2097184 | tf_op jit(solution)/shard_map/all_to_all | solution.py:100
  135.8 0.3 copy.22
  136.0 22.3 %shard_map.110 = (f32[512,3584]{1,0:T(8,128)}, f32[512,3584]{1,0:T(8,128)}, bf16[512,3584]{1,0:T(8,128)(2,1)S(1)}) custom-call(s32[1]{0:T(128)} %bitcast.me_ref, bf16[512,2048]{1,0:T(8,128)(2,1)S(1)} %bitcast.28, bf16[2048,3584]{1,0:T(8,128)(2,1)} %all-gather.4.cloned.1.call-done.h_ref, f32[512,3584]{1,0:T(8,128)} %m1_ref.1, f32[512,3584]{1,0:T(8,128)} %m2_ref.1, ...), custom_call_target="tpu_custom_call" | custom-call | flops 7516192768 | bytes 53477376 | tf_op jit(solution)/shard_map/pallas_call | solution.py:63
  158.3 1.9 copy-done
  160.2 3.8 %all-gather.6.cloned.1.call-done = bf16[1024,3584]{1,0:T(8,128)(2,1)} async-done(((bf16[128,3584]{1,0:T(8,128)(2,1)}), bf16[1024,3584]{1,0:T(8,128)(2,1)}) %all-gather.6.cloned.1.call-update) | async-done | bytes 7340048 | tf_op jit(solution)/shard_map/all_gather | solution.py:99
  164.0 7.4 %fusion.14 = f32[512,1024]{1,0:T(8,128)S(1)} fusion(bf16[512,3584]{1,0:T(8,128)(2,1)} %copy-done, bf16[1024,3584]{1,0:T(8,128)(2,1)} %all-gather.6.cloned.1.call-done), kind=kOutput, calls=%fused_computation.29 | convolution fusion | flops 3758096384 | bytes 13107200 | tf_op jit(solution)/shard_map/dot_general | solution.py:117
  171.5 0.2 copy.24
  171.6 51.9 %all_to_all.38 = f32[512,4,256]{2,0,1:T(8,128)S(1)} all-to-all(f32[512,4,256]{2,0,1:T(8,128)S(1)} %bitcast.32), channel_id=1, replica_groups=mesh['dp'=8,'tensor'=4] {'tensor'}, dimensions={1} | all-to-all | bytes 4194304 | tf_op jit(solution)/shard_map/all_to_all | solution.py:123
  223.6 9.6 %fusion.15 = f32[512,1024]{1,0:T(8,128)} fusion(bf16[512,3584]{1,0:T(8,128)(2,1)} %copy-done, bf16[1024,3584]{1,0:T(8,128)(2,1)} %all-gather.8.cloned.1.call-done), kind=kOutput, calls=%fused_computation.30 | convolution fusion | flops 3758096384 | bytes 13107200 | tf_op jit(solution)/shard_map/dot_general | solution.py:117
  233.4 1.2 collective-permute-start
  234.6 4.3 %collective-permute-start.1 = (bf16[128,512]{0,1:T(8,128)(2,1)S(1)}, bf16[128,512]{0,1:T(8,128)(2,1)S(1)}, u32[]{:S(2)}, u32[]{:S(2)}) collective-permute-start(bf16[128,512]{0,1:T(8,128)(2,1)S(1)} %get-tuple-element.56), channel_id=1, source_target_pairs={{0,0},{1,8},{2,16},{3,24},{4,4},{5,12},{6,20},{7,28},{8,1},{9,9},{... | collective-permute-start | bytes 393224 | tf_op jit(solution)/shard_map/ppermute | solution.py:143
  239.0 39.9 %reduce-scatter.2.cloned.1.call-done = f32[512,256]{1,0:T(8,128)} async-done(((f32[512,1024]{1,0:T(8,128)}), f32[512,256]{1,0:T(8,128)}) %reduce-scatter.2.cloned.1.call-update) | async-done | bytes 524304 | tf_op jit(solution)/shard_map/reduce_scatter | solution.py:127
  278.9 1.1 convert_element_type.35
  280.0 12.1 %collective-permute-start.2 = (bf16[128,512]{0,1:T(8,128)(2,1)S(1)}, bf16[128,512]{0,1:T(8,128)(2,1)S(1)}, u32[]{:S(2)}, u32[]{:S(2)}) collective-permute-start(bf16[128,512]{0,1:T(8,128)(2,1)S(1)} %get-tuple-element.61), channel_id=1, source_target_pairs={{0,4},{1,12},{2,20},{3,28},{4,0},{5,8},{6,16},{7,24},{8,5},{9,13},... | collective-permute-start | bytes 393224 | tf_op jit(solution)/shard_map/ppermute | solution.py:143
  292.1 1.9 collective-permute-start.3
  294.1 2.5 collective-permute-done.2
  296.6 11.5 %collective-permute-done.3 = bf16[128,512]{0,1:T(8,128)(2,1)S(1)} collective-permute-done((bf16[128,512]{0,1:T(8,128)(2,1)S(1)}, bf16[128,512]{0,1:T(8,128)(2,1)S(1)}, u32[]{:S(2)}, u32[]{:S(2)}) %collective-permute-start.3) | collective-permute-done | bytes 131104 | tf_op jit(solution)/shard_map/ppermute | solution.py:143
  308.2 1.0 copy.20
  (20 shorter events, 0.5 us)
Async XLA Ops:
  7.2 87.2 %all-gather.4.cloned.1.call-start = ((), (), s32[]{:S(2)}) async-start(), calls=%async_computation.3 | async-start | bytes 16515072 | tf_op jit(solution)/shard_map/all_gather | solution.py:97
  11.6 82.9 %copy-start.1 = (bf16[256,4096]{1,0:T(8,128)(2,1)S(1)}, bf16[256,4096]{1,0:T(8,128)(2,1)}, u32[]{:S(2)}) copy-start(bf16[256,4096]{1,0:T(8,128)(2,1)} %param.7) | copy-start | bytes 6291460
  11.6 152.4 %all-gather.6.cloned.1.call-start = ((), (), s32[]{:S(2)}) async-start(), calls=%async_computation.4 | async-start | bytes 8257536 | tf_op jit(solution)/shard_map/all_gather | solution.py:99
  96.9 38.9 %all-to-all-start = ((bf16[8,512,256]{2,1,0:T(8,128)(2,1)}), bf16[8,512,256]{2,1,0:T(8,128)(2,1)S(1)}, u32[]{:S(2)}, u32[]{:S(2)}) async-start(bf16[8,512,256]{2,1,0:T(8,128)(2,1)} %bitcast.31), calls=%async_computation | async-start | bytes 4194304 | tf_op jit(solution)/shard_map/all_to_all | solution.py:100
  100.9 122.7 %all-gather.8.cloned.1.call-start = ((), (), s32[]{:S(2)}) async-start(), calls=%async_computation.5 | async-start | bytes 8257536 | tf_op jit(solution)/shard_map/all_gather | solution.py:122
  158.3 1.9 copy-start
  171.4 107.5 %reduce-scatter.2.cloned.1.call-start = ((), (), s32[]{:S(2)}) async-start(), calls=%async_computation.6 | async-start | bytes 2621440 | tf_op jit(solution)/shard_map/reduce_scatter | solution.py:127
  233.4 60.6 %collective-permute-start = (bf16[128,512]{0,1:T(8,128)(2,1)S(1)}, bf16[128,512]{0,1:T(8,128)(2,1)S(1)}, u32[]{:S(2)}, u32[]{:S(2)}) collective-permute-start(bf16[128,512]{0,1:T(8,128)(2,1)S(1)} %get-tuple-element.57), channel_id=1, source_target_pairs={{0,4},{1,12},{2,20},{3,28},{4,0},{5,8},{6,16},{7,24},{8,5},{9,13},... | collective-permute-start | bytes 393224 | tf_op jit(solution)/shard_map/ppermute | solution.py:143
  234.6 59.4 %collective-permute-start.1 = (bf16[128,512]{0,1:T(8,128)(2,1)S(1)}, bf16[128,512]{0,1:T(8,128)(2,1)S(1)}, u32[]{:S(2)}, u32[]{:S(2)}) collective-permute-start(bf16[128,512]{0,1:T(8,128)(2,1)S(1)} %get-tuple-element.56), channel_id=1, source_target_pairs={{0,0},{1,8},{2,16},{3,24},{4,4},{5,12},{6,20},{7,28},{8,1},{9,9},{... | collective-permute-start | bytes 393224 | tf_op jit(solution)/shard_map/ppermute | solution.py:143
  280.0 16.6 %collective-permute-start.2 = (bf16[128,512]{0,1:T(8,128)(2,1)S(1)}, bf16[128,512]{0,1:T(8,128)(2,1)S(1)}, u32[]{:S(2)}, u32[]{:S(2)}) collective-permute-start(bf16[128,512]{0,1:T(8,128)(2,1)S(1)} %get-tuple-element.61), channel_id=1, source_target_pairs={{0,4},{1,12},{2,20},{3,28},{4,0},{5,8},{6,16},{7,24},{8,5},{9,13},... | collective-permute-start | bytes 393224 | tf_op jit(solution)/shard_map/ppermute | solution.py:143
  292.1 16.0 %collective-permute-start.3 = (bf16[128,512]{0,1:T(8,128)(2,1)S(1)}, bf16[128,512]{0,1:T(8,128)(2,1)S(1)}, u32[]{:S(2)}, u32[]{:S(2)}) collective-permute-start(bf16[128,512]{0,1:T(8,128)(2,1)S(1)} %get-tuple-element.60), channel_id=1, source_target_pairs={{0,0},{1,8},{2,16},{3,24},{4,4},{5,12},{6,20},{7,28},{8,1},{9,9},{... | collective-permute-start | bytes 393224 | tf_op jit(solution)/shard_map/ppermute | solution.py:143
Sparse Core Ops, SparseCore 0:
  11.7 82.6 all-gather.3
  96.3 67.6 all-gather.5
  171.6 49.9 all-gather.7
  233.3 45.5 reduce-scatter.1

commit v5 on v4

--- a/solution.py
+++ b/solution.py
@@ -97,6 +97,8 @@
     hidden_all = lax.all_gather(hidden, "dp", axis=0, tiled=True)
     first_own, hidden_all = lax.optimization_barrier((next_hidden[:half], hidden_all))
     first_next = lax.all_gather(first_own, "dp", axis=0, tiled=True)
+    second_own, first_next = lax.optimization_barrier((next_hidden[half:], first_next))
+    next_part = lax.all_gather(second_own, "dp", axis=0, tiled=True)
     grad_rows = lax.all_to_all(grad_out.T, "dp", 0, 1, tiled=True)
 
     grad_hidden = jnp.dot(grad_out, down_weight, preferred_element_type=jnp.float32)
@@ -112,19 +114,21 @@
 
     width = n_dp * half // n_t
     summed_parts = []
-    next_part = first_next
     for c in range(2):
         partial_out = lax.dot_general(
-            new_shard, next_part, (((1,), (1,)), ((), ())), preferred_element_type=jnp.float32
+            new_shard, first_next if c == 0 else next_part, (((1,), (1,)), ((), ())), preferred_element_type=jnp.float32
         )
         if c == 0:
-            second_own, partial_out = lax.optimization_barrier((next_hidden[half:], partial_out))
-            next_part = lax.all_gather(second_own, "dp", axis=0, tiled=True)
             blocks = lax.all_to_all(partial_out, "tensor", 1, 0, tiled=True)
             blocks, next_part = lax.optimization_barrier((blocks, next_part))
-            total = jnp.sum(jnp.reshape(blocks, (n_t,) + partial_out.shape[:1] + (width,)), axis=0)
+            blocks = jnp.reshape(blocks, (n_t,) + partial_out.shape[:1] + (width,))
+            total = jnp.sum(blocks, axis=0)
         else:
-            total = lax.psum_scatter(partial_out, "tensor", scatter_dimension=1, tiled=True)
+            total = lax.dynamic_slice_in_dim(partial_out, col * width, width, 1)
+            for s in range(1, n_t):
+                block = lax.dynamic_slice_in_dim(partial_out, ((col + s) % n_t) * width, width, 1)
+                moved = lax.ppermute(block, "tensor", [(j, (j + s) % n_t) for j in range(n_t)])
+                total = total + moved
         summed_parts.append(total.astype(jnp.bfloat16).T)
 
     sub = me % group

time: 316 us -> 363 us (1.15)
  waiting for transfers between devices: 155 us -> 235 us
  blocking collectives: 51.9 us -> 0 us
  starting transfers between devices: 23.7 us -> 42 us
  matrix products: 34.4 us -> 28.7 us
  local copies, waits for them, and re-layouts: 8.84 us -> 13.8 us
    all_to_all x1 -> x0, blocking collectives: 51.9 us -> none  [shards(): blocks = lax.all_to_all(partial_out, 'tensor', 1, 0, tiled=True)]
    all_gather x1, waiting for transfers between devices: 3.81 us -> 52.4 us  [shards(): first_next = lax.all_gather(first_own, 'dp', axis=0, tiled=True)]
    all_to_all x0 -> x1, waiting for transfers between devices: none -> 47.7 us  [shards(): blocks = lax.all_to_all(partial_out, 'tensor', 1, 0, tiled=True)]
    reduce_scatter x1 -> x0, waiting for transfers between devices: 39.9 us -> none  [shards(): lax.psum_scatter(partial_out, 'tensor', scatter_dimension=1, tiled=True)]
    ppermute x0 -> x3, waiting for transfers between devices: none -> 27 us  [shards(): lax.ppermute(block, 'tensor', [(j, (j + s) % n_t) for j in range(n_t)])]
    ppermute x4, starting transfers between devices: 19.6 us -> 30.3 us  [shards(): pieces.append(lax.ppermute(piece, ('dp', 'tensor'), perm))]
    dot_general x2, matrix products: 16.9 us -> 11.3 us  [shards(): lax.dot_general(new_shard, first_next if c == 0 else next_part, (((1,), (...]
    all_to_all x0 -> x1, starting transfers between devices: none -> 4.32 us  [shards(): blocks = lax.all_to_all(partial_out, 'tensor', 1, 0, tiled=True)]
  transfers between devices with their start and end apart: 9 -> 12, of which waited for: 6 -> 8; matrix products, arithmetic and copies ran while one was open for 8% -> 9% of each run, Pallas kernels for 7% -> 6%
where the time goes in v5:
time: 363 us; the launch traced here: 362 us
  waiting for transfers between devices  235 us (65%)
  starting transfers between devices  42 us (12%)
  matrix products  28.7 us (8%)
  Pallas kernels  22.7 us (6%)
  between operations  13.9 us (4%)
  local copies, waits for them, and re-layouts  13.8 us (4%)
  other arithmetic  6.09 us (2%)
    all_gather x1, waiting for transfers between devices, shards(): hidden_all = lax.all_gather(hidden, 'dp', axis=0, tiled=True)  79.8 us
    all_gather x1, waiting for transfers between devices, shards(): first_next = lax.all_gather(first_own, 'dp', axis=0, tiled=True)  52.4 us
    all_to_all x1, waiting for transfers between devices, shards(): blocks = lax.all_to_all(partial_out, 'tensor', 1, 0, tiled=True)  47.7 us
    ppermute x4, starting transfers between devices, shards(): pieces.append(lax.ppermute(piece, ('dp', 'tensor'), perm))  30.3 us
    ppermute x3, waiting for transfers between devices, shards(): lax.ppermute(block, 'tensor', [(j, (j + s) % n_t) for j in range(n_t)])  27 us
    pallas_call x1, Pallas kernels, owner_update(): pl.pallas_call(functools.partial(adam_kernel, blocks=tokens // tok, tok=t...  22.7 us
    all_to_all x1, waiting for transfers between devices, shards(): grad_rows = lax.all_to_all(grad_out.T, 'dp', 0, 1, tiled=True)  17.5 us
    dot_general x1, matrix products, shards(): jnp.dot(grad_out, down_weight, preferred_element_type=jnp.float32)  17.4 us
  transfers between devices with their start and end apart: 12, of which 8 were waited for; matrix products, arithmetic and copies ran while one was open for 9% of the time, Pallas kernels for 6%

profile of v5, /device:TPU:3, one launch (start us, length us, event | category | flops | bytes accessed | tf_op | source)
XLA Modules:
  0.0 361.8 jit_solution(8536432051692626280)
XLA Ops:
  7.2 4.4 %fusion.12 = bf16[256,3584]{1,0:T(8,128)(2,1)} fusion(bf16[256,3584]{1,0:T(8,128)(2,1)} %param.9, bf16[256,3584]{1,0:T(8,128)(2,1)} %param.8), kind=kLoop, calls=%fused_computation.17 | loop fusion | flops 7340032 | bytes 5505024 | tf_op jit(solution)/shard_map/convert_element_type | solution.py:89
  11.7 2.9 fusion.13
  14.6 79.8 %all-gather.4.cloned.1.call-done.h_ref = bf16[2048,3584]{1,0:T(8,128)(2,1)} async-done(((bf16[256,3584]{1,0:T(8,128)(2,1)}), bf16[2048,3584]{1,0:T(8,128)(2,1)}) %all-gather.4.cloned.1.call-update) | async-done | bytes 14680080 | tf_op jit(solution)/shard_map/all_gather | solution.py:97
  94.5 52.4 %all-gather.6.cloned.1.call-done = bf16[1024,3584]{1,0:T(8,128)(2,1)} async-done(((bf16[128,3584]{1,0:T(8,128)(2,1)}), bf16[1024,3584]{1,0:T(8,128)(2,1)}) %all-gather.6.cloned.1.call-update) | async-done | bytes 7340048 | tf_op jit(solution)/shard_map/all_gather | solution.py:99
  146.9 2.5 copy.17
  149.4 4.0 %all-to-all-start = ((bf16[8,512,256]{2,1,0:T(8,128)(2,1)}), bf16[8,512,256]{2,1,0:T(8,128)(2,1)S(1)}, u32[]{:S(2)}, u32[]{:S(2)}) async-start(bf16[8,512,256]{2,1,0:T(8,128)(2,1)} %bitcast.32), calls=%async_computation | async-start | bytes 4194304 | tf_op jit(solution)/shard_map/all_to_all | solution.py:102
  153.3 17.4 %fusion.11 = (bf16[256,3584]{1,0:T(8,128)(2,1)}, bf16[256,3584]{1,0:T(8,128)(2,1)}) fusion(bf16[256,3584]{1,0:T(8,128)(2,1)} %param.8, bf16[256,3584]{1,0:T(8,128)(2,1)} %param.9, bf16[256,4096]{1,0:T(8,128)(2,1)} %param.7, bf16[4096,3584]{1,0:T(8,128)(2,1)} %w_ref.1), kind=kOutput, calls=%fused_computation.16 | convolution fusion | flops 7529955328 | bytes 38797312 | tf_op jit(solution)/shard_map/dot_general | solution.py:104
  170.7 17.5 %all-to-all-done = bf16[8,512,256]{2,1,0:T(8,128)(2,1)S(1)} async-done(((bf16[8,512,256]{2,1,0:T(8,128)(2,1)}), bf16[8,512,256]{2,1,0:T(8,128)(2,1)S(1)}, u32[]{:S(2)}, u32[]{:S(2)}) %all-to-all-start) | async-done | bytes 2097184 | tf_op jit(solution)/shard_map/all_to_all | solution.py:102
  189.5 2.0 copy.22
  191.6 22.7 %shard_map.110 = (f32[512,3584]{1,0:T(8,128)}, f32[512,3584]{1,0:T(8,128)}, bf16[512,3584]{1,0:T(8,128)(2,1)S(1)}) custom-call(s32[1]{0:T(128)} %bitcast.me_ref, bf16[512,2048]{1,0:T(8,128)(2,1)S(1)} %bitcast.28, bf16[2048,3584]{1,0:T(8,128)(2,1)} %all-gather.4.cloned.1.call-done.h_ref, f32[512,3584]{1,0:T(8,128)} %m1_ref.1, f32[512,3584]{1,0:T(8,128)} %m2_ref.1, ...), custom_call_target="tpu_custom_call" | custom-call | flops 7516192768 | bytes 53477376 | tf_op jit(solution)/shard_map/pallas_call | solution.py:63
  214.3 4.0 %fusion.14 = f32[512,1024]{1,0:T(8,128)S(1)} fusion(bf16[512,3584]{1,0:T(8,128)(2,1)S(1)} %get-tuple-element.29, bf16[1024,3584]{1,0:T(8,128)(2,1)S(1)} %bitcast.36), kind=kOutput, calls=%fused_computation.33 | convolution fusion | flops 3758096384 | bytes 13107200 | tf_op jit(solution)/shard_map/dot_general | solution.py:118
  218.3 1.5 copy.24
  219.8 4.3 %all-to-all-start.1 = ((f32[512,4,256]{2,0,1:T(8,128)}), f32[512,4,256]{2,0,1:T(8,128)S(1)}, u32[]{:S(2)}, u32[]{:S(2)}) async-start(f32[512,4,256]{2,0,1:T(8,128)} %bitcast.30), calls=%async_computation.1 | async-start | bytes 4194304 | tf_op jit(solution)/shard_map/all_to_all | solution.py:122
  224.2 47.7 %all-to-all-done.1 = f32[512,4,256]{2,0,1:T(8,128)S(1)} async-done(((f32[512,4,256]{2,0,1:T(8,128)}), f32[512,4,256]{2,0,1:T(8,128)S(1)}, u32[]{:S(2)}, u32[]{:S(2)}) %all-to-all-start.1) | async-done | bytes 2097184 | tf_op jit(solution)/shard_map/all_to_all | solution.py:122
  271.9 7.4 %fusion.15 = f32[512,1024]{1,0:T(8,128)S(1)} fusion(bf16[512,3584]{1,0:T(8,128)(2,1)} %copy-done, bf16[1024,3584]{1,0:T(8,128)(2,1)} %all-gather.8.cloned.1.call-done), kind=kOutput, calls=%fused_computation.34 | convolution fusion | flops 3758096384 | bytes 13107200 | tf_op jit(solution)/shard_map/dot_general | solution.py:118
  283.0 2.0 collective-permute-start.4
  285.3 6.1 %collective-permute-start.1 = (bf16[128,512]{0,1:T(8,128)(2,1)S(1)}, bf16[128,512]{0,1:T(8,128)(2,1)S(1)}, u32[]{:S(2)}, u32[]{:S(2)}) collective-permute-start(bf16[128,512]{0,1:T(8,128)(2,1)S(1)} %get-tuple-element.59), channel_id=1, source_target_pairs={{0,0},{1,8},{2,16},{3,24},{4,4},{5,12},{6,20},{7,28},{8,1},{9,9},{... | collective-permute-start | bytes 393224 | tf_op jit(solution)/shard_map/ppermute | solution.py:147
  291.4 4.5 %collective-permute-done.2 = f32[512,256]{1,0:T(8,128)S(1)} collective-permute-done((f32[512,256]{1,0:T(8,128)}, f32[512,256]{1,0:T(8,128)S(1)}, u32[]{:S(2)}, u32[]{:S(2)}) %collective-permute-start.2) | collective-permute-done | bytes 524320 | tf_op jit(solution)/shard_map/ppermute | solution.py:130
  295.9 22.5 %collective-permute-done.3 = f32[512,256]{1,0:T(8,128)} collective-permute-done((f32[512,256]{1,0:T(8,128)}, f32[512,256]{1,0:T(8,128)}, u32[]{:S(2)}, u32[]{:S(2)}) %collective-permute-start.3) | collective-permute-done | bytes 524320 | tf_op jit(solution)/shard_map/ppermute | solution.py:130
  318.4 1.5 add_convert_fusion
  319.9 22.2 %collective-permute-start.5 = (bf16[128,512]{0,1:T(8,128)(2,1)S(1)}, bf16[128,512]{0,1:T(8,128)(2,1)S(1)}, u32[]{:S(2)}, u32[]{:S(2)}) collective-permute-start(bf16[128,512]{0,1:T(8,128)(2,1)S(1)} %get-tuple-element.64), channel_id=1, source_target_pairs={{0,4},{1,12},{2,20},{3,28},{4,0},{5,8},{6,16},{7,24},{8,5},{9,13},... | collective-permute-start | bytes 393224 | tf_op jit(solution)/shard_map/ppermute | solution.py:147
  342.1 1.9 collective-permute-start.6
  344.1 8.5 %collective-permute-done.5 = bf16[128,512]{0,1:T(8,128)(2,1)S(1)} collective-permute-done((bf16[128,512]{0,1:T(8,128)(2,1)S(1)}, bf16[128,512]{0,1:T(8,128)(2,1)S(1)}, u32[]{:S(2)}, u32[]{:S(2)}) %collective-permute-start.5) | collective-permute-done | bytes 131104 | tf_op jit(solution)/shard_map/ppermute | solution.py:147
  352.6 1.6 collective-permute-done.6
  (34 shorter events, 6.6 us)
Async XLA Ops:
  7.2 87.2 %all-gather.4.cloned.1.call-start = ((), (), s32[]{:S(2)}) async-start(), calls=%async_computation.2 | async-start | bytes 16515072 | tf_op jit(solution)/shard_map/all_gather | solution.py:97
  11.6 135.3 %copy-start.3 = (bf16[256,4096]{1,0:T(8,128)(2,1)S(1)}, bf16[256,4096]{1,0:T(8,128)(2,1)}, u32[]{:S(2)}) copy-start(bf16[256,4096]{1,0:T(8,128)(2,1)} %param.7) | copy-start | bytes 6291460
  11.6 135.3 %all-gather.6.cloned.1.call-start = ((), (), s32[]{:S(2)}) async-start(), calls=%async_computation.3 | async-start | bytes 8257536 | tf_op jit(solution)/shard_map/all_gather | solution.py:99
  94.4 177.5 %all-gather.8.cloned.1.call-start = ((), (), s32[]{:S(2)}) async-start(), calls=%async_computation.4 | async-start | bytes 8257536 | tf_op jit(solution)/shard_map/all_gather | solution.py:101
  149.4 38.9 %all-to-all-start = ((bf16[8,512,256]{2,1,0:T(8,128)(2,1)}), bf16[8,512,256]{2,1,0:T(8,128)(2,1)S(1)}, u32[]{:S(2)}, u32[]{:S(2)}) async-start(bf16[8,512,256]{2,1,0:T(8,128)(2,1)} %bitcast.32), calls=%async_computation | async-start | bytes 4194304 | tf_op jit(solution)/shard_map/all_to_all | solution.py:102
  188.2 1.3 copy-start.1
  189.5 24.8 %slice-start = ((s8[7340032]{0:T(1024)(128)(4,1)}), s8[4194304]{0:T(1024)(128)(4,1)S(1)}, s32[]{:S(2)}) async-start(s8[7340032]{0:T(1024)(128)(4,1)} %bitcast.35), calls=%async_computation.5 | async-start | bytes 8388608
  191.6 22.8 %slice-start.1 = ((s8[7340032]{0:T(1024)(128)(4,1)}), s8[3145728]{0:T(1024)(128)(4,1)S(1)}, s32[]{:S(2)}) async-start(s8[7340032]{0:T(1024)(128)(4,1)} %bitcast.35), calls=%async_computation.6 | async-start | bytes 6291456
  214.3 4.0 %copy-start = (bf16[512,3584]{1,0:T(8,128)(2,1)}, bf16[512,3584]{1,0:T(8,128)(2,1)S(1)}, u32[]{:S(2)}) copy-start(bf16[512,3584]{1,0:T(8,128)(2,1)S(1)} %get-tuple-element.29) | copy-start | bytes 11010052
  219.8 52.0 %all-to-all-start.1 = ((f32[512,4,256]{2,0,1:T(8,128)}), f32[512,4,256]{2,0,1:T(8,128)S(1)}, u32[]{:S(2)}, u32[]{:S(2)}) async-start(f32[512,4,256]{2,0,1:T(8,128)} %bitcast.30), calls=%async_computation.1 | async-start | bytes 4194304 | tf_op jit(solution)/shard_map/all_to_all | solution.py:122
  279.3 1.4 copy-start.2
  281.8 14.1 %collective-permute-start.2 = (f32[512,256]{1,0:T(8,128)}, f32[512,256]{1,0:T(8,128)S(1)}, u32[]{:S(2)}, u32[]{:S(2)}) collective-permute-start(f32[512,256]{1,0:T(8,128)} %get-tuple-element.52), channel_id=1, source_target_pairs={{0,1},{1,2},{2,3},{3,0},{4,5},{5,6},{6,7},{7,4},{8,9},{9,10},{10,1... | collective-permute-start | bytes 1572872 | tf_op jit(solution)/shard_map/ppermute | solution.py:130
  281.8 36.6 %collective-permute-start.3 = (f32[512,256]{1,0:T(8,128)}, f32[512,256]{1,0:T(8,128)}, u32[]{:S(2)}, u32[]{:S(2)}) collective-permute-start(f32[512,256]{1,0:T(8,128)} %get-tuple-element.54), channel_id=1, source_target_pairs={{0,2},{1,3},{2,0},{3,1},{4,6},{5,7},{6,4},{7,5},{8,10},{9,11},{10,... | collective-permute-start | bytes 1572872 | tf_op jit(solution)/shard_map/ppermute | solution.py:130
  283.0 35.4 %collective-permute-start.4 = (f32[512,256]{1,0:T(8,128)S(1)}, f32[512,256]{1,0:T(8,128)}, u32[]{:S(2)}, u32[]{:S(2)}) collective-permute-start(f32[512,256]{1,0:T(8,128)S(1)} %get-tuple-element.53), channel_id=1, source_target_pairs={{0,3},{1,0},{2,1},{3,2},{4,7},{5,4},{6,5},{7,6},{8,11},{9,8},{10,9... | collective-permute-start | bytes 1572872 | tf_op jit(solution)/shard_map/ppermute | solution.py:130
  285.2 58.8 %collective-permute-start = (bf16[128,512]{0,1:T(8,128)(2,1)S(1)}, bf16[128,512]{0,1:T(8,128)(2,1)S(1)}, u32[]{:S(2)}, u32[]{:S(2)}) collective-permute-start(bf16[128,512]{0,1:T(8,128)(2,1)S(1)} %get-tuple-element.60), channel_id=1, source_target_pairs={{0,4},{1,12},{2,20},{3,28},{4,0},{5,8},{6,16},{7,24},{8,5},{9,13},... | collective-permute-start | bytes 393224 | tf_op jit(solution)/shard_map/ppermute | solution.py:147
  285.3 58.7 %collective-permute-start.1 = (bf16[128,512]{0,1:T(8,128)(2,1)S(1)}, bf16[128,512]{0,1:T(8,128)(2,1)S(1)}, u32[]{:S(2)}, u32[]{:S(2)}) collective-permute-start(bf16[128,512]{0,1:T(8,128)(2,1)S(1)} %get-tuple-element.59), channel_id=1, source_target_pairs={{0,0},{1,8},{2,16},{3,24},{4,4},{5,12},{6,20},{7,28},{8,1},{9,9},{... | collective-permute-start | bytes 393224 | tf_op jit(solution)/shard_map/ppermute | solution.py:147
  319.9 32.7 %collective-permute-start.5 = (bf16[128,512]{0,1:T(8,128)(2,1)S(1)}, bf16[128,512]{0,1:T(8,128)(2,1)S(1)}, u32[]{:S(2)}, u32[]{:S(2)}) collective-permute-start(bf16[128,512]{0,1:T(8,128)(2,1)S(1)} %get-tuple-element.64), channel_id=1, source_target_pairs={{0,4},{1,12},{2,20},{3,28},{4,0},{5,8},{6,16},{7,24},{8,5},{9,13},... | collective-permute-start | bytes 393224 | tf_op jit(solution)/shard_map/ppermute | solution.py:147
  342.1 12.1 %collective-permute-start.6 = (bf16[128,512]{0,1:T(8,128)(2,1)S(1)}, bf16[128,512]{0,1:T(8,128)(2,1)S(1)}, u32[]{:S(2)}, u32[]{:S(2)}) collective-permute-start(bf16[128,512]{0,1:T(8,128)(2,1)S(1)} %get-tuple-element.63), channel_id=1, source_target_pairs={{0,0},{1,8},{2,16},{3,24},{4,4},{5,12},{6,20},{7,28},{8,1},{9,9},{... | collective-permute-start | bytes 393224 | tf_op jit(solution)/shard_map/ppermute | solution.py:147
Sparse Core Ops, SparseCore 0:
  11.7 82.6 all-gather.3
  96.9 49.9 all-gather.5
  148.8 67.6 all-gather.7

commit v6 on v4

--- a/solution.py
+++ b/solution.py
@@ -124,7 +124,12 @@
             blocks, next_part = lax.optimization_barrier((blocks, next_part))
             total = jnp.sum(jnp.reshape(blocks, (n_t,) + partial_out.shape[:1] + (width,)), axis=0)
         else:
-            total = lax.psum_scatter(partial_out, "tensor", scatter_dimension=1, tiled=True)
+            total = lax.dynamic_slice_in_dim(partial_out, col * width, width, 1)
+            for s in range(1, n_t):
+                block = lax.dynamic_slice_in_dim(partial_out, ((col + s) % n_t) * width, width, 1)
+                total = total + lax.ppermute(
+                    block, "tensor", [(j, (j + s) % n_t) for j in range(n_t)]
+                )
         summed_parts.append(total.astype(jnp.bfloat16).T)
 
     sub = me % group

time: 316 us -> 319 us (level)
  blocking collectives: 51.9 us -> 0 us
  waiting for transfers between devices: 155 us -> 183 us
  starting transfers between devices: 23.7 us -> 44.8 us
  local copies, waits for them, and re-layouts: 8.84 us -> 15.7 us
    all_to_all x1 -> x0, blocking collectives: 51.9 us -> none  [shards(): blocks = lax.all_to_all(partial_out, 'tensor', 1, 0, tiled=True)]
    all_to_all x0 -> x1, waiting for transfers between devices: none -> 47.8 us  [shards(): blocks = lax.all_to_all(partial_out, 'tensor', 1, 0, tiled=True)]
    reduce_scatter x1 -> x0, waiting for transfers between devices: 39.9 us -> none  [shards(): lax.psum_scatter(partial_out, 'tensor', scatter_dimension=1, tiled=True)]
    ppermute x0 -> x3, waiting for transfers between devices: none -> 27 us  [shards(): lax.ppermute(block, 'tensor', [(j, (j + s) % n_t) for j in range(n_t)])]
    ppermute x4, starting transfers between devices: 19.6 us -> 33.2 us  [shards(): pieces.append(lax.ppermute(piece, ('dp', 'tensor'), perm))]
    all_to_all x0 -> x1, starting transfers between devices: none -> 4.32 us  [shards(): blocks = lax.all_to_all(partial_out, 'tensor', 1, 0, tiled=True)]
    ppermute x4, waiting for transfers between devices: 14 us -> 10.2 us  [shards(): pieces.append(lax.ppermute(piece, ('dp', 'tensor'), perm))]
    ppermute x0 -> x3, starting transfers between devices: none -> 3.27 us  [shards(): lax.ppermute(block, 'tensor', [(j, (j + s) % n_t) for j in range(n_t)])]
  transfers between devices with their start and end apart: 9 -> 12, of which waited for: 6 -> 8; matrix products, arithmetic and copies ran while one was open for 8% -> 9% of each run, Pallas kernels for 7% -> 7%
where the time goes in v6:
time: 319 us; the launch traced here: 318 us
  waiting for transfers between devices  183 us (57%)
  starting transfers between devices  44.8 us (14%)
  matrix products  32.1 us (10%)
  Pallas kernels  22.2 us (7%)
  local copies, waits for them, and re-layouts  15.7 us (5%)
  between operations  13.9 us (4%)
  other arithmetic  6.08 us (2%)
    all_gather x1, waiting for transfers between devices, shards(): hidden_all = lax.all_gather(hidden, 'dp', axis=0, tiled=True)  79.8 us
    all_to_all x1, waiting for transfers between devices, shards(): blocks = lax.all_to_all(partial_out, 'tensor', 1, 0, tiled=True)  47.8 us
    ppermute x4, starting transfers between devices, shards(): pieces.append(lax.ppermute(piece, ('dp', 'tensor'), perm))  33.2 us
    ppermute x3, waiting for transfers between devices, shards(): lax.ppermute(block, 'tensor', [(j, (j + s) % n_t) for j in range(n_t)])  27 us
    pallas_call x1, Pallas kernels, owner_update(): pl.pallas_call(functools.partial(adam_kernel, blocks=tokens // tok, tok=t...  22.2 us
    all_to_all x1, waiting for transfers between devices, shards(): grad_rows = lax.all_to_all(grad_out.T, 'dp', 0, 1, tiled=True)  17.5 us
    dot_general x1, matrix products, shards(): jnp.dot(grad_out, down_weight, preferred_element_type=jnp.float32)  17.4 us
    dot_general x2, matrix products, shards(): lax.dot_general(new_shard, next_part, (((1,), (1,)), ((), ())), preferred...  14.7 us
  transfers between devices with their start and end apart: 12, of which 8 were waited for; matrix products, arithmetic and copies ran while one was open for 9% of the time, Pallas kernels for 7%

profile of v6, /device:TPU:3, one launch (start us, length us, event | category | flops | bytes accessed | tf_op | source)
XLA Modules:
  0.0 318.0 jit_solution(15350182177095801326)
XLA Ops:
  7.2 4.4 %fusion.12 = bf16[256,3584]{1,0:T(8,128)(2,1)} fusion(bf16[256,3584]{1,0:T(8,128)(2,1)} %param.9, bf16[256,3584]{1,0:T(8,128)(2,1)} %param.8), kind=kLoop, calls=%fused_computation.17 | loop fusion | flops 7340032 | bytes 5505024 | tf_op jit(solution)/shard_map/convert_element_type | solution.py:89
  11.7 2.9 fusion.13
  14.6 79.8 %all-gather.4.cloned.1.call-done.h_ref = bf16[2048,3584]{1,0:T(8,128)(2,1)} async-done(((bf16[256,3584]{1,0:T(8,128)(2,1)}), bf16[2048,3584]{1,0:T(8,128)(2,1)}) %all-gather.4.cloned.1.call-update) | async-done | bytes 14680080 | tf_op jit(solution)/shard_map/all_gather | solution.py:97
  94.4 2.5 copy.17
  96.9 4.0 %all-to-all-start = ((bf16[8,512,256]{2,1,0:T(8,128)(2,1)}), bf16[8,512,256]{2,1,0:T(8,128)(2,1)S(1)}, u32[]{:S(2)}, u32[]{:S(2)}) async-start(bf16[8,512,256]{2,1,0:T(8,128)(2,1)} %bitcast.32), calls=%async_computation | async-start | bytes 4194304 | tf_op jit(solution)/shard_map/all_to_all | solution.py:100
  100.9 17.4 %fusion.11 = (bf16[256,3584]{1,0:T(8,128)(2,1)}, bf16[256,3584]{1,0:T(8,128)(2,1)}) fusion(bf16[256,3584]{1,0:T(8,128)(2,1)} %param.8, bf16[256,3584]{1,0:T(8,128)(2,1)} %param.9, bf16[256,4096]{1,0:T(8,128)(2,1)} %param.7, bf16[4096,3584]{1,0:T(8,128)(2,1)} %w_ref.1), kind=kOutput, calls=%fused_computation.16 | convolution fusion | flops 7529955328 | bytes 38797312 | tf_op jit(solution)/shard_map/dot_general | solution.py:102
  118.3 17.5 %all-to-all-done = bf16[8,512,256]{2,1,0:T(8,128)(2,1)S(1)} async-done(((bf16[8,512,256]{2,1,0:T(8,128)(2,1)}), bf16[8,512,256]{2,1,0:T(8,128)(2,1)S(1)}, u32[]{:S(2)}, u32[]{:S(2)}) %all-to-all-start) | async-done | bytes 2097184 | tf_op jit(solution)/shard_map/all_to_all | solution.py:100
  137.1 1.9 copy.22
  138.9 22.2 %shard_map.110 = (f32[512,3584]{1,0:T(8,128)}, f32[512,3584]{1,0:T(8,128)}, bf16[512,3584]{1,0:T(8,128)(2,1)S(1)}) custom-call(s32[1]{0:T(128)} %bitcast.me_ref, bf16[512,2048]{1,0:T(8,128)(2,1)S(1)} %bitcast.28, bf16[2048,3584]{1,0:T(8,128)(2,1)} %all-gather.4.cloned.1.call-done.h_ref, f32[512,3584]{1,0:T(8,128)} %m1_ref.1, f32[512,3584]{1,0:T(8,128)} %m2_ref.1, ...), custom_call_target="tpu_custom_call" | custom-call | flops 7516192768 | bytes 53477376 | tf_op jit(solution)/shard_map/pallas_call | solution.py:63
  161.1 1.9 copy-done
  164.0 7.4 %fusion.14 = f32[512,1024]{1,0:T(8,128)S(1)} fusion(bf16[512,3584]{1,0:T(8,128)(2,1)} %copy-done, bf16[1024,3584]{1,0:T(8,128)(2,1)} %all-gather.6.cloned.1.call-done), kind=kOutput, calls=%fused_computation.33 | convolution fusion | flops 3758096384 | bytes 13107200 | tf_op jit(solution)/shard_map/dot_general | solution.py:117
  171.4 1.6 copy.24
  173.0 4.3 %all-to-all-start.1 = ((f32[512,4,256]{2,0,1:T(8,128)}), f32[512,4,256]{2,0,1:T(8,128)S(1)}, u32[]{:S(2)}, u32[]{:S(2)}) async-start(f32[512,4,256]{2,0,1:T(8,128)} %bitcast.30), calls=%async_computation.1 | async-start | bytes 4194304 | tf_op jit(solution)/shard_map/all_to_all | solution.py:123
  177.4 47.8 %all-to-all-done.1 = f32[512,4,256]{2,0,1:T(8,128)S(1)} async-done(((f32[512,4,256]{2,0,1:T(8,128)}), f32[512,4,256]{2,0,1:T(8,128)S(1)}, u32[]{:S(2)}, u32[]{:S(2)}) %all-to-all-start.1) | async-done | bytes 2097184 | tf_op jit(solution)/shard_map/all_to_all | solution.py:123
  225.1 7.4 %fusion.15 = f32[512,1024]{1,0:T(8,128)S(1)} fusion(bf16[512,3584]{1,0:T(8,128)(2,1)} %copy-done, bf16[1024,3584]{1,0:T(8,128)(2,1)} %all-gather.8.cloned.1.call-done), kind=kOutput, calls=%fused_computation.34 | convolution fusion | flops 3758096384 | bytes 13107200 | tf_op jit(solution)/shard_map/dot_general | solution.py:117
  236.5 1.8 collective-permute-start.4
  238.4 2.2 collective-permute-start
  240.6 4.0 %collective-permute-start.1 = (bf16[128,512]{0,1:T(8,128)(2,1)S(1)}, bf16[128,512]{0,1:T(8,128)(2,1)S(1)}, u32[]{:S(2)}, u32[]{:S(2)}) collective-permute-start(bf16[128,512]{0,1:T(8,128)(2,1)S(1)} %get-tuple-element.59), channel_id=1, source_target_pairs={{0,0},{1,8},{2,16},{3,24},{4,4},{5,12},{6,20},{7,28},{8,1},{9,9},{... | collective-permute-start | bytes 393224 | tf_op jit(solution)/shard_map/ppermute | solution.py:148
  244.6 4.6 %collective-permute-done.2 = f32[512,256]{1,0:T(8,128)S(1)} collective-permute-done((f32[512,256]{1,0:T(8,128)}, f32[512,256]{1,0:T(8,128)S(1)}, u32[]{:S(2)}, u32[]{:S(2)}) %collective-permute-start.2) | collective-permute-done | bytes 524320 | tf_op jit(solution)/shard_map/ppermute | solution.py:130
  249.2 22.4 %collective-permute-done.3 = f32[512,256]{1,0:T(8,128)} collective-permute-done((f32[512,256]{1,0:T(8,128)}, f32[512,256]{1,0:T(8,128)}, u32[]{:S(2)}, u32[]{:S(2)}) %collective-permute-start.3) | collective-permute-done | bytes 524320 | tf_op jit(solution)/shard_map/ppermute | solution.py:130
  273.1 25.2 %collective-permute-start.5 = (bf16[128,512]{0,1:T(8,128)(2,1)S(1)}, bf16[128,512]{0,1:T(8,128)(2,1)S(1)}, u32[]{:S(2)}, u32[]{:S(2)}) collective-permute-start(bf16[128,512]{0,1:T(8,128)(2,1)S(1)} %get-tuple-element.64), channel_id=1, source_target_pairs={{0,4},{1,12},{2,20},{3,28},{4,0},{5,8},{6,16},{7,24},{8,5},{9,13},... | collective-permute-start | bytes 393224 | tf_op jit(solution)/shard_map/ppermute | solution.py:148
  298.3 1.9 collective-permute-start.6
  300.3 8.5 %collective-permute-done.5 = bf16[128,512]{0,1:T(8,128)(2,1)S(1)} collective-permute-done((bf16[128,512]{0,1:T(8,128)(2,1)S(1)}, bf16[128,512]{0,1:T(8,128)(2,1)S(1)}, u32[]{:S(2)}, u32[]{:S(2)}) %collective-permute-start.5) | collective-permute-done | bytes 131104 | tf_op jit(solution)/shard_map/ppermute | solution.py:148
  308.8 1.6 collective-permute-done.6
  (29 shorter events, 9.1 us)
Async XLA Ops:
  7.2 87.2 %all-gather.4.cloned.1.call-start = ((), (), s32[]{:S(2)}) async-start(), calls=%async_computation.2 | async-start | bytes 16515072 | tf_op jit(solution)/shard_map/all_gather | solution.py:97
  11.6 82.9 %copy-start.3 = (bf16[256,4096]{1,0:T(8,128)(2,1)S(1)}, bf16[256,4096]{1,0:T(8,128)(2,1)}, u32[]{:S(2)}) copy-start(bf16[256,4096]{1,0:T(8,128)(2,1)} %param.7) | copy-start | bytes 6291460
  11.6 152.4 %all-gather.6.cloned.1.call-start = ((), (), s32[]{:S(2)}) async-start(), calls=%async_computation.3 | async-start | bytes 8257536 | tf_op jit(solution)/shard_map/all_gather | solution.py:99
  96.9 38.9 %all-to-all-start = ((bf16[8,512,256]{2,1,0:T(8,128)(2,1)}), bf16[8,512,256]{2,1,0:T(8,128)(2,1)S(1)}, u32[]{:S(2)}, u32[]{:S(2)}) async-start(bf16[8,512,256]{2,1,0:T(8,128)(2,1)} %bitcast.32), calls=%async_computation | async-start | bytes 4194304 | tf_op jit(solution)/shard_map/all_to_all | solution.py:100
  100.9 124.3 %all-gather.8.cloned.1.call-start = ((), (), s32[]{:S(2)}) async-start(), calls=%async_computation.4 | async-start | bytes 8257536 | tf_op jit(solution)/shard_map/all_gather | solution.py:122
  135.8 1.3 copy-start.1
  161.1 1.9 copy-start
  173.0 52.1 %all-to-all-start.1 = ((f32[512,4,256]{2,0,1:T(8,128)}), f32[512,4,256]{2,0,1:T(8,128)S(1)}, u32[]{:S(2)}, u32[]{:S(2)}) async-start(f32[512,4,256]{2,0,1:T(8,128)} %bitcast.30), calls=%async_computation.1 | async-start | bytes 4194304 | tf_op jit(solution)/shard_map/all_to_all | solution.py:123
  232.5 1.3 copy-start.2
  235.0 14.2 %collective-permute-start.2 = (f32[512,256]{1,0:T(8,128)}, f32[512,256]{1,0:T(8,128)S(1)}, u32[]{:S(2)}, u32[]{:S(2)}) collective-permute-start(f32[512,256]{1,0:T(8,128)} %get-tuple-element.52), channel_id=1, source_target_pairs={{0,1},{1,2},{2,3},{3,0},{4,5},{5,6},{6,7},{7,4},{8,9},{9,10},{10,1... | collective-permute-start | bytes 1572872 | tf_op jit(solution)/shard_map/ppermute | solution.py:130
  235.0 36.6 %collective-permute-start.3 = (f32[512,256]{1,0:T(8,128)}, f32[512,256]{1,0:T(8,128)}, u32[]{:S(2)}, u32[]{:S(2)}) collective-permute-start(f32[512,256]{1,0:T(8,128)} %get-tuple-element.54), channel_id=1, source_target_pairs={{0,2},{1,3},{2,0},{3,1},{4,6},{5,7},{6,4},{7,5},{8,10},{9,11},{10,... | collective-permute-start | bytes 1572872 | tf_op jit(solution)/shard_map/ppermute | solution.py:130
  236.5 35.2 %collective-permute-start.4 = (f32[512,256]{1,0:T(8,128)S(1)}, f32[512,256]{1,0:T(8,128)}, u32[]{:S(2)}, u32[]{:S(2)}) collective-permute-start(f32[512,256]{1,0:T(8,128)S(1)} %get-tuple-element.53), channel_id=1, source_target_pairs={{0,3},{1,0},{2,1},{3,2},{4,7},{5,4},{6,5},{7,6},{8,11},{9,8},{10,9... | collective-permute-start | bytes 1572872 | tf_op jit(solution)/shard_map/ppermute | solution.py:130
  238.4 61.8 %collective-permute-start = (bf16[128,512]{0,1:T(8,128)(2,1)S(1)}, bf16[128,512]{0,1:T(8,128)(2,1)S(1)}, u32[]{:S(2)}, u32[]{:S(2)}) collective-permute-start(bf16[128,512]{0,1:T(8,128)(2,1)S(1)} %get-tuple-element.60), channel_id=1, source_target_pairs={{0,4},{1,12},{2,20},{3,28},{4,0},{5,8},{6,16},{7,24},{8,5},{9,13},... | collective-permute-start | bytes 393224 | tf_op jit(solution)/shard_map/ppermute | solution.py:148
  240.6 59.6 %collective-permute-start.1 = (bf16[128,512]{0,1:T(8,128)(2,1)S(1)}, bf16[128,512]{0,1:T(8,128)(2,1)S(1)}, u32[]{:S(2)}, u32[]{:S(2)}) collective-permute-start(bf16[128,512]{0,1:T(8,128)(2,1)S(1)} %get-tuple-element.59), channel_id=1, source_target_pairs={{0,0},{1,8},{2,16},{3,24},{4,4},{5,12},{6,20},{7,28},{8,1},{9,9},{... | collective-permute-start | bytes 393224 | tf_op jit(solution)/shard_map/ppermute | solution.py:148
  273.1 35.7 %collective-permute-start.5 = (bf16[128,512]{0,1:T(8,128)(2,1)S(1)}, bf16[128,512]{0,1:T(8,128)(2,1)S(1)}, u32[]{:S(2)}, u32[]{:S(2)}) collective-permute-start(bf16[128,512]{0,1:T(8,128)(2,1)S(1)} %get-tuple-element.64), channel_id=1, source_target_pairs={{0,4},{1,12},{2,20},{3,28},{4,0},{5,8},{6,16},{7,24},{8,5},{9,13},... | collective-permute-start | bytes 393224 | tf_op jit(solution)/shard_map/ppermute | solution.py:148
  298.3 12.1 %collective-permute-start.6 = (bf16[128,512]{0,1:T(8,128)(2,1)S(1)}, bf16[128,512]{0,1:T(8,128)(2,1)S(1)}, u32[]{:S(2)}, u32[]{:S(2)}) collective-permute-start(bf16[128,512]{0,1:T(8,128)(2,1)S(1)} %get-tuple-element.63), channel_id=1, source_target_pairs={{0,0},{1,8},{2,16},{3,24},{4,4},{5,12},{6,20},{7,28},{8,1},{9,9},{... | collective-permute-start | bytes 393224 | tf_op jit(solution)/shard_map/ppermute | solution.py:148
Sparse Core Ops, SparseCore 0:
  11.7 82.6 all-gather.3
  96.3 67.6 all-gather.5
  171.6 49.9 all-gather.7

commit v7 on v4

--- a/solution.py
+++ b/solution.py
@@ -73,6 +73,29 @@
     )(jnp.reshape(me, (1,)).astype(jnp.int32), grad_rows, hidden_all, first_moment, second_moment, down_weight)
 
 
+def gather_plane(x):
+    half = x.shape[0] // 2
+
+    def swap(v, k):
+        return lax.ppermute(v, "dp", [(i, i ^ k) for i in range(8)])
+
+    along_x = swap(x, 2)
+    along_y = swap(x, 4)
+    partner = swap(x, 1)
+    diagonal = jnp.concatenate([swap(along_x[:half], 4), swap(along_y[half:], 2)], axis=0)
+    blocks = [
+        x,
+        partner,
+        along_x,
+        swap(along_x, 1),
+        along_y,
+        swap(along_y, 1),
+        diagonal,
+        swap(diagonal, 1),
+    ]
+    return jnp.concatenate(blocks, axis=0)
+
+
 def shards(grad_out, gate_input, up_input, next_hidden, down_weight, first_moment, second_moment):
     n_dp = lax.axis_size("dp")
     n_t = lax.axis_size("tensor")
@@ -94,10 +117,19 @@
     activated = gate_value * sigmoid_gate
 
     half = tok // 2
-    hidden_all = lax.all_gather(hidden, "dp", axis=0, tiled=True)
+    plane = n_dp == 8
+    if plane:
+        hidden_all = gather_plane(hidden)
+    else:
+        hidden_all = lax.all_gather(hidden, "dp", axis=0, tiled=True)
     first_own, hidden_all = lax.optimization_barrier((next_hidden[:half], hidden_all))
     first_next = lax.all_gather(first_own, "dp", axis=0, tiled=True)
     grad_rows = lax.all_to_all(grad_out.T, "dp", 0, 1, tiled=True)
+    if plane:
+        grad_rows = jnp.concatenate(
+            [lax.dynamic_slice_in_dim(grad_rows, (me ^ p) * tok, tok, 1) for p in range(n_dp)],
+            axis=1,
+        )
 
     grad_hidden = jnp.dot(grad_out, down_weight, preferred_element_type=jnp.float32)
     gate_grad = (

time: 316 us -> 308 us (0.975)
  waiting for transfers between devices: 155 us -> 130 us
  local copies, waits for them, and re-layouts: 8.84 us -> 19.2 us
  starting transfers between devices: 23.7 us -> 31.1 us
    all_gather x1 -> x0, waiting for transfers between devices: 79.8 us -> none  [shards(): hidden_all = lax.all_gather(hidden, 'dp', axis=0, tiled=True)]
    ppermute x0 -> x8, waiting for transfers between devices: none -> 55 us  [swap(): return lax.ppermute(v, 'dp', [(i, i ^ k) for i in range(8)])]
    unnamed x5 -> x22, local copies, waits for them, and re-layouts: 2.93 us -> 13.5 us
    ppermute x0 -> x8, starting transfers between devices: none -> 7.69 us  [swap(): return lax.ppermute(v, 'dp', [(i, i ^ k) for i in range(8)])]
  transfers between devices with their start and end apart: 9 -> 16, of which waited for: 6 -> 8; matrix products, arithmetic and copies ran while one was open for 8% -> 11% of each run, Pallas kernels for 7% -> 7%
where the time goes in v7:
time: 308 us
  waiting for transfers between devices  130 us (42%)
  blocking collectives  51.9 us (17%)
  matrix products  34.3 us (11%)
  starting transfers between devices  31.1 us (10%)
  Pallas kernels  22.2 us (7%)
  local copies, waits for them, and re-layouts  19.2 us (6%)
  between operations  14 us (5%)
  other arithmetic  4.7 us (2%)
    ppermute x8, waiting for transfers between devices, swap(): return lax.ppermute(v, 'dp', [(i, i ^ k) for i in range(8)])  55 us
    all_to_all x1, blocking collectives, shards(): blocks = lax.all_to_all(partial_out, 'tensor', 1, 0, tiled=True)  51.9 us
    reduce_scatter x1, waiting for transfers between devices, shards(): lax.psum_scatter(partial_out, 'tensor', scatter_dimension=1, tiled=True)  39.9 us
    pallas_call x1, Pallas kernels, owner_update(): pl.pallas_call(functools.partial(adam_kernel, blocks=tokens // tok, tok=t...  22.2 us
    ppermute x4, starting transfers between devices, shards(): pieces.append(lax.ppermute(piece, ('dp', 'tensor'), perm))  19.6 us
    all_to_all x1, waiting for transfers between devices, shards(): grad_rows = lax.all_to_all(grad_out.T, 'dp', 0, 1, tiled=True)  17.5 us
    dot_general x1, matrix products, shards(): jnp.dot(grad_out, down_weight, preferred_element_type=jnp.float32)  17.4 us
    dot_general x2, matrix products, shards(): lax.dot_general(new_shard, next_part, (((1,), (1,)), ((), ())), preferred...  16.9 us
  transfers between devices with their start and end apart: 16, of which 8 were waited for; matrix products, arithmetic and copies ran while one was open for 11% of the time, Pallas kernels for 7%

profile of v7, /device:TPU:3, one launch (start us, length us, event | category | flops | bytes accessed | tf_op | source)
XLA Modules:
  0.0 307.7 jit_solution(9411463422738483193)
XLA Ops:
  7.2 3.3 %fusion.12 = bf16[256,3584]{1,0:T(8,128)(2,1)S(1)} fusion(bf16[256,3584]{1,0:T(8,128)(2,1)} %param.9, bf16[256,3584]{1,0:T(8,128)(2,1)} %param.8), kind=kLoop, calls=%fused_computation.17 | loop fusion | flops 7340032 | bytes 5505024 | tf_op jit(solution)/shard_map/convert_element_type | solution.py:112
  10.6 1.5 collective-permute-start.3
  14.6 36.8 %collective-permute-done.1 = bf16[256,3584]{1,0:T(8,128)(2,1)S(1)} collective-permute-done((bf16[256,3584]{1,0:T(8,128)(2,1)S(1)}, bf16[256,3584]{1,0:T(8,128)(2,1)S(1)}, u32[]{:S(2)}, u32[]{:S(2)}) %collective-permute-start.1) | collective-permute-done | bytes 1835040 | tf_op jit(solution)/shard_map/ppermute | solution.py:80
  51.4 1.5 collective-permute-start.2
  53.0 1.4 constant_dynamic-update-slice_fusion.8
  58.0 1.4 constant_dynamic-update-slice_fusion.6
  59.4 17.1 %collective-permute-done.5 = bf16[128,3584]{1,0:T(8,128)(2,1)S(1)} collective-permute-done((bf16[128,3584]{1,0:T(8,128)(2,1)S(1)}, bf16[128,3584]{1,0:T(8,128)(2,1)S(1)}, u32[]{:S(2)}, u32[]{:S(2)}) %collective-permute-start.5) | collective-permute-done | bytes 917536 | tf_op jit(solution)/shard_map/ppermute | solution.py:80
  80.2 1.4 constant_dynamic-update-slice_fusion.4
  86.3 2.5 copy.17
  88.8 3.7 %all-to-all-start = ((bf16[8,512,256]{2,1,0:T(8,128)(2,1)}), bf16[8,512,256]{2,1,0:T(8,128)(2,1)S(1)}, u32[]{:S(2)}, u32[]{:S(2)}) async-start(bf16[8,512,256]{2,1,0:T(8,128)(2,1)} %bitcast.38), calls=%async_computation | async-start | bytes 4194304 | tf_op jit(solution)/shard_map/all_to_all | solution.py:127
  92.5 17.4 %fusion.11 = (bf16[256,3584]{1,0:T(8,128)(2,1)}, bf16[256,3584]{1,0:T(8,128)(2,1)}) fusion(bf16[256,3584]{1,0:T(8,128)(2,1)} %param.8, bf16[256,3584]{1,0:T(8,128)(2,1)} %param.9, bf16[256,4096]{1,0:T(8,128)(2,1)} %param.7, bf16[4096,3584]{1,0:T(8,128)(2,1)} %w_ref.1), kind=kOutput, calls=%fused_computation.16 | convolution fusion | flops 7529955328 | bytes 38797312 | tf_op jit(solution)/shard_map/dot_general | solution.py:134
  109.9 17.5 %all-to-all-done = bf16[8,512,256]{2,1,0:T(8,128)(2,1)S(1)} async-done(((bf16[8,512,256]{2,1,0:T(8,128)(2,1)}), bf16[8,512,256]{2,1,0:T(8,128)(2,1)S(1)}, u32[]{:S(2)}, u32[]{:S(2)}) %all-to-all-start) | async-done | bytes 2097184 | tf_op jit(solution)/shard_map/all_to_all | solution.py:127
  128.1 22.2 %shard_map.110 = (f32[512,3584]{1,0:T(8,128)}, f32[512,3584]{1,0:T(8,128)}, bf16[512,3584]{1,0:T(8,128)(2,1)S(1)}) custom-call(s32[1]{0:T(128)} %bitcast.me_ref, bf16[512,2048]{1,0:T(8,128)(2,1)S(1)} %dynamic-slice_dynamic-update-slice_fusion.g_ref, bf16[2048,3584]{1,0:T(8,128)(2,1)} %constant_dynamic-update-slice_fusion.h_ref, f32[512,3584]{1,0:T(8,128)} %m1_ref.1, ...), custom_call_target="tpu_custom_call" | custom-call | flops 7516192768 | bytes 53477376 | tf_op jit(solution)/shard_map/pallas_call | solution.py:63
  150.3 1.9 copy-done
  152.3 3.7 %all-gather.3.cloned.1.call-done = bf16[1024,3584]{1,0:T(8,128)(2,1)} async-done(((bf16[128,3584]{1,0:T(8,128)(2,1)}), bf16[1024,3584]{1,0:T(8,128)(2,1)}) %all-gather.3.cloned.1.call-update) | async-done | bytes 7340048 | tf_op jit(solution)/shard_map/all_gather | solution.py:126
  156.0 7.4 %fusion.14 = f32[512,1024]{1,0:T(8,128)S(1)} fusion(bf16[512,3584]{1,0:T(8,128)(2,1)} %copy-done, bf16[1024,3584]{1,0:T(8,128)(2,1)} %all-gather.3.cloned.1.call-done), kind=kOutput, calls=%fused_computation.47 | convolution fusion | flops 3758096384 | bytes 13107200 | tf_op jit(solution)/shard_map/dot_general | solution.py:149
  163.6 51.9 %all_to_all.38 = f32[512,4,256]{2,0,1:T(8,128)S(1)} all-to-all(f32[512,4,256]{2,0,1:T(8,128)S(1)} %bitcast.39), channel_id=1, replica_groups=mesh['dp'=8,'tensor'=4] {'tensor'}, dimensions={1} | all-to-all | bytes 4194304 | tf_op jit(solution)/shard_map/all_to_all | solution.py:155
  215.5 9.6 %fusion.15 = f32[512,1024]{1,0:T(8,128)} fusion(bf16[512,3584]{1,0:T(8,128)(2,1)} %copy-done, bf16[1024,3584]{1,0:T(8,128)(2,1)} %all-gather.5.cloned.1.call-done), kind=kOutput, calls=%fused_computation.48 | convolution fusion | flops 3758096384 | bytes 13107200 | tf_op jit(solution)/shard_map/dot_general | solution.py:149
  226.6 4.3 %collective-permute-start.9 = (bf16[128,512]{0,1:T(8,128)(2,1)S(1)}, bf16[128,512]{0,1:T(8,128)(2,1)S(1)}, u32[]{:S(2)}, u32[]{:S(2)}) collective-permute-start(bf16[128,512]{0,1:T(8,128)(2,1)S(1)} %get-tuple-element.56), channel_id=1, source_target_pairs={{0,0},{1,8},{2,16},{3,24},{4,4},{5,12},{6,20},{7,28},{8,1},{9,9},{... | collective-permute-start | bytes 393224 | tf_op jit(solution)/shard_map/ppermute | solution.py:175
  230.9 39.9 %reduce-scatter.2.cloned.1.call-done = f32[512,256]{1,0:T(8,128)} async-done(((f32[512,1024]{1,0:T(8,128)}), f32[512,256]{1,0:T(8,128)}) %reduce-scatter.2.cloned.1.call-update) | async-done | bytes 524304 | tf_op jit(solution)/shard_map/reduce_scatter | solution.py:159
  271.9 12.1 %collective-permute-start.10 = (bf16[128,512]{0,1:T(8,128)(2,1)S(1)}, bf16[128,512]{0,1:T(8,128)(2,1)S(1)}, u32[]{:S(2)}, u32[]{:S(2)}) collective-permute-start(bf16[128,512]{0,1:T(8,128)(2,1)S(1)} %get-tuple-element.61), channel_id=1, source_target_pairs={{0,4},{1,12},{2,20},{3,28},{4,0},{5,8},{6,16},{7,24},{8,5},{9,13},... | collective-permute-start | bytes 393224 | tf_op jit(solution)/shard_map/ppermute | solution.py:175
  284.0 1.9 collective-permute-start.11
  286.0 2.5 collective-permute-done.10
  288.5 11.5 %collective-permute-done.11 = bf16[128,512]{0,1:T(8,128)(2,1)S(1)} collective-permute-done((bf16[128,512]{0,1:T(8,128)(2,1)S(1)}, bf16[128,512]{0,1:T(8,128)(2,1)S(1)}, u32[]{:S(2)}, u32[]{:S(2)}) %collective-permute-start.11) | collective-permute-done | bytes 131104 | tf_op jit(solution)/shard_map/ppermute | solution.py:175
  (55 shorter events, 19.2 us)
Async XLA Ops:
  7.2 6.1 %copy-start.2 = (bf16[256,3584]{1,0:T(8,128)(2,1)S(1)}, bf16[256,3584]{1,0:T(8,128)(2,1)}, u32[]{:S(2)}) copy-start(bf16[256,3584]{1,0:T(8,128)(2,1)} %param.10) | copy-start | bytes 5505028
  7.2 148.8 %all-gather.3.cloned.1.call-start = ((), (), s32[]{:S(2)}) async-start(), calls=%async_computation.3 | async-start | bytes 8257536 | tf_op jit(solution)/shard_map/all_gather | solution.py:126
  10.5 40.9 %collective-permute-start.1 = (bf16[256,3584]{1,0:T(8,128)(2,1)S(1)}, bf16[256,3584]{1,0:T(8,128)(2,1)S(1)}, u32[]{:S(2)}, u32[]{:S(2)}) collective-permute-start(bf16[256,3584]{1,0:T(8,128)(2,1)S(1)} %fusion.12), channel_id=1, source_target_pairs={{0,8},{4,12},{8,0},{12,4},{16,24},{20,28},{24,16},{28,20},{1,9},{5... | collective-permute-start | bytes 5505032 | tf_op jit(solution)/shard_map/ppermute | solution.py:80
  10.6 45.2 %collective-permute-start.3 = (bf16[256,3584]{1,0:T(8,128)(2,1)S(1)}, bf16[256,3584]{1,0:T(8,128)(2,1)S(1)}, u32[]{:S(2)}, u32[]{:S(2)}) collective-permute-start(bf16[256,3584]{1,0:T(8,128)(2,1)S(1)} %fusion.12), channel_id=1, source_target_pairs={{0,16},{4,20},{8,24},{12,28},{16,0},{20,4},{24,8},{28,12},{1,17},{... | collective-permute-start | bytes 5505032 | tf_op jit(solution)/shard_map/ppermute | solution.py:80
  12.1 44.6 %collective-permute-start = (bf16[256,3584]{1,0:T(8,128)(2,1)S(1)}, bf16[256,3584]{1,0:T(8,128)(2,1)S(1)}, u32[]{:S(2)}, u32[]{:S(2)}) collective-permute-start(bf16[256,3584]{1,0:T(8,128)(2,1)S(1)} %fusion.12), channel_id=1, source_target_pairs={{0,4},{4,0},{8,12},{12,8},{16,20},{20,16},{24,28},{28,24},{1,5},{5... | collective-permute-start | bytes 5505032 | tf_op jit(solution)/shard_map/ppermute | solution.py:80
  51.4 27.4 %collective-permute-start.2 = (bf16[256,3584]{1,0:T(8,128)(2,1)S(1)}, bf16[256,3584]{1,0:T(8,128)(2,1)S(1)}, u32[]{:S(2)}, u32[]{:S(2)}) collective-permute-start(bf16[256,3584]{1,0:T(8,128)(2,1)S(1)} %collective-permute-done.1), channel_id=1, source_target_pairs={{0,4},{4,0},{8,12},{12,8},{16,20},{20,16},{24,28},{28,24},{1,5},{5... | collective-permute-start | bytes 5505032 | tf_op jit(solution)/shard_map/ppermute | solution.py:80
  54.4 22.0 %collective-permute-start.5 = (bf16[128,3584]{1,0:T(8,128)(2,1)S(1)}, bf16[128,3584]{1,0:T(8,128)(2,1)S(1)}, u32[]{:S(2)}, u32[]{:S(2)}) collective-permute-start(bf16[128,3584]{1,0:T(8,128)(2,1)S(1)} %slice.16), channel_id=1, source_target_pairs={{0,16},{4,20},{8,24},{12,28},{16,0},{20,4},{24,8},{28,12},{1,17},{... | collective-permute-start | bytes 2752520 | tf_op jit(solution)/shard_map/ppermute | solution.py:80
  55.8 21.7 %collective-permute-start.6 = (bf16[128,3584]{1,0:T(8,128)(2,1)S(1)}, bf16[128,3584]{1,0:T(8,128)(2,1)S(1)}, u32[]{:S(2)}, u32[]{:S(2)}) collective-permute-start(bf16[128,3584]{1,0:T(8,128)(2,1)S(1)} %slice.17), channel_id=1, source_target_pairs={{0,8},{4,12},{8,0},{12,4},{16,24},{20,28},{24,16},{28,20},{1,9},{5... | collective-permute-start | bytes 2752520 | tf_op jit(solution)/shard_map/ppermute | solution.py:80
  56.1 25.5 %collective-permute-start.4 = (bf16[256,3584]{1,0:T(8,128)(2,1)S(1)}, bf16[256,3584]{1,0:T(8,128)(2,1)S(1)}, u32[]{:S(2)}, u32[]{:S(2)}) collective-permute-start(bf16[256,3584]{1,0:T(8,128)(2,1)S(1)} %collective-permute-done.3), channel_id=1, source_target_pairs={{0,4},{4,0},{8,12},{12,8},{16,20},{20,16},{24,28},{28,24},{1,5},{5... | collective-permute-start | bytes 5505032 | tf_op jit(solution)/shard_map/ppermute | solution.py:80
  77.6 7.3 %collective-permute-start.7 = (bf16[256,3584]{1,0:T(8,128)(2,1)S(1)}, bf16[256,3584]{1,0:T(8,128)(2,1)S(1)}, u32[]{:S(2)}, u32[]{:S(2)}) collective-permute-start(bf16[256,3584]{1,0:T(8,128)(2,1)S(1)} %pad_maximum_fusion), channel_id=1, source_target_pairs={{0,4},{4,0},{8,12},{12,8},{16,20},{20,16},{24,28},{28,24},{1,5},{5... | collective-permute-start | bytes 5505032 | tf_op jit(solution)/shard_map/ppermute | solution.py:80
  83.9 2.4 copy-start.1
  88.8 38.6 %all-to-all-start = ((bf16[8,512,256]{2,1,0:T(8,128)(2,1)}), bf16[8,512,256]{2,1,0:T(8,128)(2,1)S(1)}, u32[]{:S(2)}, u32[]{:S(2)}) async-start(bf16[8,512,256]{2,1,0:T(8,128)(2,1)} %bitcast.38), calls=%async_computation | async-start | bytes 4194304 | tf_op jit(solution)/shard_map/all_to_all | solution.py:127
  92.5 123.0 %all-gather.5.cloned.1.call-start = ((), (), s32[]{:S(2)}) async-start(), calls=%async_computation.4 | async-start | bytes 8257536 | tf_op jit(solution)/shard_map/all_gather | solution.py:154
  150.3 1.9 copy-start
  163.4 107.4 %reduce-scatter.2.cloned.1.call-start = ((), (), s32[]{:S(2)}) async-start(), calls=%async_computation.5 | async-start | bytes 2621440 | tf_op jit(solution)/shard_map/reduce_scatter | solution.py:159
  225.3 60.6 %collective-permute-start.8 = (bf16[128,512]{0,1:T(8,128)(2,1)S(1)}, bf16[128,512]{0,1:T(8,128)(2,1)S(1)}, u32[]{:S(2)}, u32[]{:S(2)}) collective-permute-start(bf16[128,512]{0,1:T(8,128)(2,1)S(1)} %get-tuple-element.57), channel_id=1, source_target_pairs={{0,4},{1,12},{2,20},{3,28},{4,0},{5,8},{6,16},{7,24},{8,5},{9,13},... | collective-permute-start | bytes 393224 | tf_op jit(solution)/shard_map/ppermute | solution.py:175
  226.6 59.4 %collective-permute-start.9 = (bf16[128,512]{0,1:T(8,128)(2,1)S(1)}, bf16[128,512]{0,1:T(8,128)(2,1)S(1)}, u32[]{:S(2)}, u32[]{:S(2)}) collective-permute-start(bf16[128,512]{0,1:T(8,128)(2,1)S(1)} %get-tuple-element.56), channel_id=1, source_target_pairs={{0,0},{1,8},{2,16},{3,24},{4,4},{5,12},{6,20},{7,28},{8,1},{9,9},{... | collective-permute-start | bytes 393224 | tf_op jit(solution)/shard_map/ppermute | solution.py:175
  271.9 16.6 %collective-permute-start.10 = (bf16[128,512]{0,1:T(8,128)(2,1)S(1)}, bf16[128,512]{0,1:T(8,128)(2,1)S(1)}, u32[]{:S(2)}, u32[]{:S(2)}) collective-permute-start(bf16[128,512]{0,1:T(8,128)(2,1)S(1)} %get-tuple-element.61), channel_id=1, source_target_pairs={{0,4},{1,12},{2,20},{3,28},{4,0},{5,8},{6,16},{7,24},{8,5},{9,13},... | collective-permute-start | bytes 393224 | tf_op jit(solution)/shard_map/ppermute | solution.py:175
  284.0 16.0 %collective-permute-start.11 = (bf16[128,512]{0,1:T(8,128)(2,1)S(1)}, bf16[128,512]{0,1:T(8,128)(2,1)S(1)}, u32[]{:S(2)}, u32[]{:S(2)}) collective-permute-start(bf16[128,512]{0,1:T(8,128)(2,1)S(1)} %get-tuple-element.60), channel_id=1, source_target_pairs={{0,0},{1,8},{2,16},{3,24},{4,4},{5,12},{6,20},{7,28},{8,1},{9,9},{... | collective-permute-start | bytes 393224 | tf_op jit(solution)/shard_map/ppermute | solution.py:175
Sparse Core Ops, SparseCore 0:
  86.5 69.4 all-gather.2
  163.5 49.9 all-gather.4
  225.2 45.5 reduce-scatter.1

commit v8 on v3

--- a/solution.py
+++ b/solution.py
@@ -73,6 +73,33 @@
     )(jnp.reshape(me, (1,)).astype(jnp.int32), grad_rows, hidden_all, first_moment, second_moment, down_weight)
 
 
+def gather_plane(x, me):
+    rows = x.shape[0]
+    half = rows // 2
+
+    def swap(v, k):
+        return lax.ppermute(v, "dp", [(i, i ^ k) for i in range(8)])
+
+    along_x = swap(x, 2)
+    along_y = swap(x, 4)
+    partner = swap(x, 1)
+    diagonal = jnp.concatenate([swap(along_x[:half], 4), swap(along_y[half:], 2)], axis=0)
+    blocks = [
+        x,
+        partner,
+        along_x,
+        swap(along_x, 1),
+        along_y,
+        swap(along_y, 1),
+        diagonal,
+        swap(diagonal, 1),
+    ]
+    out = jnp.zeros((8 * rows,) + x.shape[1:], x.dtype)
+    for p, block in enumerate(blocks):
+        out = lax.dynamic_update_slice_in_dim(out, block, (me ^ p) * rows, 0)
+    return out
+
+
 def shards(grad_out, gate_input, up_input, next_hidden, down_weight, first_moment, second_moment):
     n_dp = lax.axis_size("dp")
     n_t = lax.axis_size("tensor")
@@ -93,8 +120,16 @@
     sigmoid_gate = jax.nn.sigmoid(gate_value)
     activated = gate_value * sigmoid_gate
 
-    hidden_all = lax.all_gather(hidden, "dp", axis=0, tiled=True)
-    next_all = lax.all_gather(next_hidden, "dp", axis=0, tiled=True)
+    plane = n_dp == 8
+    if plane:
+        hidden_all = gather_plane(hidden, me)
+    else:
+        hidden_all = lax.all_gather(hidden, "dp", axis=0, tiled=True)
+    next_own, hidden_all = lax.optimization_barrier((next_hidden, hidden_all))
+    if plane:
+        next_all = gather_plane(next_own, me)
+    else:
+        next_all = lax.all_gather(next_own, "dp", axis=0, tiled=True)
     grad_rows = lax.all_to_all(grad_out.T, "dp", 0, 1, tiled=True)
 
     grad_hidden = jnp.dot(grad_out, down_weight, preferred_element_type=jnp.float32)
@@ -106,6 +141,7 @@
     moment_one, moment_two, new_shard = owner_update(
         me, grad_rows, hidden_all, first_moment, second_moment, down_weight, tok
     )
+    gate_grad, up_grad, new_shard = lax.optimization_barrier((gate_grad, up_grad, new_shard))
 
     partial_out = lax.dot_general(
         new_shard, next_all, (((1,), (1,)), ((), ())), preferred_element_type=jnp.float32
@@ -115,6 +151,7 @@
         .astype(jnp.bfloat16)
         .T
     )
+
     sub = me % group
     pieces = []
     for k in range(group):

time: 334 us -> 329 us (0.985)
  waiting for transfers between devices: 245 us -> 175 us
  local copies, waits for them, and re-layouts: 8.55 us -> 57.7 us
  starting transfers between devices: 9.51 us -> 26.2 us
    all_gather x2 -> x0, waiting for transfers between devices: 108 us -> none  [the longest x1 58.9 us: shards(): next_all = lax.all_gather(next_hidden, 'dp', axis=0, tiled=True)]
    ppermute x0 -> x16, waiting for transfers between devices: none -> 64.6 us  [swap(): return lax.ppermute(v, 'dp', [(i, i ^ k) for i in range(8)])]
    all_to_all x1, waiting for transfers between devices: 42 us -> 0.01 us  [shards(): grad_rows = lax.all_to_all(grad_out.T, 'dp', 0, 1, tiled=True)]
    dynamic_update_slice x0 -> x16, local copies, waits for them, and re-layouts: none -> 34.1 us  [gather_plane(): out = lax.dynamic_update_slice_in_dim(out, block, (me ^ p) * rows, 0)]
    ppermute x0 -> x16, starting transfers between devices: none -> 16.7 us  [swap(): return lax.ppermute(v, 'dp', [(i, i ^ k) for i in range(8)])]
    ppermute x2, waiting for transfers between devices: 17 us -> 33 us  [shards(): pieces.append(lax.ppermute(piece, ('dp', 'tensor'), perm))]
    another operation x0 -> x2, local copies, waits for them, and re-layouts: none -> 12.3 us
    slice x0 -> x4, local copies, waits for them, and re-layouts: none -> 4.96 us  [the longest x2 2.48 us: gather_plane(): along_y[half:]]
  transfers between devices with their start and end apart: 6 -> 20, of which waited for: 6 -> 7; matrix products, arithmetic and copies ran while one was open for 6% -> 21% of each run, Pallas kernels for 7% -> 7%
where the time goes in v8:
time: 329 us
  waiting for transfers between devices  175 us (53%)
  local copies, waits for them, and re-layouts  57.7 us (18%)
  matrix products  28 us (9%)
  starting transfers between devices  26.2 us (8%)
  Pallas kernels  21.6 us (7%)
  between operations  14.2 us (4%)
  other arithmetic  5.89 us (2%)
    reduce_scatter x1, waiting for transfers between devices, shards(): lax.psum_scatter(partial_out, 'tensor', scatter_dimension=1, tiled=True)  77.5 us
    ppermute x16, waiting for transfers between devices, swap(): return lax.ppermute(v, 'dp', [(i, i ^ k) for i in range(8)])  64.6 us
    dynamic_update_slice x16, local copies, waits for them, and re-layouts, gather_plane(): out = lax.dynamic_update_slice_in_dim(out, block, (me ^ p) * rows, 0)  34.1 us
    ppermute x2, waiting for transfers between devices, shards(): pieces.append(lax.ppermute(piece, ('dp', 'tensor'), perm))  33 us
    pallas_call x1, Pallas kernels, owner_update(): pl.pallas_call(functools.partial(adam_kernel, blocks=tokens // tok, tok=t...  21.6 us
    ppermute x16, starting transfers between devices, swap(): return lax.ppermute(v, 'dp', [(i, i ^ k) for i in range(8)])  16.7 us
    dot_general x1, matrix products, shards(): jnp.dot(grad_out, down_weight, preferred_element_type=jnp.float32)  15.5 us
    dot_general x1, matrix products, shards(): lax.dot_general(new_shard, next_all, (((1,), (1,)), ((), ())), preferred_...  12.5 us
  transfers between devices with their start and end apart: 20, of which 7 were waited for; matrix products, arithmetic and copies ran while one was open for 21% of the time, Pallas kernels for 7%

profile of v8, /device:TPU:3, one launch (start us, length us, event | category | flops | bytes accessed | tf_op | source)
XLA Modules:
  0.0 328.6 jit_solution(1064771983297350307)
XLA Ops:
  7.2 4.5 %fusion.12 = bf16[256,3584]{1,0:T(8,128)(2,1)} fusion(bf16[256,3584]{1,0:T(8,128)(2,1)} %param.9, bf16[256,3584]{1,0:T(8,128)(2,1)} %param.8), kind=kLoop, calls=%fused_computation.17 | loop fusion | flops 7340032 | bytes 5505024 | tf_op jit(solution)/shard_map/convert_element_type | solution.py:116
  14.4 2.4 copy.14
  16.9 4.6 %all-to-all-start = ((bf16[8,512,256]{2,1,0:T(8,128)(2,1)}), bf16[8,512,256]{2,1,0:T(8,128)(2,1)S(1)}, u32[]{:S(2)}, u32[]{:S(2)}) async-start(bf16[8,512,256]{2,1,0:T(8,128)(2,1)} %bitcast.16), calls=%async_computation | async-start | bytes 4194304 | tf_op jit(solution)/shard_map/all_to_all | solution.py:133
  21.5 6.1 %broadcast.11.clone = bf16[2048,3584]{1,0:T(8,128)(2,1)} broadcast(bf16[]{:T(256)} %constant.44.clone.1), dimensions={} | broadcast | bytes 14680066 | tf_op jit(solution)/shard_map/broadcast.2
  27.7 2.9 constant_dynamic-update-slice_fusion.19
  30.5 22.4 %collective-permute-done.1 = bf16[256,3584]{1,0:T(8,128)(2,1)} collective-permute-done((bf16[256,3584]{1,0:T(8,128)(2,1)}, bf16[256,3584]{1,0:T(8,128)(2,1)}, u32[]{:S(2)}, u32[]{:S(2)}) %collective-permute-start.1) | collective-permute-done | bytes 1835040 | tf_op jit(solution)/shard_map/ppermute | solution.py:81
  57.0 5.1 %collective-permute-start.2 = (bf16[256,3584]{1,0:T(8,128)(2,1)}, bf16[256,3584]{1,0:T(8,128)(2,1)S(1)}, u32[]{:S(2)}, u32[]{:S(2)}) collective-permute-start(bf16[256,3584]{1,0:T(8,128)(2,1)} %collective-permute-done.1), channel_id=1, source_target_pairs={{0,4},{4,0},{8,12},{12,8},{16,20},{20,16},{24,28},{28,24},{1,5},{5... | collective-permute-start | bytes 5505032 | tf_op jit(solution)/shard_map/ppermute | solution.py:81
  62.1 2.9 constant_dynamic-update-slice_fusion.18
  65.0 2.8 constant_dynamic-update-slice_fusion.17
  67.9 27.1 %collective-permute-done.5 = bf16[128,3584]{1,0:T(8,128)(2,1)S(1)} collective-permute-done((bf16[128,3584]{1,0:T(8,128)(2,1)S(1)}, bf16[128,3584]{1,0:T(8,128)(2,1)S(1)}, u32[]{:S(2)}, u32[]{:S(2)}) %collective-permute-start.5) | collective-permute-done | bytes 917536 | tf_op jit(solution)/shard_map/ppermute | solution.py:81
  98.1 2.8 constant_dynamic-update-slice_fusion.15
  108.3 15.5 %fusion.11 = (bf16[256,3584]{1,0:T(8,128)(2,1)}, bf16[256,3584]{1,0:T(8,128)(2,1)}) fusion(bf16[256,3584]{1,0:T(8,128)(2,1)S(1)} %copy-done.4, bf16[256,3584]{1,0:T(8,128)(2,1)S(1)} %copy-done.5, bf16[256,4096]{1,0:T(8,128)(2,1)S(1)} %copy-done.3, bf16[4096,3584]{1,0:T(8,128)(2,1)} %w_ref.1), kind=kOutput, calls=%fused_computation.16 | convolution fusion | flops 7529955328 | bytes 38797312 | tf_op jit(solution)/shard_map/dot_general | solution.py:135
  124.1 21.6 %shard_map.110 = (f32[512,3584]{1,0:T(8,128)}, f32[512,3584]{1,0:T(8,128)}, bf16[512,3584]{1,0:T(8,128)(2,1)S(1)}) custom-call(s32[1]{0:T(128)} %bitcast.me_ref, bf16[512,2048]{1,0:T(8,128)(2,1)S(1)} %bitcast.14, bf16[2048,3584]{1,0:T(8,128)(2,1)} %constant_dynamic-update-slice_fusion.12.h_ref, f32[512,3584]{1,0:T(8,128)} %m1_ref.1, f32[512,3584]{1,0:T(8,128)} %m2_ref.1, ...), custom_call_target="tpu_custom_call" | custom-call | flops 7516192768 | bytes 53477376 | tf_op jit(solution)/shard_map/pallas_call | solution.py:63
  147.5 6.1 %broadcast.11 = bf16[2048,3584]{1,0:T(8,128)(2,1)} broadcast(bf16[]{:T(256)} %constant.44.clone.1), dimensions={} | broadcast | bytes 14680066 | tf_op jit(solution)/shard_map/broadcast.2
  153.6 2.9 constant_dynamic-update-slice_fusion.11
  160.2 2.9 constant_dynamic-update-slice_fusion.10
  163.1 2.8 constant_dynamic-update-slice_fusion.9
  166.0 13.8 %collective-permute-done.13 = bf16[128,3584]{1,0:T(8,128)(2,1)S(1)} collective-permute-done((bf16[128,3584]{1,0:T(8,128)(2,1)S(1)}, bf16[128,3584]{1,0:T(8,128)(2,1)S(1)}, u32[]{:S(2)}, u32[]{:S(2)}) %collective-permute-start.13) | collective-permute-done | bytes 917536 | tf_op jit(solution)/shard_map/ppermute | solution.py:81
  183.7 2.8 constant_dynamic-update-slice_fusion.7
  191.4 12.5 %fusion.13 = f32[512,2048]{1,0:T(8,128)} fusion(bf16[512,3584]{1,0:T(8,128)(2,1)S(1)} %copy-done.1, bf16[2048,3584]{1,0:T(8,128)(2,1)} %constant_dynamic-update-slice_fusion.4), kind=kOutput, calls=%fused_computation.43 | convolution fusion | flops 7516192768 | bytes 22544384 | tf_op jit(solution)/shard_map/dot_general | solution.py:146
  203.9 77.5 %reduce-scatter.2.cloned.1.call-done = f32[512,512]{1,0:T(8,128)} async-done(((f32[512,2048]{1,0:T(8,128)}), f32[512,512]{1,0:T(8,128)}) %reduce-scatter.2.cloned.1.call-update) | async-done | bytes 1048592 | tf_op jit(solution)/shard_map/reduce_scatter | solution.py:150
  284.6 3.1 collective-permute-start.17
  287.7 27.3 %collective-permute-done.16 = bf16[256,512]{0,1:T(8,128)(2,1)S(1)} collective-permute-done((bf16[256,512]{0,1:T(8,128)(2,1)S(1)}, bf16[256,512]{0,1:T(8,128)(2,1)S(1)}, u32[]{:S(2)}, u32[]{:S(2)}) %collective-permute-start.16) | collective-permute-done | bytes 262176 | tf_op jit(solution)/shard_map/ppermute | solution.py:166
  315.0 5.6 %collective-permute-done.17 = bf16[256,512]{0,1:T(8,128)(2,1)S(1)} collective-permute-done((bf16[256,512]{0,1:T(8,128)(2,1)S(1)}, bf16[256,512]{0,1:T(8,128)(2,1)S(1)}, u32[]{:S(2)}, u32[]{:S(2)}) %collective-permute-start.17) | collective-permute-done | bytes 262176 | tf_op jit(solution)/shard_map/ppermute | solution.py:166
  (66 shorter events, 36.2 us)
Async XLA Ops:
  7.2 7.3 %copy-start.2 = (bf16[256,4096]{1,0:T(8,128)(2,1)S(1)}, bf16[256,4096]{1,0:T(8,128)(2,1)}, u32[]{:S(2)}) copy-start(bf16[256,4096]{1,0:T(8,128)(2,1)} %param.7) | copy-start | bytes 6291460
  11.7 41.2 %collective-permute-start.1 = (bf16[256,3584]{1,0:T(8,128)(2,1)}, bf16[256,3584]{1,0:T(8,128)(2,1)}, u32[]{:S(2)}, u32[]{:S(2)}) collective-permute-start(bf16[256,3584]{1,0:T(8,128)(2,1)} %fusion.12), channel_id=1, source_target_pairs={{0,8},{4,12},{8,0},{12,4},{16,24},{20,28},{24,16},{28,20},{1,9},{5... | collective-permute-start | bytes 5505032 | tf_op jit(solution)/shard_map/ppermute | solution.py:81
  11.7 43.7 %collective-permute-start.3 = (bf16[256,3584]{1,0:T(8,128)(2,1)}, bf16[256,3584]{1,0:T(8,128)(2,1)}, u32[]{:S(2)}, u32[]{:S(2)}) collective-permute-start(bf16[256,3584]{1,0:T(8,128)(2,1)} %fusion.12), channel_id=1, source_target_pairs={{0,16},{4,20},{8,24},{12,28},{16,0},{20,4},{24,8},{28,12},{1,17},{... | collective-permute-start | bytes 5505032 | tf_op jit(solution)/shard_map/ppermute | solution.py:81
  13.2 48.9 %collective-permute-start = (bf16[256,3584]{1,0:T(8,128)(2,1)}, bf16[256,3584]{1,0:T(8,128)(2,1)}, u32[]{:S(2)}, u32[]{:S(2)}) collective-permute-start(bf16[256,3584]{1,0:T(8,128)(2,1)} %fusion.12), channel_id=1, source_target_pairs={{0,4},{4,0},{8,12},{12,8},{16,20},{20,16},{24,28},{28,24},{1,5},{5... | collective-permute-start | bytes 5505032 | tf_op jit(solution)/shard_map/ppermute | solution.py:81
  16.9 107.0 %all-to-all-start = ((bf16[8,512,256]{2,1,0:T(8,128)(2,1)}), bf16[8,512,256]{2,1,0:T(8,128)(2,1)S(1)}, u32[]{:S(2)}, u32[]{:S(2)}) async-start(bf16[8,512,256]{2,1,0:T(8,128)(2,1)} %bitcast.16), calls=%async_computation | async-start | bytes 4194304 | tf_op jit(solution)/shard_map/all_to_all | solution.py:133
  21.5 259.9 %reduce-scatter.2.cloned.1.call-start = ((), (), s32[]{:S(2)}) async-start(), calls=%async_computation.2 | async-start | bytes 5242880 | tf_op jit(solution)/shard_map/reduce_scatter | solution.py:150
  54.1 40.8 %collective-permute-start.5 = (bf16[128,3584]{1,0:T(8,128)(2,1)S(1)}, bf16[128,3584]{1,0:T(8,128)(2,1)S(1)}, u32[]{:S(2)}, u32[]{:S(2)}) collective-permute-start(bf16[128,3584]{1,0:T(8,128)(2,1)S(1)} %slice.16), channel_id=1, source_target_pairs={{0,16},{4,20},{8,24},{12,28},{16,0},{20,4},{24,8},{28,12},{1,17},{... | collective-permute-start | bytes 2752520 | tf_op jit(solution)/shard_map/ppermute | solution.py:81
  56.7 38.4 %collective-permute-start.6 = (bf16[128,3584]{1,0:T(8,128)(2,1)S(1)}, bf16[128,3584]{1,0:T(8,128)(2,1)S(1)}, u32[]{:S(2)}, u32[]{:S(2)}) collective-permute-start(bf16[128,3584]{1,0:T(8,128)(2,1)S(1)} %slice.17), channel_id=1, source_target_pairs={{0,8},{4,12},{8,0},{12,4},{16,24},{20,28},{24,16},{28,20},{1,9},{5... | collective-permute-start | bytes 2752520 | tf_op jit(solution)/shard_map/ppermute | solution.py:81
  57.0 39.7 %collective-permute-start.2 = (bf16[256,3584]{1,0:T(8,128)(2,1)}, bf16[256,3584]{1,0:T(8,128)(2,1)S(1)}, u32[]{:S(2)}, u32[]{:S(2)}) collective-permute-start(bf16[256,3584]{1,0:T(8,128)(2,1)} %collective-permute-done.1), channel_id=1, source_target_pairs={{0,4},{4,0},{8,12},{12,8},{16,20},{20,16},{24,28},{28,24},{1,5},{5... | collective-permute-start | bytes 5505032 | tf_op jit(solution)/shard_map/ppermute | solution.py:81
  62.1 38.9 %collective-permute-start.4 = (bf16[256,3584]{1,0:T(8,128)(2,1)}, bf16[256,3584]{1,0:T(8,128)(2,1)S(1)}, u32[]{:S(2)}, u32[]{:S(2)}) collective-permute-start(bf16[256,3584]{1,0:T(8,128)(2,1)} %collective-permute-done.3), channel_id=1, source_target_pairs={{0,4},{4,0},{8,12},{12,8},{16,20},{20,16},{24,28},{28,24},{1,5},{5... | collective-permute-start | bytes 5505032 | tf_op jit(solution)/shard_map/ppermute | solution.py:81
  95.1 8.6 %collective-permute-start.7 = (bf16[256,3584]{1,0:T(8,128)(2,1)S(1)}, bf16[256,3584]{1,0:T(8,128)(2,1)S(1)}, u32[]{:S(2)}, u32[]{:S(2)}) collective-permute-start(bf16[256,3584]{1,0:T(8,128)(2,1)S(1)} %constant_dynamic-update-slice_fusion), channel_id=1, source_target_pairs={{0,4},{4,0},{8,12},{12,8},{16,20},{20,16},{24,28},{28,24},{1,5},{5... | collective-permute-start | bytes 5505032 | tf_op jit(solution)/shard_map/ppermute | solution.py:81
  102.4 5.9 %copy-start.3 = (bf16[256,4096]{1,0:T(8,128)(2,1)S(1)}, bf16[256,4096]{1,0:T(8,128)(2,1)}, u32[]{:S(2)}) copy-start(bf16[256,4096]{1,0:T(8,128)(2,1)} %param.7) | copy-start | bytes 6291460
  102.4 5.9 %copy-start.4 = (bf16[256,3584]{1,0:T(8,128)(2,1)S(1)}, bf16[256,3584]{1,0:T(8,128)(2,1)}, u32[]{:S(2)}) copy-start(bf16[256,3584]{1,0:T(8,128)(2,1)} %param.8) | copy-start | bytes 5505028
  102.4 5.9 %copy-start.5 = (bf16[256,3584]{1,0:T(8,128)(2,1)S(1)}, bf16[256,3584]{1,0:T(8,128)(2,1)}, u32[]{:S(2)}) copy-start(bf16[256,3584]{1,0:T(8,128)(2,1)} %param.9) | copy-start | bytes 5505028
  105.2 51.3 %collective-permute-start.9 = (bf16[256,3584]{1,0:T(8,128)(2,1)}, bf16[256,3584]{1,0:T(8,128)(2,1)}, u32[]{:S(2)}, u32[]{:S(2)}) collective-permute-start(bf16[256,3584]{1,0:T(8,128)(2,1)} %param.10), channel_id=1, source_target_pairs={{0,8},{4,12},{8,0},{12,4},{16,24},{20,28},{24,16},{28,20},{1,9},{5... | collective-permute-start | bytes 5505032 | tf_op jit(solution)/shard_map/ppermute | solution.py:81
  106.6 51.5 %collective-permute-start.11 = (bf16[256,3584]{1,0:T(8,128)(2,1)}, bf16[256,3584]{1,0:T(8,128)(2,1)}, u32[]{:S(2)}, u32[]{:S(2)}) collective-permute-start(bf16[256,3584]{1,0:T(8,128)(2,1)} %param.10), channel_id=1, source_target_pairs={{0,16},{4,20},{8,24},{12,28},{16,0},{20,4},{24,8},{28,12},{1,17},{... | collective-permute-start | bytes 5505032 | tf_op jit(solution)/shard_map/ppermute | solution.py:81
  107.8 52.4 %collective-permute-start.8 = (bf16[256,3584]{1,0:T(8,128)(2,1)}, bf16[256,3584]{1,0:T(8,128)(2,1)}, u32[]{:S(2)}, u32[]{:S(2)}) collective-permute-start(bf16[256,3584]{1,0:T(8,128)(2,1)} %param.10), channel_id=1, source_target_pairs={{0,4},{4,0},{8,12},{12,8},{16,20},{20,16},{24,28},{28,24},{1,5},{5... | collective-permute-start | bytes 5505032 | tf_op jit(solution)/shard_map/ppermute | solution.py:81
  157.7 22.0 %collective-permute-start.13 = (bf16[128,3584]{1,0:T(8,128)(2,1)S(1)}, bf16[128,3584]{1,0:T(8,128)(2,1)S(1)}, u32[]{:S(2)}, u32[]{:S(2)}) collective-permute-start(bf16[128,3584]{1,0:T(8,128)(2,1)S(1)} %slice.18), channel_id=1, source_target_pairs={{0,16},{4,20},{8,24},{12,28},{16,0},{20,4},{24,8},{28,12},{1,17},{... | collective-permute-start | bytes 2752520 | tf_op jit(solution)/shard_map/ppermute | solution.py:81
  159.4 21.6 %collective-permute-start.14 = (bf16[128,3584]{1,0:T(8,128)(2,1)S(1)}, bf16[128,3584]{1,0:T(8,128)(2,1)S(1)}, u32[]{:S(2)}, u32[]{:S(2)}) collective-permute-start(bf16[128,3584]{1,0:T(8,128)(2,1)S(1)} %slice.19), channel_id=1, source_target_pairs={{0,8},{4,12},{8,0},{12,4},{16,24},{20,28},{24,16},{28,20},{1,9},{5... | collective-permute-start | bytes 2752520 | tf_op jit(solution)/shard_map/ppermute | solution.py:81
  159.6 22.7 %collective-permute-start.10 = (bf16[256,3584]{1,0:T(8,128)(2,1)}, bf16[256,3584]{1,0:T(8,128)(2,1)S(1)}, u32[]{:S(2)}, u32[]{:S(2)}) collective-permute-start(bf16[256,3584]{1,0:T(8,128)(2,1)} %collective-permute-done.9), channel_id=1, source_target_pairs={{0,4},{4,0},{8,12},{12,8},{16,20},{20,16},{24,28},{28,24},{1,5},{5... | collective-permute-start | bytes 5505032 | tf_op jit(solution)/shard_map/ppermute | solution.py:81
  160.2 26.4 %collective-permute-start.12 = (bf16[256,3584]{1,0:T(8,128)(2,1)}, bf16[256,3584]{1,0:T(8,128)(2,1)S(1)}, u32[]{:S(2)}, u32[]{:S(2)}) collective-permute-start(bf16[256,3584]{1,0:T(8,128)(2,1)} %collective-permute-done.11), channel_id=1, source_target_pairs={{0,4},{4,0},{8,12},{12,8},{16,20},{20,16},{24,28},{28,24},{1,5},{5... | collective-permute-start | bytes 5505032 | tf_op jit(solution)/shard_map/ppermute | solution.py:81
  181.1 8.3 %collective-permute-start.15 = (bf16[256,3584]{1,0:T(8,128)(2,1)S(1)}, bf16[256,3584]{1,0:T(8,128)(2,1)S(1)}, u32[]{:S(2)}, u32[]{:S(2)}) collective-permute-start(bf16[256,3584]{1,0:T(8,128)(2,1)S(1)} %constant_dynamic-update-slice_fusion.2), channel_id=1, source_target_pairs={{0,4},{4,0},{8,12},{12,8},{16,20},{20,16},{24,28},{28,24},{1,5},{5... | collective-permute-start | bytes 5505032 | tf_op jit(solution)/shard_map/ppermute | solution.py:81
  282.8 32.2 %collective-permute-start.16 = (bf16[256,512]{0,1:T(8,128)(2,1)S(1)}, bf16[256,512]{0,1:T(8,128)(2,1)S(1)}, u32[]{:S(2)}, u32[]{:S(2)}) collective-permute-start(bf16[256,512]{0,1:T(8,128)(2,1)S(1)} %get-tuple-element.42), channel_id=1, source_target_pairs={{0,4},{1,12},{2,20},{3,28},{4,0},{5,8},{6,16},{7,24},{8,5},{9,13},... | collective-permute-start | bytes 786440 | tf_op jit(solution)/shard_map/ppermute | solution.py:166
  284.6 36.1 %collective-permute-start.17 = (bf16[256,512]{0,1:T(8,128)(2,1)S(1)}, bf16[256,512]{0,1:T(8,128)(2,1)S(1)}, u32[]{:S(2)}, u32[]{:S(2)}) collective-permute-start(bf16[256,512]{0,1:T(8,128)(2,1)S(1)} %get-tuple-element.41), channel_id=1, source_target_pairs={{0,0},{1,8},{2,16},{3,24},{4,4},{5,12},{6,20},{7,28},{8,1},{9,9},{... | collective-permute-start | bytes 786440 | tf_op jit(solution)/shard_map/ppermute | solution.py:166
  (2 other events, 5.2 us)
Sparse Core Ops, SparseCore 0:
  204.0 77.3 reduce-scatter.1

commit v9 on v7

--- a/solution.py
+++ b/solution.py
@@ -93,7 +93,7 @@
         diagonal,
         swap(diagonal, 1),
     ]
-    return jnp.concatenate(blocks, axis=0)
+    return blocks
 
 
 def shards(grad_out, gate_input, up_input, next_hidden, down_weight, first_moment, second_moment):
@@ -119,10 +119,11 @@
     half = tok // 2
     plane = n_dp == 8
     if plane:
-        hidden_all = gather_plane(hidden)
+        hidden_blocks = gather_plane(hidden)
     else:
-        hidden_all = lax.all_gather(hidden, "dp", axis=0, tiled=True)
-    first_own, hidden_all = lax.optimization_barrier((next_hidden[:half], hidden_all))
+        hidden_blocks = [lax.all_gather(hidden, "dp", axis=0, tiled=True)]
+    first_own, hidden_blocks = lax.optimization_barrier((next_hidden[:half], hidden_blocks))
+    hidden_all = jnp.concatenate(hidden_blocks, axis=0)
     first_next = lax.all_gather(first_own, "dp", axis=0, tiled=True)
     grad_rows = lax.all_to_all(grad_out.T, "dp", 0, 1, tiled=True)
     if plane:

time: 308 us -> 314 us (1.019)
  local copies, waits for them, and re-layouts: 19.2 us -> 25.8 us
    unnamed x22 -> x56, local copies, waits for them, and re-layouts: 13.5 us -> 21.1 us
    all_gather x1, waiting for transfers between devices: 3.72 us -> 0.01 us  [shards(): first_next = lax.all_gather(first_own, 'dp', axis=0, tiled=True)]
    ppermute x8, waiting for transfers between devices: 55 us -> 58.4 us  [swap(): return lax.ppermute(v, 'dp', [(i, i ^ k) for i in range(8)])]
  transfers between devices with their start and end apart: 16 -> 16, of which waited for: 8 -> 8; matrix products, arithmetic and copies ran while one was open for 11% -> 8% of each run, Pallas kernels for 7% -> 7%
where the time goes in v9:
time: 314 us; the launch traced here: 313 us
  waiting for transfers between devices  129 us (41%)
  blocking collectives  52.2 us (17%)
  matrix products  34.3 us (11%)
  starting transfers between devices  31.9 us (10%)
  local copies, waits for them, and re-layouts  25.8 us (8%)
  Pallas kernels  21.6 us (7%)
  between operations  14.2 us (5%)
  other arithmetic  4.46 us (1%)
    ppermute x8, waiting for transfers between devices, swap(): return lax.ppermute(v, 'dp', [(i, i ^ k) for i in range(8)])  58.4 us
    all_to_all x1, blocking collectives, shards(): blocks = lax.all_to_all(partial_out, 'tensor', 1, 0, tiled=True)  52.2 us
    reduce_scatter x1, waiting for transfers between devices, shards(): lax.psum_scatter(partial_out, 'tensor', scatter_dimension=1, tiled=True)  39.8 us
    pallas_call x1, Pallas kernels, owner_update(): pl.pallas_call(functools.partial(adam_kernel, blocks=tokens // tok, tok=t...  21.6 us
    unnamed x56, local copies, waits for them, and re-layouts  21.1 us
    ppermute x4, starting transfers between devices, shards(): pieces.append(lax.ppermute(piece, ('dp', 'tensor'), perm))  19.3 us
    all_to_all x1, waiting for transfers between devices, shards(): grad_rows = lax.all_to_all(grad_out.T, 'dp', 0, 1, tiled=True)  17.6 us
    dot_general x1, matrix products, shards(): jnp.dot(grad_out, down_weight, preferred_element_type=jnp.float32)  17.3 us
  transfers between devices with their start and end apart: 16, of which 8 were waited for; matrix products, arithmetic and copies ran while one was open for 8% of the time, Pallas kernels for 7%

profile of v9, /device:TPU:3, one launch (start us, length us, event | category | flops | bytes accessed | tf_op | source)
XLA Modules:
  0.0 313.2 jit_solution(18020157676545899713)
XLA Ops:
  7.2 3.1 %fusion.12 = bf16[256,3584]{1,0:T(8,128)(2,1)S(1)} fusion(bf16[256,3584]{1,0:T(8,128)(2,1)} %param.9, bf16[256,3584]{1,0:T(8,128)(2,1)} %param.8), kind=kLoop, calls=%fused_computation.17 | loop fusion | flops 7340032 | bytes 5505024 | tf_op jit(solution)/shard_map/convert_element_type | solution.py:112
  10.5 1.5 collective-permute-start.3
  11.9 39.4 %collective-permute-done.1 = bf16[256,3584]{1,0:T(8,128)(2,1)S(1)} collective-permute-done((bf16[256,3584]{1,0:T(8,128)(2,1)S(1)}, bf16[256,3584]{1,0:T(8,128)(2,1)S(1)}, u32[]{:S(2)}, u32[]{:S(2)}) %collective-permute-start.1) | collective-permute-done | bytes 1835040 | tf_op jit(solution)/shard_map/ppermute | solution.py:80
  53.1 2.1 collective-permute-start
  55.7 16.0 %collective-permute-done.5 = bf16[128,3584]{1,0:T(8,128)(2,1)S(1)} collective-permute-done((bf16[128,3584]{1,0:T(8,128)(2,1)S(1)}, bf16[128,3584]{1,0:T(8,128)(2,1)S(1)}, u32[]{:S(2)}, u32[]{:S(2)}) %collective-permute-start.5) | collective-permute-done | bytes 917536 | tf_op jit(solution)/shard_map/ppermute | solution.py:80
  73.0 2.8 collective-permute-start.7
  77.2 2.0 collective-permute-done.7
  80.9 2.5 copy.17
  83.3 3.8 %all-to-all-start = ((bf16[8,512,256]{2,1,0:T(8,128)(2,1)}), bf16[8,512,256]{2,1,0:T(8,128)(2,1)S(1)}, u32[]{:S(2)}, u32[]{:S(2)}) async-start(bf16[8,512,256]{2,1,0:T(8,128)(2,1)} %bitcast.38), calls=%async_computation | async-start | bytes 4194304 | tf_op jit(solution)/shard_map/all_to_all | solution.py:128
  87.1 17.3 %fusion.11 = (bf16[256,3584]{1,0:T(8,128)(2,1)}, bf16[256,3584]{1,0:T(8,128)(2,1)}) fusion(bf16[256,3584]{1,0:T(8,128)(2,1)} %param.8, bf16[256,3584]{1,0:T(8,128)(2,1)} %param.9, bf16[256,4096]{1,0:T(8,128)(2,1)} %param.7, bf16[4096,3584]{1,0:T(8,128)(2,1)} %w_ref.1), kind=kOutput, calls=%fused_computation.16 | convolution fusion | flops 7529955328 | bytes 38797312 | tf_op jit(solution)/shard_map/dot_general | solution.py:135
  104.4 17.6 %all-to-all-done = bf16[8,512,256]{2,1,0:T(8,128)(2,1)S(1)} async-done(((bf16[8,512,256]{2,1,0:T(8,128)(2,1)}), bf16[8,512,256]{2,1,0:T(8,128)(2,1)S(1)}, u32[]{:S(2)}, u32[]{:S(2)}) %all-to-all-start) | async-done | bytes 2097184 | tf_op jit(solution)/shard_map/all_to_all | solution.py:128
  126.0 1.4 copy-done.15
  127.6 1.6 copy-done.5
  133.8 5.2 %copy-done.1 = bf16[2048,3584]{1,0:T(8,128)(2,1)} copy-done((bf16[2048,3584]{1,0:T(8,128)(2,1)}, bf16[2048,3584]{1,0:T(8,128)(2,1)S(1)}, u32[]{:S(2)}) %copy-start.1) | copy-done | bytes 14680088
  139.0 21.6 %shard_map.110 = (f32[512,3584]{1,0:T(8,128)}, f32[512,3584]{1,0:T(8,128)}, bf16[512,3584]{1,0:T(8,128)(2,1)S(1)}) custom-call(s32[1]{0:T(128)} %bitcast.me_ref, bf16[512,2048]{1,0:T(8,128)(2,1)S(1)} %dynamic-slice_dynamic-update-slice_fusion.g_ref, bf16[2048,3584]{1,0:T(8,128)(2,1)} %copy-done.1, f32[512,3584]{1,0:T(8,128)} %m1_ref.1, f32[512,3584]{1,0:T(8,128)} %m2_ref.1, ...), custom_call_target="tpu_custom_call" | custom-call | flops 7516192768 | bytes 53477376 | tf_op jit(solution)/shard_map/pallas_call | solution.py:63
  160.6 1.9 copy-done
  162.5 7.4 %fusion.14 = f32[512,1024]{1,0:T(8,128)S(1)} fusion(bf16[512,3584]{1,0:T(8,128)(2,1)} %copy-done, bf16[1024,3584]{1,0:T(8,128)(2,1)} %all-gather.3.cloned.1.call-done), kind=kOutput, calls=%fused_computation.47 | convolution fusion | flops 3758096384 | bytes 13107200 | tf_op jit(solution)/shard_map/dot_general | solution.py:150
  170.3 52.2 %all_to_all.38 = f32[512,4,256]{2,0,1:T(8,128)S(1)} all-to-all(f32[512,4,256]{2,0,1:T(8,128)S(1)} %bitcast.39), channel_id=1, replica_groups=mesh['dp'=8,'tensor'=4] {'tensor'}, dimensions={1} | all-to-all | bytes 4194304 | tf_op jit(solution)/shard_map/all_to_all | solution.py:156
  222.5 9.6 %fusion.15 = f32[512,1024]{1,0:T(8,128)} fusion(bf16[512,3584]{1,0:T(8,128)(2,1)} %copy-done, bf16[1024,3584]{1,0:T(8,128)(2,1)} %all-gather.5.cloned.1.call-done), kind=kOutput, calls=%fused_computation.48 | convolution fusion | flops 3758096384 | bytes 13107200 | tf_op jit(solution)/shard_map/dot_general | solution.py:150
  232.5 5.6 %collective-permute-start.9 = (bf16[128,512]{0,1:T(8,128)(2,1)S(1)}, bf16[128,512]{0,1:T(8,128)(2,1)S(1)}, u32[]{:S(2)}, u32[]{:S(2)}) collective-permute-start(bf16[128,512]{0,1:T(8,128)(2,1)S(1)} %get-tuple-element.70), channel_id=1, source_target_pairs={{0,0},{1,8},{2,16},{3,24},{4,4},{5,12},{6,20},{7,28},{8,1},{9,9},{... | collective-permute-start | bytes 393224 | tf_op jit(solution)/shard_map/ppermute | solution.py:176
  238.1 39.8 %reduce-scatter.2.cloned.1.call-done = f32[512,256]{1,0:T(8,128)} async-done(((f32[512,1024]{1,0:T(8,128)}), f32[512,256]{1,0:T(8,128)}) %reduce-scatter.2.cloned.1.call-update) | async-done | bytes 524304 | tf_op jit(solution)/shard_map/reduce_scatter | solution.py:160
  279.0 11.7 %collective-permute-start.10 = (bf16[128,512]{0,1:T(8,128)(2,1)S(1)}, bf16[128,512]{0,1:T(8,128)(2,1)S(1)}, u32[]{:S(2)}, u32[]{:S(2)}) collective-permute-start(bf16[128,512]{0,1:T(8,128)(2,1)S(1)} %get-tuple-element.75), channel_id=1, source_target_pairs={{0,4},{1,12},{2,20},{3,28},{4,0},{5,8},{6,16},{7,24},{8,5},{9,13},... | collective-permute-start | bytes 393224 | tf_op jit(solution)/shard_map/ppermute | solution.py:176
  290.7 1.9 collective-permute-start.11
  294.1 11.5 %collective-permute-done.11 = bf16[128,512]{0,1:T(8,128)(2,1)S(1)} collective-permute-done((bf16[128,512]{0,1:T(8,128)(2,1)S(1)}, bf16[128,512]{0,1:T(8,128)(2,1)S(1)}, u32[]{:S(2)}, u32[]{:S(2)}) %collective-permute-start.11) | collective-permute-done | bytes 131104 | tf_op jit(solution)/shard_map/ppermute | solution.py:176
  (89 shorter events, 19.5 us)
Async XLA Ops:
  7.2 155.3 %all-gather.3.cloned.1.call-start = ((), (), s32[]{:S(2)}) async-start(), calls=%async_computation.3 | async-start | bytes 8257536 | tf_op jit(solution)/shard_map/all_gather | solution.py:127
  10.4 61.5 %copy-start.2 = (bf16[256,3584]{1,0:T(8,128)(2,1)}, bf16[256,3584]{1,0:T(8,128)(2,1)S(1)}, u32[]{:S(2)}) copy-start(bf16[256,3584]{1,0:T(8,128)(2,1)S(1)} %fusion.12) | copy-start | bytes 5505028
  10.4 40.9 %collective-permute-start.1 = (bf16[256,3584]{1,0:T(8,128)(2,1)S(1)}, bf16[256,3584]{1,0:T(8,128)(2,1)S(1)}, u32[]{:S(2)}, u32[]{:S(2)}) collective-permute-start(bf16[256,3584]{1,0:T(8,128)(2,1)S(1)} %fusion.12), channel_id=1, source_target_pairs={{0,8},{4,12},{8,0},{12,4},{16,24},{20,28},{24,16},{28,20},{1,9},{5... | collective-permute-start | bytes 5505032 | tf_op jit(solution)/shard_map/ppermute | solution.py:80
  10.5 42.2 %collective-permute-start.3 = (bf16[256,3584]{1,0:T(8,128)(2,1)S(1)}, bf16[256,3584]{1,0:T(8,128)(2,1)S(1)}, u32[]{:S(2)}, u32[]{:S(2)}) collective-permute-start(bf16[256,3584]{1,0:T(8,128)(2,1)S(1)} %fusion.12), channel_id=1, source_target_pairs={{0,16},{4,20},{8,24},{12,28},{16,0},{20,4},{24,8},{28,12},{1,17},{... | collective-permute-start | bytes 5505032 | tf_op jit(solution)/shard_map/ppermute | solution.py:80
  51.3 20.5 %copy-start.6 = (bf16[256,3584]{1,0:T(8,128)(2,1)}, bf16[256,3584]{1,0:T(8,128)(2,1)S(1)}, u32[]{:S(2)}) copy-start(bf16[256,3584]{1,0:T(8,128)(2,1)S(1)} %collective-permute-done.1) | copy-start | bytes 5505028
  51.4 20.4 %collective-permute-start.5 = (bf16[128,3584]{1,0:T(8,128)(2,1)S(1)}, bf16[128,3584]{1,0:T(8,128)(2,1)S(1)}, u32[]{:S(2)}, u32[]{:S(2)}) collective-permute-start(bf16[128,3584]{1,0:T(8,128)(2,1)S(1)} %slice.16), channel_id=1, source_target_pairs={{0,16},{4,20},{8,24},{12,28},{16,0},{20,4},{24,8},{28,12},{1,17},{... | collective-permute-start | bytes 2752520 | tf_op jit(solution)/shard_map/ppermute | solution.py:80
  52.7 20.2 %copy-start.4 = (bf16[256,3584]{1,0:T(8,128)(2,1)}, bf16[256,3584]{1,0:T(8,128)(2,1)S(1)}, u32[]{:S(2)}) copy-start(bf16[256,3584]{1,0:T(8,128)(2,1)S(1)} %collective-permute-done.3) | copy-start | bytes 5505028
  52.8 23.0 %copy-start.11 = (bf16[256,3584]{1,0:T(8,128)(2,1)S(1)}, bf16[256,3584]{1,0:T(8,128)(2,1)}, u32[]{:S(2)}) copy-start(bf16[256,3584]{1,0:T(8,128)(2,1)} %param.10) | copy-start | bytes 5505028
  52.8 20.1 %collective-permute-start.6 = (bf16[128,3584]{1,0:T(8,128)(2,1)S(1)}, bf16[128,3584]{1,0:T(8,128)(2,1)S(1)}, u32[]{:S(2)}, u32[]{:S(2)}) collective-permute-start(bf16[128,3584]{1,0:T(8,128)(2,1)S(1)} %slice.17), channel_id=1, source_target_pairs={{0,8},{4,12},{8,0},{12,4},{16,24},{20,28},{24,16},{28,20},{1,9},{5... | collective-permute-start | bytes 2752520 | tf_op jit(solution)/shard_map/ppermute | solution.py:80
  53.1 24.1 %collective-permute-start = (bf16[256,3584]{1,0:T(8,128)(2,1)S(1)}, bf16[256,3584]{1,0:T(8,128)(2,1)S(1)}, u32[]{:S(2)}, u32[]{:S(2)}) collective-permute-start(bf16[256,3584]{1,0:T(8,128)(2,1)S(1)} %fusion.12), channel_id=1, source_target_pairs={{0,4},{4,0},{8,12},{12,8},{16,20},{20,16},{24,28},{28,24},{1,5},{5... | collective-permute-start | bytes 5505032 | tf_op jit(solution)/shard_map/ppermute | solution.py:80
  55.2 21.9 %collective-permute-start.2 = (bf16[256,3584]{1,0:T(8,128)(2,1)S(1)}, bf16[256,3584]{1,0:T(8,128)(2,1)S(1)}, u32[]{:S(2)}, u32[]{:S(2)}) collective-permute-start(bf16[256,3584]{1,0:T(8,128)(2,1)S(1)} %collective-permute-done.1), channel_id=1, source_target_pairs={{0,4},{4,0},{8,12},{12,8},{16,20},{20,16},{24,28},{28,24},{1,5},{5... | collective-permute-start | bytes 5505032 | tf_op jit(solution)/shard_map/ppermute | solution.py:80
  55.2 22.0 %collective-permute-start.4 = (bf16[256,3584]{1,0:T(8,128)(2,1)S(1)}, bf16[256,3584]{1,0:T(8,128)(2,1)S(1)}, u32[]{:S(2)}, u32[]{:S(2)}) collective-permute-start(bf16[256,3584]{1,0:T(8,128)(2,1)S(1)} %collective-permute-done.3), channel_id=1, source_target_pairs={{0,4},{4,0},{8,12},{12,8},{16,20},{20,16},{24,28},{28,24},{1,5},{5... | collective-permute-start | bytes 5505032 | tf_op jit(solution)/shard_map/ppermute | solution.py:80
  72.9 4.2 %copy-start.8 = (bf16[256,3584]{1,0:T(8,128)(2,1)}, bf16[256,3584]{1,0:T(8,128)(2,1)S(1)}, u32[]{:S(2)}) copy-start(bf16[256,3584]{1,0:T(8,128)(2,1)S(1)} %constant_dynamic-update-slice_fusion) | copy-start | bytes 5505028
  72.9 7.9 %copy-start.10 = (bf16[256,4096]{1,0:T(8,128)(2,1)S(1)}, bf16[256,4096]{1,0:T(8,128)(2,1)}, u32[]{:S(2)}) copy-start(bf16[256,4096]{1,0:T(8,128)(2,1)} %param.7) | copy-start | bytes 6291460
  73.0 6.2 %collective-permute-start.7 = (bf16[256,3584]{1,0:T(8,128)(2,1)S(1)}, bf16[256,3584]{1,0:T(8,128)(2,1)S(1)}, u32[]{:S(2)}, u32[]{:S(2)}) collective-permute-start(bf16[256,3584]{1,0:T(8,128)(2,1)S(1)} %constant_dynamic-update-slice_fusion), channel_id=1, source_target_pairs={{0,4},{4,0},{8,12},{12,8},{16,20},{20,16},{24,28},{28,24},{1,5},{5... | collective-permute-start | bytes 5505032 | tf_op jit(solution)/shard_map/ppermute | solution.py:80
  77.2 2.4 copy-start.12
  83.3 38.7 %all-to-all-start = ((bf16[8,512,256]{2,1,0:T(8,128)(2,1)}), bf16[8,512,256]{2,1,0:T(8,128)(2,1)S(1)}, u32[]{:S(2)}, u32[]{:S(2)}) async-start(bf16[8,512,256]{2,1,0:T(8,128)(2,1)} %bitcast.38), calls=%async_computation | async-start | bytes 4194304 | tf_op jit(solution)/shard_map/all_to_all | solution.py:128
  87.1 135.4 %all-gather.5.cloned.1.call-start = ((), (), s32[]{:S(2)}) async-start(), calls=%async_computation.4 | async-start | bytes 8257536 | tf_op jit(solution)/shard_map/all_gather | solution.py:155
  133.8 5.2 %copy-start.1 = (bf16[2048,3584]{1,0:T(8,128)(2,1)}, bf16[2048,3584]{1,0:T(8,128)(2,1)S(1)}, u32[]{:S(2)}) copy-start(bf16[2048,3584]{1,0:T(8,128)(2,1)S(1)} %constant_dynamic-update-slice_fusion.2.h_ref) | copy-start | bytes 44040196
  169.9 108.0 %reduce-scatter.2.cloned.1.call-start = ((), (), s32[]{:S(2)}) async-start(), calls=%async_computation.5 | async-start | bytes 2621440 | tf_op jit(solution)/shard_map/reduce_scatter | solution.py:160
  232.4 60.3 %collective-permute-start.8 = (bf16[128,512]{0,1:T(8,128)(2,1)S(1)}, bf16[128,512]{0,1:T(8,128)(2,1)S(1)}, u32[]{:S(2)}, u32[]{:S(2)}) collective-permute-start(bf16[128,512]{0,1:T(8,128)(2,1)S(1)} %get-tuple-element.71), channel_id=1, source_target_pairs={{0,4},{1,12},{2,20},{3,28},{4,0},{5,8},{6,16},{7,24},{8,5},{9,13},... | collective-permute-start | bytes 393224 | tf_op jit(solution)/shard_map/ppermute | solution.py:176
  232.5 60.2 %collective-permute-start.9 = (bf16[128,512]{0,1:T(8,128)(2,1)S(1)}, bf16[128,512]{0,1:T(8,128)(2,1)S(1)}, u32[]{:S(2)}, u32[]{:S(2)}) collective-permute-start(bf16[128,512]{0,1:T(8,128)(2,1)S(1)} %get-tuple-element.70), channel_id=1, source_target_pairs={{0,0},{1,8},{2,16},{3,24},{4,4},{5,12},{6,20},{7,28},{8,1},{9,9},{... | collective-permute-start | bytes 393224 | tf_op jit(solution)/shard_map/ppermute | solution.py:176
  279.0 15.1 %collective-permute-start.10 = (bf16[128,512]{0,1:T(8,128)(2,1)S(1)}, bf16[128,512]{0,1:T(8,128)(2,1)S(1)}, u32[]{:S(2)}, u32[]{:S(2)}) collective-permute-start(bf16[128,512]{0,1:T(8,128)(2,1)S(1)} %get-tuple-element.75), channel_id=1, source_target_pairs={{0,4},{1,12},{2,20},{3,28},{4,0},{5,8},{6,16},{7,24},{8,5},{9,13},... | collective-permute-start | bytes 393224 | tf_op jit(solution)/shard_map/ppermute | solution.py:176
  290.7 14.8 %collective-permute-start.11 = (bf16[128,512]{0,1:T(8,128)(2,1)S(1)}, bf16[128,512]{0,1:T(8,128)(2,1)S(1)}, u32[]{:S(2)}, u32[]{:S(2)}) collective-permute-start(bf16[128,512]{0,1:T(8,128)(2,1)S(1)} %get-tuple-element.74), channel_id=1, source_target_pairs={{0,0},{1,8},{2,16},{3,24},{4,4},{5,12},{6,20},{7,28},{8,1},{9,9},{... | collective-permute-start | bytes 393224 | tf_op jit(solution)/shard_map/ppermute | solution.py:176
  (12 other events, 19.7 us)
Sparse Core Ops, SparseCore 0:
  81.0 69.5 all-gather.2
  170.0 50.7 all-gather.4
  232.3 45.5 reduce-scatter.1

commit v10 on v7

--- a/solution.py
+++ b/solution.py
@@ -93,7 +93,7 @@
         diagonal,
         swap(diagonal, 1),
     ]
-    return jnp.concatenate(blocks, axis=0)
+    return blocks
 
 
 def shards(grad_out, gate_input, up_input, next_hidden, down_weight, first_moment, second_moment):
@@ -119,11 +119,14 @@
     half = tok // 2
     plane = n_dp == 8
     if plane:
-        hidden_all = gather_plane(hidden)
+        hidden_all = jnp.concatenate(gather_plane(hidden), axis=0)
     else:
         hidden_all = lax.all_gather(hidden, "dp", axis=0, tiled=True)
     first_own, hidden_all = lax.optimization_barrier((next_hidden[:half], hidden_all))
-    first_next = lax.all_gather(first_own, "dp", axis=0, tiled=True)
+    if plane:
+        first_next = jnp.concatenate(gather_plane(first_own), axis=0)
+    else:
+        first_next = lax.all_gather(first_own, "dp", axis=0, tiled=True)
     grad_rows = lax.all_to_all(grad_out.T, "dp", 0, 1, tiled=True)
     if plane:
         grad_rows = jnp.concatenate(
@@ -164,14 +167,21 @@
     for c in range(2):
         pieces = []
         for k in range(group):
-            s = (sub + k) % group
-            piece = lax.dynamic_slice_in_dim(summed_parts[c], s * half, half, 0)
             perm = []
-            for i in range(n_dp):
-                for j in range(n_t):
-                    si = (i % group + k) % group
-                    dst = (group * j + si) * n_t + i // group
-                    perm.append((i * n_t + j, dst))
+            if plane and c == 0:
+                piece = summed_parts[c][k * half : (k + 1) * half]
+                for i in range(n_dp):
+                    for j in range(n_t):
+                        dst = (i ^ (group * j + k)) * n_t + i // group
+                        perm.append((i * n_t + j, dst))
+            else:
+                s = (sub + k) % group
+                piece = lax.dynamic_slice_in_dim(summed_parts[c], s * half, half, 0)
+                for i in range(n_dp):
+                    for j in range(n_t):
+                        si = (i % group + k) % group
+                        dst = (group * j + si) * n_t + i // group
+                        perm.append((i * n_t + j, dst))
             pieces.append(lax.ppermute(piece, ("dp", "tensor"), perm))
         ordered = []
         for r in range(group):

time: 308 us -> 302 us (0.981)
  waiting for transfers between devices: 130 us -> 113 us
  local copies, waits for them, and re-layouts: 19.2 us -> 26.1 us
  starting transfers between devices: 31.1 us -> 37.5 us
  matrix products: 34.3 us -> 30.2 us
    ppermute x8 -> x16, waiting for transfers between devices: 55 us -> 22 us  [swap(): return lax.ppermute(v, 'dp', [(i, i ^ k) for i in range(8)])]
    all_to_all x1, waiting for transfers between devices: 17.5 us -> 34.6 us  [shards(): grad_rows = lax.all_to_all(grad_out.T, 'dp', 0, 1, tiled=True)]
    ppermute x8 -> x16, starting transfers between devices: 7.69 us -> 15.7 us  [swap(): return lax.ppermute(v, 'dp', [(i, i ^ k) for i in range(8)])]
    unnamed x22 -> x30, local copies, waits for them, and re-layouts: 13.5 us -> 18.1 us
    all_gather x1 -> x0, waiting for transfers between devices: 3.72 us -> none  [shards(): first_next = lax.all_gather(first_own, 'dp', axis=0, tiled=True)]
    dot_general x2, matrix products: 16.9 us -> 13.6 us  [shards(): lax.dot_general(new_shard, next_part, (((1,), (1,)), ((), ())), preferred...]
  transfers between devices with their start and end apart: 16 -> 23, of which waited for: 8 -> 9; matrix products, arithmetic and copies ran while one was open for 11% -> 14% of each run, Pallas kernels for 7% -> 7%
where the time goes in v10:
time: 302 us; the launch traced here: 301 us
  waiting for transfers between devices  113 us (37%)
  blocking collectives  52.3 us (17%)
  starting transfers between devices  37.5 us (12%)
  matrix products  30.2 us (10%)
  local copies, waits for them, and re-layouts  26.1 us (9%)
  Pallas kernels  21.5 us (7%)
  between operations  14.4 us (5%)
  other arithmetic  6.01 us (2%)
    all_to_all x1, blocking collectives, shards(): blocks = lax.all_to_all(partial_out, 'tensor', 1, 0, tiled=True)  52.3 us
    reduce_scatter x1, waiting for transfers between devices, shards(): lax.psum_scatter(partial_out, 'tensor', scatter_dimension=1, tiled=True)  42 us
    all_to_all x1, waiting for transfers between devices, shards(): grad_rows = lax.all_to_all(grad_out.T, 'dp', 0, 1, tiled=True)  34.6 us
    ppermute x16, waiting for transfers between devices, swap(): return lax.ppermute(v, 'dp', [(i, i ^ k) for i in range(8)])  22 us
    pallas_call x1, Pallas kernels, owner_update(): pl.pallas_call(functools.partial(adam_kernel, blocks=tokens // tok, tok=t...  21.5 us
    unnamed x30, local copies, waits for them, and re-layouts  18.1 us
    ppermute x4, starting transfers between devices, shards(): pieces.append(lax.ppermute(piece, ('dp', 'tensor'), perm))  16.6 us
    dot_general x1, matrix products, shards(): jnp.dot(grad_out, down_weight, preferred_element_type=jnp.float32)  16.6 us
  transfers between devices with their start and end apart: 23, of which 9 were waited for; matrix products, arithmetic and copies ran while one was open for 14% of the time, Pallas kernels for 7%

profile of v10, /device:TPU:3, one launch (start us, length us, event | category | flops | bytes accessed | tf_op | source)
XLA Modules:
  0.0 301.5 jit_solution(15965012055074231299)
XLA Ops:
  7.2 4.5 %fusion.12 = bf16[256,3584]{1,0:T(8,128)(2,1)} fusion(bf16[256,3584]{1,0:T(8,128)(2,1)} %param.9, bf16[256,3584]{1,0:T(8,128)(2,1)} %param.8), kind=kLoop, calls=%fused_computation.17 | loop fusion | flops 7340032 | bytes 5505024 | tf_op jit(solution)/shard_map/convert_element_type | solution.py:112
  13.9 2.4 copy.17
  16.3 5.2 %all-to-all-start = ((bf16[8,512,256]{2,1,0:T(8,128)(2,1)}), bf16[8,512,256]{2,1,0:T(8,128)(2,1)S(1)}, u32[]{:S(2)}, u32[]{:S(2)}) async-start(bf16[8,512,256]{2,1,0:T(8,128)(2,1)} %bitcast.37), calls=%async_computation | async-start | bytes 4194304 | tf_op jit(solution)/shard_map/all_to_all | solution.py:130
  21.5 16.6 %fusion.11 = (bf16[256,3584]{1,0:T(8,128)(2,1)}, bf16[256,3584]{1,0:T(8,128)(2,1)}) fusion(bf16[256,3584]{1,0:T(8,128)(2,1)} %param.8, bf16[256,3584]{1,0:T(8,128)(2,1)} %param.9, bf16[256,4096]{1,0:T(8,128)(2,1)} %param.7, bf16[4096,3584]{1,0:T(8,128)(2,1)} %w_ref.1), kind=kOutput, calls=%fused_computation.16 | convolution fusion | flops 7529955328 | bytes 38797312 | tf_op jit(solution)/shard_map/dot_general | solution.py:137
  38.1 3.0 constant_dynamic-update-slice_fusion.8
  42.2 34.6 %all-to-all-done = bf16[8,512,256]{2,1,0:T(8,128)(2,1)S(1)} async-done(((bf16[8,512,256]{2,1,0:T(8,128)(2,1)}), bf16[8,512,256]{2,1,0:T(8,128)(2,1)S(1)}, u32[]{:S(2)}, u32[]{:S(2)}) %all-to-all-start) | async-done | bytes 2097184 | tf_op jit(solution)/shard_map/all_to_all | solution.py:130
  84.1 2.8 constant_dynamic-update-slice_fusion.7
  86.9 2.9 constant_dynamic-update-slice_fusion.6
  89.8 9.6 %collective-permute-done.5 = bf16[128,3584]{1,0:T(8,128)(2,1)S(1)} collective-permute-done((bf16[128,3584]{1,0:T(8,128)(2,1)S(1)}, bf16[128,3584]{1,0:T(8,128)(2,1)S(1)}, u32[]{:S(2)}, u32[]{:S(2)}) %collective-permute-start.5) | collective-permute-done | bytes 917536 | tf_op jit(solution)/shard_map/ppermute | solution.py:80
  99.4 1.8 collective-permute-done.6
  101.4 2.4 collective-permute-start.7
  105.1 2.9 constant_dynamic-update-slice_fusion.4
  114.0 21.5 %shard_map.110 = (f32[512,3584]{1,0:T(8,128)}, f32[512,3584]{1,0:T(8,128)}, bf16[512,3584]{1,0:T(8,128)(2,1)S(1)}) custom-call(s32[1]{0:T(128)} %bitcast.me_ref, bf16[512,2048]{1,0:T(8,128)(2,1)S(1)} %dynamic-slice_dynamic-update-slice_fusion.g_ref, bf16[2048,3584]{1,0:T(8,128)(2,1)} %constant_dynamic-update-slice_fusion.h_ref, f32[512,3584]{1,0:T(8,128)} %m1_ref.1, ...), custom_call_target="tpu_custom_call" | custom-call | flops 7516192768 | bytes 53477376 | tf_op jit(solution)/shard_map/pallas_call | solution.py:63
  139.3 7.4 %collective-permute-done.13 = bf16[64,3584]{1,0:T(8,128)(2,1)S(1)} collective-permute-done((bf16[64,3584]{1,0:T(8,128)(2,1)S(1)}, bf16[64,3584]{1,0:T(8,128)(2,1)S(1)}, u32[]{:S(2)}, u32[]{:S(2)}) %collective-permute-start.13) | collective-permute-done | bytes 458784 | tf_op jit(solution)/shard_map/ppermute | solution.py:80
  148.0 2.3 collective-permute-start.15
  152.5 4.0 %fusion.15 = f32[512,1024]{1,0:T(8,128)S(1)} fusion(bf16[512,3584]{1,0:T(8,128)(2,1)S(1)} %get-tuple-element.29, bf16[1024,3584]{1,0:T(8,128)(2,1)S(1)} %constant_dynamic-update-slice_fusion.9), kind=kOutput, calls=%fused_computation.57 | convolution fusion | flops 3758096384 | bytes 13107200 | tf_op jit(solution)/shard_map/dot_general | solution.py:152
  156.8 52.3 %all_to_all.38 = f32[512,4,256]{2,0,1:T(8,128)S(1)} all-to-all(f32[512,4,256]{2,0,1:T(8,128)S(1)} %bitcast.38), channel_id=1, replica_groups=mesh['dp'=8,'tensor'=4] {'tensor'}, dimensions={1} | all-to-all | bytes 4194304 | tf_op jit(solution)/shard_map/all_to_all | solution.py:158
  209.1 9.6 %fusion.16 = f32[512,1024]{1,0:T(8,128)} fusion(bf16[512,3584]{1,0:T(8,128)(2,1)} %copy-done, bf16[1024,3584]{1,0:T(8,128)(2,1)} %all-gather.2.cloned.1.call-done), kind=kOutput, calls=%fused_computation.58 | convolution fusion | flops 3758096384 | bytes 13107200 | tf_op jit(solution)/shard_map/dot_general | solution.py:152
  220.1 2.1 collective-permute-start.17
  222.4 42.0 %reduce-scatter.2.cloned.1.call-done = f32[512,256]{1,0:T(8,128)} async-done(((f32[512,1024]{1,0:T(8,128)}), f32[512,256]{1,0:T(8,128)}) %reduce-scatter.2.cloned.1.call-update) | async-done | bytes 524304 | tf_op jit(solution)/shard_map/reduce_scatter | solution.py:162
  265.5 11.3 %collective-permute-start.18 = (bf16[128,512]{0,1:T(8,128)(2,1)S(1)}, bf16[128,512]{0,1:T(8,128)(2,1)S(1)}, u32[]{:S(2)}, u32[]{:S(2)}) collective-permute-start(bf16[128,512]{0,1:T(8,128)(2,1)S(1)} %get-tuple-element.61), channel_id=1, source_target_pairs={{0,4},{1,12},{2,20},{3,28},{4,0},{5,8},{6,16},{7,24},{8,5},{9,13},... | collective-permute-start | bytes 393224 | tf_op jit(solution)/shard_map/ppermute | solution.py:185
  276.8 1.9 collective-permute-start.19
  278.7 3.7 %collective-permute-done.18 = bf16[128,512]{0,1:T(8,128)(2,1)S(1)} collective-permute-done((bf16[128,512]{0,1:T(8,128)(2,1)S(1)}, bf16[128,512]{0,1:T(8,128)(2,1)S(1)}, u32[]{:S(2)}, u32[]{:S(2)}) %collective-permute-start.18) | collective-permute-done | bytes 131104 | tf_op jit(solution)/shard_map/ppermute | solution.py:185
  282.4 11.1 %collective-permute-done.19 = bf16[128,512]{0,1:T(8,128)(2,1)S(1)} collective-permute-done((bf16[128,512]{0,1:T(8,128)(2,1)S(1)}, bf16[128,512]{0,1:T(8,128)(2,1)S(1)}, u32[]{:S(2)}, u32[]{:S(2)}) %collective-permute-start.19) | collective-permute-done | bytes 131104 | tf_op jit(solution)/shard_map/ppermute | solution.py:185
  (80 shorter events, 28.9 us)
Async XLA Ops:
  11.7 72.4 %collective-permute-start = (bf16[256,3584]{1,0:T(8,128)(2,1)}, bf16[256,3584]{1,0:T(8,128)(2,1)}, u32[]{:S(2)}, u32[]{:S(2)}) collective-permute-start(bf16[256,3584]{1,0:T(8,128)(2,1)} %fusion.12), channel_id=1, source_target_pairs={{0,4},{4,0},{8,12},{12,8},{16,20},{20,16},{24,28},{28,24},{1,5},{5... | collective-permute-start | bytes 5505032 | tf_op jit(solution)/shard_map/ppermute | solution.py:80
  12.4 64.7 %collective-permute-start.1 = (bf16[256,3584]{1,0:T(8,128)(2,1)}, bf16[256,3584]{1,0:T(8,128)(2,1)}, u32[]{:S(2)}, u32[]{:S(2)}) collective-permute-start(bf16[256,3584]{1,0:T(8,128)(2,1)} %fusion.12), channel_id=1, source_target_pairs={{0,8},{4,12},{8,0},{12,4},{16,24},{20,28},{24,16},{28,20},{1,9},{5... | collective-permute-start | bytes 5505032 | tf_op jit(solution)/shard_map/ppermute | solution.py:80
  12.4 67.1 %collective-permute-start.3 = (bf16[256,3584]{1,0:T(8,128)(2,1)}, bf16[256,3584]{1,0:T(8,128)(2,1)}, u32[]{:S(2)}, u32[]{:S(2)}) collective-permute-start(bf16[256,3584]{1,0:T(8,128)(2,1)} %fusion.12), channel_id=1, source_target_pairs={{0,16},{4,20},{8,24},{12,28},{16,0},{20,4},{24,8},{28,12},{1,17},{... | collective-permute-start | bytes 5505032 | tf_op jit(solution)/shard_map/ppermute | solution.py:80
  16.3 60.5 %all-to-all-start = ((bf16[8,512,256]{2,1,0:T(8,128)(2,1)}), bf16[8,512,256]{2,1,0:T(8,128)(2,1)S(1)}, u32[]{:S(2)}, u32[]{:S(2)}) async-start(bf16[8,512,256]{2,1,0:T(8,128)(2,1)} %bitcast.37), calls=%async_computation | async-start | bytes 4194304 | tf_op jit(solution)/shard_map/all_to_all | solution.py:130
  21.5 187.6 %all-gather.2.cloned.1.call-start = ((), (), s32[]{:S(2)}) async-start(), calls=%async_computation.3 | async-start | bytes 8257536 | tf_op jit(solution)/shard_map/all_gather | solution.py:157
  78.3 21.1 %collective-permute-start.5 = (bf16[128,3584]{1,0:T(8,128)(2,1)S(1)}, bf16[128,3584]{1,0:T(8,128)(2,1)S(1)}, u32[]{:S(2)}, u32[]{:S(2)}) collective-permute-start(bf16[128,3584]{1,0:T(8,128)(2,1)S(1)} %slice.32), channel_id=1, source_target_pairs={{0,16},{4,20},{8,24},{12,28},{16,0},{20,4},{24,8},{28,12},{1,17},{... | collective-permute-start | bytes 2752520 | tf_op jit(solution)/shard_map/ppermute | solution.py:80
  80.7 20.5 %collective-permute-start.6 = (bf16[128,3584]{1,0:T(8,128)(2,1)S(1)}, bf16[128,3584]{1,0:T(8,128)(2,1)S(1)}, u32[]{:S(2)}, u32[]{:S(2)}) collective-permute-start(bf16[128,3584]{1,0:T(8,128)(2,1)S(1)} %slice.33), channel_id=1, source_target_pairs={{0,8},{4,12},{8,0},{12,4},{16,24},{20,28},{24,16},{28,20},{1,9},{5... | collective-permute-start | bytes 2752520 | tf_op jit(solution)/shard_map/ppermute | solution.py:80
  82.0 21.7 %collective-permute-start.2 = (bf16[256,3584]{1,0:T(8,128)(2,1)}, bf16[256,3584]{1,0:T(8,128)(2,1)S(1)}, u32[]{:S(2)}, u32[]{:S(2)}) collective-permute-start(bf16[256,3584]{1,0:T(8,128)(2,1)} %collective-permute-done.1), channel_id=1, source_target_pairs={{0,4},{4,0},{8,12},{12,8},{16,20},{20,16},{24,28},{28,24},{1,5},{5... | collective-permute-start | bytes 5505032 | tf_op jit(solution)/shard_map/ppermute | solution.py:80
  83.7 24.4 %collective-permute-start.4 = (bf16[256,3584]{1,0:T(8,128)(2,1)}, bf16[256,3584]{1,0:T(8,128)(2,1)S(1)}, u32[]{:S(2)}, u32[]{:S(2)}) collective-permute-start(bf16[256,3584]{1,0:T(8,128)(2,1)} %collective-permute-done.3), channel_id=1, source_target_pairs={{0,4},{4,0},{8,12},{12,8},{16,20},{20,16},{24,28},{28,24},{1,5},{5... | collective-permute-start | bytes 5505032 | tf_op jit(solution)/shard_map/ppermute | solution.py:80
  101.4 10.1 %collective-permute-start.7 = (bf16[256,3584]{1,0:T(8,128)(2,1)S(1)}, bf16[256,3584]{1,0:T(8,128)(2,1)S(1)}, u32[]{:S(2)}, u32[]{:S(2)}) collective-permute-start(bf16[256,3584]{1,0:T(8,128)(2,1)S(1)} %pad_maximum_fusion), channel_id=1, source_target_pairs={{0,4},{4,0},{8,12},{12,8},{16,20},{20,16},{24,28},{28,24},{1,5},{5... | collective-permute-start | bytes 5505032 | tf_op jit(solution)/shard_map/ppermute | solution.py:80
  112.8 26.4 %collective-permute-start.8 = (bf16[128,3584]{1,0:T(8,128)(2,1)S(1)}, bf16[128,3584]{1,0:T(8,128)(2,1)S(1)}, u32[]{:S(2)}, u32[]{:S(2)}) collective-permute-start(bf16[128,3584]{1,0:T(8,128)(2,1)S(1)} %get-tuple-element.30), channel_id=1, source_target_pairs={{0,4},{4,0},{8,12},{12,8},{16,20},{20,16},{24,28},{28,24},{1,5},{5... | collective-permute-start | bytes 2752520 | tf_op jit(solution)/shard_map/ppermute | solution.py:80
  112.8 22.8 %collective-permute-start.9 = (bf16[128,3584]{1,0:T(8,128)(2,1)S(1)}, bf16[128,3584]{1,0:T(8,128)(2,1)S(1)}, u32[]{:S(2)}, u32[]{:S(2)}) collective-permute-start(bf16[128,3584]{1,0:T(8,128)(2,1)S(1)} %get-tuple-element.30), channel_id=1, source_target_pairs={{0,8},{4,12},{8,0},{12,4},{16,24},{20,28},{24,16},{28,20},{1,9},{5... | collective-permute-start | bytes 2752520 | tf_op jit(solution)/shard_map/ppermute | solution.py:80
  114.0 23.2 %collective-permute-start.11 = (bf16[128,3584]{1,0:T(8,128)(2,1)S(1)}, bf16[128,3584]{1,0:T(8,128)(2,1)S(1)}, u32[]{:S(2)}, u32[]{:S(2)}) collective-permute-start(bf16[128,3584]{1,0:T(8,128)(2,1)S(1)} %get-tuple-element.30), channel_id=1, source_target_pairs={{0,16},{4,20},{8,24},{12,28},{16,0},{20,4},{24,8},{28,12},{1,17},{... | collective-permute-start | bytes 2752520 | tf_op jit(solution)/shard_map/ppermute | solution.py:80
  135.6 17.0 %copy-start = (bf16[512,3584]{1,0:T(8,128)(2,1)}, bf16[512,3584]{1,0:T(8,128)(2,1)S(1)}, u32[]{:S(2)}) copy-start(bf16[512,3584]{1,0:T(8,128)(2,1)S(1)} %get-tuple-element.29) | copy-start | bytes 11010052
  135.7 11.0 %collective-permute-start.13 = (bf16[64,3584]{1,0:T(8,128)(2,1)S(1)}, bf16[64,3584]{1,0:T(8,128)(2,1)S(1)}, u32[]{:S(2)}, u32[]{:S(2)}) collective-permute-start(bf16[64,3584]{1,0:T(8,128)(2,1)S(1)} %slice.34), channel_id=1, source_target_pairs={{0,16},{4,20},{8,24},{12,28},{16,0},{20,4},{24,8},{28,12},{1,17},{... | collective-permute-start | bytes 1376264 | tf_op jit(solution)/shard_map/ppermute | solution.py:80
  137.2 10.7 %collective-permute-start.14 = (bf16[64,3584]{1,0:T(8,128)(2,1)S(1)}, bf16[64,3584]{1,0:T(8,128)(2,1)S(1)}, u32[]{:S(2)}, u32[]{:S(2)}) collective-permute-start(bf16[64,3584]{1,0:T(8,128)(2,1)S(1)} %slice.35), channel_id=1, source_target_pairs={{0,8},{4,12},{8,0},{12,4},{16,24},{20,28},{24,16},{28,20},{1,9},{5... | collective-permute-start | bytes 1376264 | tf_op jit(solution)/shard_map/ppermute | solution.py:80
  137.6 12.8 %collective-permute-start.10 = (bf16[128,3584]{1,0:T(8,128)(2,1)S(1)}, bf16[128,3584]{1,0:T(8,128)(2,1)S(1)}, u32[]{:S(2)}, u32[]{:S(2)}) collective-permute-start(bf16[128,3584]{1,0:T(8,128)(2,1)S(1)} %collective-permute-done.9), channel_id=1, source_target_pairs={{0,4},{4,0},{8,12},{12,8},{16,20},{20,16},{24,28},{28,24},{1,5},{5... | collective-permute-start | bytes 2752520 | tf_op jit(solution)/shard_map/ppermute | solution.py:80
  139.2 11.3 %collective-permute-start.12 = (bf16[128,3584]{1,0:T(8,128)(2,1)S(1)}, bf16[128,3584]{1,0:T(8,128)(2,1)S(1)}, u32[]{:S(2)}, u32[]{:S(2)}) collective-permute-start(bf16[128,3584]{1,0:T(8,128)(2,1)S(1)} %collective-permute-done.11), channel_id=1, source_target_pairs={{0,4},{4,0},{8,12},{12,8},{16,20},{20,16},{24,28},{28,24},{1,5},{5... | collective-permute-start | bytes 2752520 | tf_op jit(solution)/shard_map/ppermute | solution.py:80
  148.0 4.4 %collective-permute-start.15 = (bf16[128,3584]{1,0:T(8,128)(2,1)S(1)}, bf16[128,3584]{1,0:T(8,128)(2,1)S(1)}, u32[]{:S(2)}, u32[]{:S(2)}) collective-permute-start(bf16[128,3584]{1,0:T(8,128)(2,1)S(1)} %pad_maximum_fusion.1), channel_id=1, source_target_pairs={{0,4},{4,0},{8,12},{12,8},{16,20},{20,16},{24,28},{28,24},{1,5},{5... | collective-permute-start | bytes 2752520 | tf_op jit(solution)/shard_map/ppermute | solution.py:80
  156.5 107.8 %reduce-scatter.2.cloned.1.call-start = ((), (), s32[]{:S(2)}) async-start(), calls=%async_computation.4 | async-start | bytes 2621440 | tf_op jit(solution)/shard_map/reduce_scatter | solution.py:162
  218.9 59.8 %collective-permute-start.16 = (bf16[128,512]{0,1:T(8,128)(2,1)S(1)}, bf16[128,512]{0,1:T(8,128)(2,1)S(1)}, u32[]{:S(2)}, u32[]{:S(2)}) collective-permute-start(bf16[128,512]{0,1:T(8,128)(2,1)S(1)} %get-tuple-element.57), channel_id=1, source_target_pairs={{0,4},{1,12},{2,20},{3,28},{4,0},{5,8},{6,16},{7,24},{8,13},{9,5},... | collective-permute-start | bytes 393224 | tf_op jit(solution)/shard_map/ppermute | solution.py:185
  220.1 58.6 %collective-permute-start.17 = (bf16[128,512]{0,1:T(8,128)(2,1)S(1)}, bf16[128,512]{0,1:T(8,128)(2,1)S(1)}, u32[]{:S(2)}, u32[]{:S(2)}) collective-permute-start(bf16[128,512]{0,1:T(8,128)(2,1)S(1)} %get-tuple-element.56), channel_id=1, source_target_pairs={{0,0},{1,8},{2,16},{3,24},{4,4},{5,12},{6,20},{7,28},{8,9},{9,1},{... | collective-permute-start | bytes 393224 | tf_op jit(solution)/shard_map/ppermute | solution.py:185
  265.5 16.9 %collective-permute-start.18 = (bf16[128,512]{0,1:T(8,128)(2,1)S(1)}, bf16[128,512]{0,1:T(8,128)(2,1)S(1)}, u32[]{:S(2)}, u32[]{:S(2)}) collective-permute-start(bf16[128,512]{0,1:T(8,128)(2,1)S(1)} %get-tuple-element.61), channel_id=1, source_target_pairs={{0,4},{1,12},{2,20},{3,28},{4,0},{5,8},{6,16},{7,24},{8,5},{9,13},... | collective-permute-start | bytes 393224 | tf_op jit(solution)/shard_map/ppermute | solution.py:185
  276.8 16.8 %collective-permute-start.19 = (bf16[128,512]{0,1:T(8,128)(2,1)S(1)}, bf16[128,512]{0,1:T(8,128)(2,1)S(1)}, u32[]{:S(2)}, u32[]{:S(2)}) collective-permute-start(bf16[128,512]{0,1:T(8,128)(2,1)S(1)} %get-tuple-element.60), channel_id=1, source_target_pairs={{0,0},{1,8},{2,16},{3,24},{4,4},{5,12},{6,20},{7,28},{8,1},{9,9},{... | collective-permute-start | bytes 393224 | tf_op jit(solution)/shard_map/ppermute | solution.py:185
  (2 other events, 9.7 us)
Sparse Core Ops, SparseCore 0:
  156.7 50.3 all-gather.1
  218.8 45.5 reduce-scatter.1

commit v11 on v10

--- a/solution.py
+++ b/solution.py
@@ -122,12 +122,14 @@
         hidden_all = jnp.concatenate(gather_plane(hidden), axis=0)
     else:
         hidden_all = lax.all_gather(hidden, "dp", axis=0, tiled=True)
-    first_own, hidden_all = lax.optimization_barrier((next_hidden[:half], hidden_all))
+    first_own, grad_t, hidden_all = lax.optimization_barrier(
+        (next_hidden[:half], grad_out.T, hidden_all)
+    )
     if plane:
         first_next = jnp.concatenate(gather_plane(first_own), axis=0)
     else:
         first_next = lax.all_gather(first_own, "dp", axis=0, tiled=True)
-    grad_rows = lax.all_to_all(grad_out.T, "dp", 0, 1, tiled=True)
+    grad_rows = lax.all_to_all(grad_t, "dp", 0, 1, tiled=True)
     if plane:
         grad_rows = jnp.concatenate(
             [lax.dynamic_slice_in_dim(grad_rows, (me ^ p) * tok, tok, 1) for p in range(n_dp)],

time: 302 us -> 323 us (1.070)
  waiting for transfers between devices: 113 us -> 138 us
    ppermute x16, waiting for transfers between devices: 22 us -> 82.9 us  [swap(): return lax.ppermute(v, 'dp', [(i, i ^ k) for i in range(8)])]
    all_to_all x1, waiting for transfers between devices: 34.6 us -> 0.01 us  [shards(): grad_rows = lax.all_to_all(grad_t, 'dp', 0, 1, tiled=True)]
    ppermute x16, starting transfers between devices: 15.7 us -> 11 us  [swap(): return lax.ppermute(v, 'dp', [(i, i ^ k) for i in range(8)])]
    unnamed x30 -> x44, local copies, waits for them, and re-layouts: 18.1 us -> 19 us
  transfers between devices with their start and end apart: 23 -> 23, of which waited for: 9 -> 7; matrix products, arithmetic and copies ran while one was open for 14% -> 13% of each run, Pallas kernels for 7% -> 7%
where the time goes in v11:
time: 323 us
  waiting for transfers between devices  138 us (43%)
  blocking collectives  52.4 us (16%)
  starting transfers between devices  34.4 us (11%)
  matrix products  28.7 us (9%)
  local copies, waits for them, and re-layouts  26.6 us (8%)
  Pallas kernels  22.4 us (7%)
  between operations  14.5 us (4%)
  other arithmetic  5.76 us (2%)
    ppermute x16, waiting for transfers between devices, swap(): return lax.ppermute(v, 'dp', [(i, i ^ k) for i in range(8)])  82.9 us
    all_to_all x1, blocking collectives, shards(): blocks = lax.all_to_all(partial_out, 'tensor', 1, 0, tiled=True)  52.4 us
    reduce_scatter x1, waiting for transfers between devices, shards(): lax.psum_scatter(partial_out, 'tensor', scatter_dimension=1, tiled=True)  42.3 us
    pallas_call x1, Pallas kernels, owner_update(): pl.pallas_call(functools.partial(adam_kernel, blocks=tokens // tok, tok=t...  22.4 us
    unnamed x44, local copies, waits for them, and re-layouts  19 us
    ppermute x4, starting transfers between devices, shards(): pieces.append(lax.ppermute(piece, ('dp', 'tensor'), perm))  17.6 us
    dot_general x1, matrix products, shards(): jnp.dot(grad_out, down_weight, preferred_element_type=jnp.float32)  15.1 us
    dot_general x2, matrix products, shards(): lax.dot_general(new_shard, next_part, (((1,), (1,)), ((), ())), preferred...  13.6 us
  transfers between devices with their start and end apart: 23, of which 7 were waited for; matrix products, arithmetic and copies ran while one was open for 13% of the time, Pallas kernels for 7%

profile of v11, /device:TPU:3, one launch (start us, length us, event | category | flops | bytes accessed | tf_op | source)
XLA Modules:
  0.0 322.9 jit_solution(15108756872936310245)
XLA Ops:
  7.2 3.3 %fusion.12 = bf16[256,3584]{1,0:T(8,128)(2,1)S(1)} fusion(bf16[256,3584]{1,0:T(8,128)(2,1)} %param.9, bf16[256,3584]{1,0:T(8,128)(2,1)} %param.8), kind=kLoop, calls=%fused_computation.17 | loop fusion | flops 7340032 | bytes 5505024 | tf_op jit(solution)/shard_map/convert_element_type | solution.py:112
  10.5 1.5 collective-permute-start.3
  14.3 37.1 %collective-permute-done.1 = bf16[256,3584]{1,0:T(8,128)(2,1)S(1)} collective-permute-done((bf16[256,3584]{1,0:T(8,128)(2,1)S(1)}, bf16[256,3584]{1,0:T(8,128)(2,1)S(1)}, u32[]{:S(2)}, u32[]{:S(2)}) %collective-permute-start.1) | collective-permute-done | bytes 1835040 | tf_op jit(solution)/shard_map/ppermute | solution.py:80
  51.4 1.5 collective-permute-start.2
  53.0 1.4 constant_dynamic-update-slice_fusion.8
  56.6 1.4 constant_dynamic-update-slice_fusion.7
  58.0 1.4 constant_dynamic-update-slice_fusion.6
  59.4 17.1 %collective-permute-done.5 = bf16[128,3584]{1,0:T(8,128)(2,1)S(1)} collective-permute-done((bf16[128,3584]{1,0:T(8,128)(2,1)S(1)}, bf16[128,3584]{1,0:T(8,128)(2,1)S(1)}, u32[]{:S(2)}, u32[]{:S(2)}) %collective-permute-start.5) | collective-permute-done | bytes 917536 | tf_op jit(solution)/shard_map/ppermute | solution.py:80
  80.1 1.5 constant_dynamic-update-slice_fusion.4
  85.0 1.4 constant_dynamic-update-slice_fusion.h_ref
  86.8 15.1 %fusion.11 = (bf16[256,3584]{1,0:T(8,128)(2,1)}, bf16[256,3584]{1,0:T(8,128)(2,1)}) fusion(bf16[256,3584]{1,0:T(8,128)(2,1)S(1)} %copy-done.5, bf16[256,3584]{1,0:T(8,128)(2,1)S(1)} %copy-done.6, bf16[256,4096]{1,0:T(8,128)(2,1)S(1)} %copy-done.1, bf16[4096,3584]{1,0:T(8,128)(2,1)} %w_ref.1), kind=kOutput, calls=%fused_computation.16 | convolution fusion | flops 7529955328 | bytes 38797312 | tf_op jit(solution)/shard_map/dot_general | solution.py:139
  101.9 2.4 copy.17
  104.3 5.8 %all-to-all-start = ((bf16[8,512,256]{2,1,0:T(8,128)(2,1)}), bf16[8,512,256]{2,1,0:T(8,128)(2,1)S(1)}, u32[]{:S(2)}, u32[]{:S(2)}) async-start(bf16[8,512,256]{2,1,0:T(8,128)(2,1)} %bitcast.37), calls=%async_computation | async-start | bytes 4194304 | tf_op jit(solution)/shard_map/all_to_all | solution.py:132
  117.3 27.7 %collective-permute-done.13 = bf16[64,3584]{1,0:T(8,128)(2,1)S(1)} collective-permute-done((bf16[64,3584]{1,0:T(8,128)(2,1)S(1)}, bf16[64,3584]{1,0:T(8,128)(2,1)S(1)}, u32[]{:S(2)}, u32[]{:S(2)}) %collective-permute-start.13) | collective-permute-done | bytes 458784 | tf_op jit(solution)/shard_map/ppermute | solution.py:80
  147.2 22.4 %shard_map.110 = (f32[512,3584]{1,0:T(8,128)}, f32[512,3584]{1,0:T(8,128)}, bf16[512,3584]{1,0:T(8,128)(2,1)S(1)}) custom-call(s32[1]{0:T(128)} %bitcast.me_ref, bf16[512,2048]{1,0:T(8,128)(2,1)S(1)} %dynamic-slice_dynamic-update-slice_fusion.g_ref, bf16[2048,3584]{1,0:T(8,128)(2,1)} %constant_dynamic-update-slice_fusion.h_ref, f32[512,3584]{1,0:T(8,128)} %m1_ref.1, ...), custom_call_target="tpu_custom_call" | custom-call | flops 7516192768 | bytes 53477376 | tf_op jit(solution)/shard_map/pallas_call | solution.py:63
  169.7 2.1 constant_dynamic-update-slice_fusion.14
  174.5 4.0 %fusion.15 = f32[512,1024]{1,0:T(8,128)S(1)} fusion(bf16[512,3584]{1,0:T(8,128)(2,1)S(1)} %get-tuple-element.31, bf16[1024,3584]{1,0:T(8,128)(2,1)S(1)} %constant_dynamic-update-slice_fusion.9), kind=kOutput, calls=%fused_computation.57 | convolution fusion | flops 3758096384 | bytes 13107200 | tf_op jit(solution)/shard_map/dot_general | solution.py:154
  178.7 52.4 %all_to_all.38 = f32[512,4,256]{2,0,1:T(8,128)S(1)} all-to-all(f32[512,4,256]{2,0,1:T(8,128)S(1)} %bitcast.38), channel_id=1, replica_groups=mesh['dp'=8,'tensor'=4] {'tensor'}, dimensions={1} | all-to-all | bytes 4194304 | tf_op jit(solution)/shard_map/all_to_all | solution.py:160
  231.1 9.6 %fusion.16 = f32[512,1024]{1,0:T(8,128)} fusion(bf16[512,3584]{1,0:T(8,128)(2,1)} %copy-done, bf16[1024,3584]{1,0:T(8,128)(2,1)} %all-gather.2.cloned.1.call-done), kind=kOutput, calls=%fused_computation.58 | convolution fusion | flops 3758096384 | bytes 13107200 | tf_op jit(solution)/shard_map/dot_general | solution.py:154
  241.9 2.3 collective-permute-start.17
  244.2 42.3 %reduce-scatter.2.cloned.1.call-done = f32[512,256]{1,0:T(8,128)} async-done(((f32[512,1024]{1,0:T(8,128)}), f32[512,256]{1,0:T(8,128)}) %reduce-scatter.2.cloned.1.call-update) | async-done | bytes 524304 | tf_op jit(solution)/shard_map/reduce_scatter | solution.py:164
  287.6 12.4 %collective-permute-start.18 = (bf16[128,512]{0,1:T(8,128)(2,1)S(1)}, bf16[128,512]{0,1:T(8,128)(2,1)S(1)}, u32[]{:S(2)}, u32[]{:S(2)}) collective-permute-start(bf16[128,512]{0,1:T(8,128)(2,1)S(1)} %get-tuple-element.63), channel_id=1, source_target_pairs={{0,4},{1,12},{2,20},{3,28},{4,0},{5,8},{6,16},{7,24},{8,5},{9,13},... | collective-permute-start | bytes 393224 | tf_op jit(solution)/shard_map/ppermute | solution.py:187
  300.1 1.9 collective-permute-start.19
  303.3 11.6 %collective-permute-done.19 = bf16[128,512]{0,1:T(8,128)(2,1)S(1)} collective-permute-done((bf16[128,512]{0,1:T(8,128)(2,1)S(1)}, bf16[128,512]{0,1:T(8,128)(2,1)S(1)}, u32[]{:S(2)}, u32[]{:S(2)}) %collective-permute-start.19) | collective-permute-done | bytes 131104 | tf_op jit(solution)/shard_map/ppermute | solution.py:187
  (95 shorter events, 29.1 us)
Async XLA Ops:
  10.5 40.9 %collective-permute-start.1 = (bf16[256,3584]{1,0:T(8,128)(2,1)S(1)}, bf16[256,3584]{1,0:T(8,128)(2,1)S(1)}, u32[]{:S(2)}, u32[]{:S(2)}) collective-permute-start(bf16[256,3584]{1,0:T(8,128)(2,1)S(1)} %fusion.12), channel_id=1, source_target_pairs={{0,8},{4,12},{8,0},{12,4},{16,24},{20,28},{24,16},{28,20},{1,9},{5... | collective-permute-start | bytes 5505032 | tf_op jit(solution)/shard_map/ppermute | solution.py:80
  10.5 45.2 %collective-permute-start.3 = (bf16[256,3584]{1,0:T(8,128)(2,1)S(1)}, bf16[256,3584]{1,0:T(8,128)(2,1)S(1)}, u32[]{:S(2)}, u32[]{:S(2)}) collective-permute-start(bf16[256,3584]{1,0:T(8,128)(2,1)S(1)} %fusion.12), channel_id=1, source_target_pairs={{0,16},{4,20},{8,24},{12,28},{16,0},{20,4},{24,8},{28,12},{1,17},{... | collective-permute-start | bytes 5505032 | tf_op jit(solution)/shard_map/ppermute | solution.py:80
  12.0 44.6 %collective-permute-start = (bf16[256,3584]{1,0:T(8,128)(2,1)S(1)}, bf16[256,3584]{1,0:T(8,128)(2,1)S(1)}, u32[]{:S(2)}, u32[]{:S(2)}) collective-permute-start(bf16[256,3584]{1,0:T(8,128)(2,1)S(1)} %fusion.12), channel_id=1, source_target_pairs={{0,4},{4,0},{8,12},{12,8},{16,20},{20,16},{24,28},{28,24},{1,5},{5... | collective-permute-start | bytes 5505032 | tf_op jit(solution)/shard_map/ppermute | solution.py:80
  51.4 27.4 %collective-permute-start.2 = (bf16[256,3584]{1,0:T(8,128)(2,1)S(1)}, bf16[256,3584]{1,0:T(8,128)(2,1)S(1)}, u32[]{:S(2)}, u32[]{:S(2)}) collective-permute-start(bf16[256,3584]{1,0:T(8,128)(2,1)S(1)} %collective-permute-done.1), channel_id=1, source_target_pairs={{0,4},{4,0},{8,12},{12,8},{16,20},{20,16},{24,28},{28,24},{1,5},{5... | collective-permute-start | bytes 5505032 | tf_op jit(solution)/shard_map/ppermute | solution.py:80
  54.4 22.0 %collective-permute-start.5 = (bf16[128,3584]{1,0:T(8,128)(2,1)S(1)}, bf16[128,3584]{1,0:T(8,128)(2,1)S(1)}, u32[]{:S(2)}, u32[]{:S(2)}) collective-permute-start(bf16[128,3584]{1,0:T(8,128)(2,1)S(1)} %slice.32), channel_id=1, source_target_pairs={{0,16},{4,20},{8,24},{12,28},{16,0},{20,4},{24,8},{28,12},{1,17},{... | collective-permute-start | bytes 2752520 | tf_op jit(solution)/shard_map/ppermute | solution.py:80
  55.8 21.7 %collective-permute-start.6 = (bf16[128,3584]{1,0:T(8,128)(2,1)S(1)}, bf16[128,3584]{1,0:T(8,128)(2,1)S(1)}, u32[]{:S(2)}, u32[]{:S(2)}) collective-permute-start(bf16[128,3584]{1,0:T(8,128)(2,1)S(1)} %slice.33), channel_id=1, source_target_pairs={{0,8},{4,12},{8,0},{12,4},{16,24},{20,28},{24,16},{28,20},{1,9},{5... | collective-permute-start | bytes 2752520 | tf_op jit(solution)/shard_map/ppermute | solution.py:80
  56.1 25.5 %collective-permute-start.4 = (bf16[256,3584]{1,0:T(8,128)(2,1)S(1)}, bf16[256,3584]{1,0:T(8,128)(2,1)S(1)}, u32[]{:S(2)}, u32[]{:S(2)}) collective-permute-start(bf16[256,3584]{1,0:T(8,128)(2,1)S(1)} %collective-permute-done.3), channel_id=1, source_target_pairs={{0,4},{4,0},{8,12},{12,8},{16,20},{20,16},{24,28},{28,24},{1,5},{5... | collective-permute-start | bytes 5505032 | tf_op jit(solution)/shard_map/ppermute | solution.py:80
  77.6 7.4 %collective-permute-start.7 = (bf16[256,3584]{1,0:T(8,128)(2,1)S(1)}, bf16[256,3584]{1,0:T(8,128)(2,1)S(1)}, u32[]{:S(2)}, u32[]{:S(2)}) collective-permute-start(bf16[256,3584]{1,0:T(8,128)(2,1)S(1)} %pad_maximum_fusion), channel_id=1, source_target_pairs={{0,4},{4,0},{8,12},{12,8},{16,20},{20,16},{24,28},{28,24},{1,5},{5... | collective-permute-start | bytes 5505032 | tf_op jit(solution)/shard_map/ppermute | solution.py:80
  86.4 28.5 %collective-permute-start.8 = (bf16[128,3584]{1,0:T(8,128)(2,1)S(1)}, bf16[128,3584]{1,0:T(8,128)(2,1)}, u32[]{:S(2)}, u32[]{:S(2)}) collective-permute-start(bf16[128,3584]{1,0:T(8,128)(2,1)S(1)} %get-tuple-element.32), channel_id=1, source_target_pairs={{0,4},{4,0},{8,12},{12,8},{16,20},{20,16},{24,28},{28,24},{1,5},{5... | collective-permute-start | bytes 2752520 | tf_op jit(solution)/shard_map/ppermute | solution.py:80
  86.4 23.8 %collective-permute-start.9 = (bf16[128,3584]{1,0:T(8,128)(2,1)S(1)}, bf16[128,3584]{1,0:T(8,128)(2,1)}, u32[]{:S(2)}, u32[]{:S(2)}) collective-permute-start(bf16[128,3584]{1,0:T(8,128)(2,1)S(1)} %get-tuple-element.32), channel_id=1, source_target_pairs={{0,8},{4,12},{8,0},{12,4},{16,24},{20,28},{24,16},{28,20},{1,9},{5... | collective-permute-start | bytes 2752520 | tf_op jit(solution)/shard_map/ppermute | solution.py:80
  86.6 25.9 %collective-permute-start.11 = (bf16[128,3584]{1,0:T(8,128)(2,1)S(1)}, bf16[128,3584]{1,0:T(8,128)(2,1)}, u32[]{:S(2)}, u32[]{:S(2)}) collective-permute-start(bf16[128,3584]{1,0:T(8,128)(2,1)S(1)} %get-tuple-element.32), channel_id=1, source_target_pairs={{0,16},{4,20},{8,24},{12,28},{16,0},{20,4},{24,8},{28,12},{1,17},{... | collective-permute-start | bytes 2752520 | tf_op jit(solution)/shard_map/ppermute | solution.py:80
  104.3 42.2 %all-to-all-start = ((bf16[8,512,256]{2,1,0:T(8,128)(2,1)}), bf16[8,512,256]{2,1,0:T(8,128)(2,1)S(1)}, u32[]{:S(2)}, u32[]{:S(2)}) async-start(bf16[8,512,256]{2,1,0:T(8,128)(2,1)} %bitcast.37), calls=%async_computation | async-start | bytes 4194304 | tf_op jit(solution)/shard_map/all_to_all | solution.py:132
  110.1 121.0 %all-gather.2.cloned.1.call-start = ((), (), s32[]{:S(2)}) async-start(), calls=%async_computation.3 | async-start | bytes 8257536 | tf_op jit(solution)/shard_map/all_gather | solution.py:159
  111.2 33.8 %collective-permute-start.13 = (bf16[64,3584]{1,0:T(8,128)(2,1)S(1)}, bf16[64,3584]{1,0:T(8,128)(2,1)S(1)}, u32[]{:S(2)}, u32[]{:S(2)}) collective-permute-start(bf16[64,3584]{1,0:T(8,128)(2,1)S(1)} %slice.34), channel_id=1, source_target_pairs={{0,16},{4,20},{8,24},{12,28},{16,0},{20,4},{24,8},{28,12},{1,17},{... | collective-permute-start | bytes 1376264 | tf_op jit(solution)/shard_map/ppermute | solution.py:80
  113.6 31.4 %collective-permute-start.14 = (bf16[64,3584]{1,0:T(8,128)(2,1)S(1)}, bf16[64,3584]{1,0:T(8,128)(2,1)S(1)}, u32[]{:S(2)}, u32[]{:S(2)}) collective-permute-start(bf16[64,3584]{1,0:T(8,128)(2,1)S(1)} %slice.35), channel_id=1, source_target_pairs={{0,8},{4,12},{8,0},{12,4},{16,24},{20,28},{24,16},{28,20},{1,9},{5... | collective-permute-start | bytes 1376264 | tf_op jit(solution)/shard_map/ppermute | solution.py:80
  113.9 55.7 %collective-permute-start.10 = (bf16[128,3584]{1,0:T(8,128)(2,1)}, bf16[128,3584]{1,0:T(8,128)(2,1)}, u32[]{:S(2)}, u32[]{:S(2)}) collective-permute-start(bf16[128,3584]{1,0:T(8,128)(2,1)} %collective-permute-done.9), channel_id=1, source_target_pairs={{0,4},{4,0},{8,12},{12,8},{16,20},{20,16},{24,28},{28,24},{1,5},{5... | collective-permute-start | bytes 2752520 | tf_op jit(solution)/shard_map/ppermute | solution.py:80
  114.8 58.2 %collective-permute-start.12 = (bf16[128,3584]{1,0:T(8,128)(2,1)}, bf16[128,3584]{1,0:T(8,128)(2,1)}, u32[]{:S(2)}, u32[]{:S(2)}) collective-permute-start(bf16[128,3584]{1,0:T(8,128)(2,1)} %collective-permute-done.11), channel_id=1, source_target_pairs={{0,4},{4,0},{8,12},{12,8},{16,20},{20,16},{24,28},{28,24},{1,5},{5... | collective-permute-start | bytes 2752520 | tf_op jit(solution)/shard_map/ppermute | solution.py:80
  117.3 28.7 %copy-start.7 = (bf16[1024,3584]{1,0:T(8,128)(2,1)}, bf16[1024,3584]{1,0:T(8,128)(2,1)S(1)}, u32[]{:S(2)}) copy-start(bf16[1024,3584]{1,0:T(8,128)(2,1)S(1)} %constant_dynamic-update-slice_fusion.15) | copy-start | bytes 22020100
  146.1 28.3 %collective-permute-start.15 = (bf16[128,3584]{1,0:T(8,128)(2,1)}, bf16[128,3584]{1,0:T(8,128)(2,1)S(1)}, u32[]{:S(2)}, u32[]{:S(2)}) collective-permute-start(bf16[128,3584]{1,0:T(8,128)(2,1)} %pad_maximum_fusion.1), channel_id=1, source_target_pairs={{0,4},{4,0},{8,12},{12,8},{16,20},{20,16},{24,28},{28,24},{1,5},{5... | collective-permute-start | bytes 2752520 | tf_op jit(solution)/shard_map/ppermute | solution.py:80
  178.5 108.0 %reduce-scatter.2.cloned.1.call-start = ((), (), s32[]{:S(2)}) async-start(), calls=%async_computation.4 | async-start | bytes 2621440 | tf_op jit(solution)/shard_map/reduce_scatter | solution.py:164
  240.9 61.1 %collective-permute-start.16 = (bf16[128,512]{0,1:T(8,128)(2,1)S(1)}, bf16[128,512]{0,1:T(8,128)(2,1)S(1)}, u32[]{:S(2)}, u32[]{:S(2)}) collective-permute-start(bf16[128,512]{0,1:T(8,128)(2,1)S(1)} %get-tuple-element.59), channel_id=1, source_target_pairs={{0,4},{1,12},{2,20},{3,28},{4,0},{5,8},{6,16},{7,24},{8,13},{9,5},... | collective-permute-start | bytes 393224 | tf_op jit(solution)/shard_map/ppermute | solution.py:187
  241.9 60.1 %collective-permute-start.17 = (bf16[128,512]{0,1:T(8,128)(2,1)S(1)}, bf16[128,512]{0,1:T(8,128)(2,1)S(1)}, u32[]{:S(2)}, u32[]{:S(2)}) collective-permute-start(bf16[128,512]{0,1:T(8,128)(2,1)S(1)} %get-tuple-element.58), channel_id=1, source_target_pairs={{0,0},{1,8},{2,16},{3,24},{4,4},{5,12},{6,20},{7,28},{8,9},{9,1},{... | collective-permute-start | bytes 393224 | tf_op jit(solution)/shard_map/ppermute | solution.py:187
  287.6 15.7 %collective-permute-start.18 = (bf16[128,512]{0,1:T(8,128)(2,1)S(1)}, bf16[128,512]{0,1:T(8,128)(2,1)S(1)}, u32[]{:S(2)}, u32[]{:S(2)}) collective-permute-start(bf16[128,512]{0,1:T(8,128)(2,1)S(1)} %get-tuple-element.63), channel_id=1, source_target_pairs={{0,4},{1,12},{2,20},{3,28},{4,0},{5,8},{6,16},{7,24},{8,5},{9,13},... | collective-permute-start | bytes 393224 | tf_op jit(solution)/shard_map/ppermute | solution.py:187
  300.1 14.9 %collective-permute-start.19 = (bf16[128,512]{0,1:T(8,128)(2,1)S(1)}, bf16[128,512]{0,1:T(8,128)(2,1)S(1)}, u32[]{:S(2)}, u32[]{:S(2)}) collective-permute-start(bf16[128,512]{0,1:T(8,128)(2,1)S(1)} %get-tuple-element.62), channel_id=1, source_target_pairs={{0,0},{1,8},{2,16},{3,24},{4,4},{5,12},{6,20},{7,28},{8,1},{9,9},{... | collective-permute-start | bytes 393224 | tf_op jit(solution)/shard_map/ppermute | solution.py:187
  (9 other events, 72.9 us)
Sparse Core Ops, SparseCore 0:
  178.6 50.2 all-gather.1
  240.8 45.6 reduce-scatter.1

commit v12 on v10

--- a/solution.py
+++ b/solution.py
@@ -73,7 +73,7 @@
     )(jnp.reshape(me, (1,)).astype(jnp.int32), grad_rows, hidden_all, first_moment, second_moment, down_weight)
 
 
-def gather_plane(x):
+def gather_plane(x, extra=None):
     half = x.shape[0] // 2
 
     def swap(v, k):
@@ -82,6 +82,8 @@
     along_x = swap(x, 2)
     along_y = swap(x, 4)
     partner = swap(x, 1)
+    if extra is not None:
+        along_x, along_y, partner, extra = lax.optimization_barrier((along_x, along_y, partner, extra))
     diagonal = jnp.concatenate([swap(along_x[:half], 4), swap(along_y[half:], 2)], axis=0)
     blocks = [
         x,
@@ -93,7 +95,7 @@
         diagonal,
         swap(diagonal, 1),
     ]
-    return blocks
+    return blocks, extra
 
 
 def shards(grad_out, gate_input, up_input, next_hidden, down_weight, first_moment, second_moment):
@@ -119,15 +121,17 @@
     half = tok // 2
     plane = n_dp == 8
     if plane:
-        hidden_all = jnp.concatenate(gather_plane(hidden), axis=0)
+        hidden_blocks, grad_t = gather_plane(hidden, grad_out.T)
+        hidden_all = jnp.concatenate(hidden_blocks, axis=0)
     else:
         hidden_all = lax.all_gather(hidden, "dp", axis=0, tiled=True)
+        grad_t = grad_out.T
     first_own, hidden_all = lax.optimization_barrier((next_hidden[:half], hidden_all))
     if plane:
-        first_next = jnp.concatenate(gather_plane(first_own), axis=0)
+        first_next = jnp.concatenate(gather_plane(first_own)[0], axis=0)
     else:
         first_next = lax.all_gather(first_own, "dp", axis=0, tiled=True)
-    grad_rows = lax.all_to_all(grad_out.T, "dp", 0, 1, tiled=True)
+    grad_rows = lax.all_to_all(grad_t, "dp", 0, 1, tiled=True)
     if plane:
         grad_rows = jnp.concatenate(
             [lax.dynamic_slice_in_dim(grad_rows, (me ^ p) * tok, tok, 1) for p in range(n_dp)],

time: 302 us -> 312 us (1.033)
  local copies, waits for them, and re-layouts: 26.1 us -> 34.2 us
  waiting for transfers between devices: 113 us -> 117 us
    ppermute x16, waiting for transfers between devices: 22 us -> 60.6 us  [swap(): return lax.ppermute(v, 'dp', [(i, i ^ k) for i in range(8)])]
    all_to_all x1, waiting for transfers between devices: 34.6 us -> 0.01 us  [shards(): grad_rows = lax.all_to_all(grad_t, 'dp', 0, 1, tiled=True)]
    optimization_barrier x0 -> x1, local copies, waits for them, and re-layouts: none -> 4.07 us  [gather_plane(): lax.optimization_barrier((along_x, along_y, partner, extra))]
    unnamed x30 -> x36, local copies, waits for them, and re-layouts: 18.1 us -> 21.7 us
    ppermute x16, starting transfers between devices: 15.7 us -> 12.2 us  [swap(): return lax.ppermute(v, 'dp', [(i, i ^ k) for i in range(8)])]
where the time goes in v12:
time: 312 us; the launch traced here: 311 us
  waiting for transfers between devices  117 us (38%)
  blocking collectives  52.1 us (17%)
  starting transfers between devices  36 us (12%)
  local copies, waits for them, and re-layouts  34.2 us (11%)
  matrix products  30.1 us (10%)
  Pallas kernels  21.6 us (7%)
  between operations  14.4 us (5%)
  other arithmetic  5.96 us (2%)
    ppermute x16, waiting for transfers between devices, swap(): return lax.ppermute(v, 'dp', [(i, i ^ k) for i in range(8)])  60.6 us
    all_to_all x1, blocking collectives, shards(): blocks = lax.all_to_all(partial_out, 'tensor', 1, 0, tiled=True)  52.1 us
    reduce_scatter x1, waiting for transfers between devices, shards(): lax.psum_scatter(partial_out, 'tensor', scatter_dimension=1, tiled=True)  42.1 us
    unnamed x36, local copies, waits for them, and re-layouts  21.7 us
    pallas_call x1, Pallas kernels, owner_update(): pl.pallas_call(functools.partial(adam_kernel, blocks=tokens // tok, tok=t...  21.6 us
    ppermute x4, starting transfers between devices, shards(): pieces.append(lax.ppermute(piece, ('dp', 'tensor'), perm))  17.4 us
    dot_general x1, matrix products, shards(): jnp.dot(grad_out, down_weight, preferred_element_type=jnp.float32)  16.5 us
    ppermute x4, waiting for transfers between devices, shards(): pieces.append(lax.ppermute(piece, ('dp', 'tensor'), perm))  13.9 us
  transfers between devices with their start and end apart: 23, of which 9 were waited for; matrix products, arithmetic and copies ran while one was open for 14% of the time, Pallas kernels for 7%

profile of v12, /device:TPU:3, one launch (start us, length us, event | category | flops | bytes accessed | tf_op | source)
XLA Modules:
  0.0 311.0 jit_solution(1403022904952412409)
XLA Ops:
  7.2 3.1 %fusion.12 = bf16[256,3584]{1,0:T(8,128)(2,1)S(1)} fusion(bf16[256,3584]{1,0:T(8,128)(2,1)} %param.9, bf16[256,3584]{1,0:T(8,128)(2,1)} %param.8), kind=kLoop, calls=%fused_computation.17 | loop fusion | flops 7340032 | bytes 5505024 | tf_op jit(solution)/shard_map/convert_element_type | solution.py:114
  13.1 2.5 fusion.13
  15.7 16.5 %fusion.11 = (bf16[256,3584]{1,0:T(8,128)(2,1)}, bf16[256,3584]{1,0:T(8,128)(2,1)}) fusion(bf16[256,3584]{1,0:T(8,128)(2,1)} %param.8, bf16[256,3584]{1,0:T(8,128)(2,1)} %param.9, bf16[256,4096]{1,0:T(8,128)(2,1)} %param.7, bf16[4096,3584]{1,0:T(8,128)(2,1)} %w_ref.1), kind=kOutput, calls=%fused_computation.16 | convolution fusion | flops 7529955328 | bytes 38797312 | tf_op jit(solution)/shard_map/dot_general | solution.py:141
  32.2 19.2 %collective-permute-done = bf16[256,3584]{1,0:T(8,128)(2,1)} collective-permute-done((bf16[256,3584]{1,0:T(8,128)(2,1)S(1)}, bf16[256,3584]{1,0:T(8,128)(2,1)}, u32[]{:S(2)}, u32[]{:S(2)}) %collective-permute-start) | collective-permute-done | bytes 1835040 | tf_op jit(solution)/shard_map/ppermute | solution.py:80
  51.5 4.1 %copy.17 = bf16[4096,256]{1,0:T(8,128)(2,1)} copy(bf16[4096,256]{0,1:T(8,128)(2,1)} %bitcast.39) | data formatting | bytes 4194304 | tf_op jit(solution)/shard_map/optimization_barrier | solution.py:86
  55.5 6.4 %all-to-all-start = ((bf16[8,512,256]{2,1,0:T(8,128)(2,1)}), bf16[8,512,256]{2,1,0:T(8,128)(2,1)S(1)}, u32[]{:S(2)}, u32[]{:S(2)}) async-start(bf16[8,512,256]{2,1,0:T(8,128)(2,1)} %bitcast.37), calls=%async_computation | async-start | bytes 4194304 | tf_op jit(solution)/shard_map/all_to_all | solution.py:134
  61.9 2.9 constant_dynamic-update-slice_fusion.8
  69.4 2.8 constant_dynamic-update-slice_fusion.7
  72.2 2.9 constant_dynamic-update-slice_fusion.6
  75.1 31.5 %collective-permute-done.5 = bf16[128,3584]{1,0:T(8,128)(2,1)S(1)} collective-permute-done((bf16[128,3584]{1,0:T(8,128)(2,1)S(1)}, bf16[128,3584]{1,0:T(8,128)(2,1)S(1)}, u32[]{:S(2)}, u32[]{:S(2)}) %collective-permute-start.5) | collective-permute-done | bytes 917536 | tf_op jit(solution)/shard_map/ppermute | solution.py:80
  109.7 2.9 constant_dynamic-update-slice_fusion.5
  112.5 3.0 constant_dynamic-update-slice_fusion.4
  115.6 2.9 constant_dynamic-update-slice_fusion.3
  120.5 2.8 constant_dynamic-update-slice_fusion.h_ref
  124.7 21.6 %shard_map.110 = (f32[512,3584]{1,0:T(8,128)}, f32[512,3584]{1,0:T(8,128)}, bf16[512,3584]{1,0:T(8,128)(2,1)S(1)}) custom-call(s32[1]{0:T(128)} %bitcast.me_ref, bf16[512,2048]{1,0:T(8,128)(2,1)S(1)} %dynamic-slice_dynamic-update-slice_fusion.g_ref, bf16[2048,3584]{1,0:T(8,128)(2,1)} %constant_dynamic-update-slice_fusion.h_ref, f32[512,3584]{1,0:T(8,128)} %m1_ref.1, ...), custom_call_target="tpu_custom_call" | custom-call | flops 7516192768 | bytes 53477376 | tf_op jit(solution)/shard_map/pallas_call | solution.py:63
  149.9 7.5 %collective-permute-done.13 = bf16[64,3584]{1,0:T(8,128)(2,1)S(1)} collective-permute-done((bf16[64,3584]{1,0:T(8,128)(2,1)S(1)}, bf16[64,3584]{1,0:T(8,128)(2,1)S(1)}, u32[]{:S(2)}, u32[]{:S(2)}) %collective-permute-start.13) | collective-permute-done | bytes 458784 | tf_op jit(solution)/shard_map/ppermute | solution.py:80
  162.3 4.0 %fusion.15 = f32[512,1024]{1,0:T(8,128)S(1)} fusion(bf16[512,3584]{1,0:T(8,128)(2,1)S(1)} %get-tuple-element.37, bf16[1024,3584]{1,0:T(8,128)(2,1)S(1)} %constant_dynamic-update-slice_fusion.9), kind=kOutput, calls=%fused_computation.57 | convolution fusion | flops 3758096384 | bytes 13107200 | tf_op jit(solution)/shard_map/dot_general | solution.py:156
  166.5 52.1 %all_to_all.38 = f32[512,4,256]{2,0,1:T(8,128)S(1)} all-to-all(f32[512,4,256]{2,0,1:T(8,128)S(1)} %bitcast.38), channel_id=1, replica_groups=mesh['dp'=8,'tensor'=4] {'tensor'}, dimensions={1} | all-to-all | bytes 4194304 | tf_op jit(solution)/shard_map/all_to_all | solution.py:162
  218.7 9.6 %fusion.16 = f32[512,1024]{1,0:T(8,128)} fusion(bf16[512,3584]{1,0:T(8,128)(2,1)} %copy-done, bf16[1024,3584]{1,0:T(8,128)(2,1)} %all-gather.2.cloned.1.call-done), kind=kOutput, calls=%fused_computation.58 | convolution fusion | flops 3758096384 | bytes 13107200 | tf_op jit(solution)/shard_map/dot_general | solution.py:156
  229.8 3.0 collective-permute-start.17
  232.8 42.1 %reduce-scatter.2.cloned.1.call-done = f32[512,256]{1,0:T(8,128)} async-done(((f32[512,1024]{1,0:T(8,128)}), f32[512,256]{1,0:T(8,128)}) %reduce-scatter.2.cloned.1.call-update) | async-done | bytes 524304 | tf_op jit(solution)/shard_map/reduce_scatter | solution.py:166
  276.0 11.2 %collective-permute-start.18 = (bf16[128,512]{0,1:T(8,128)(2,1)S(1)}, bf16[128,512]{0,1:T(8,128)(2,1)S(1)}, u32[]{:S(2)}, u32[]{:S(2)}) collective-permute-start(bf16[128,512]{0,1:T(8,128)(2,1)S(1)} %get-tuple-element.69), channel_id=1, source_target_pairs={{0,4},{1,12},{2,20},{3,28},{4,0},{5,8},{6,16},{7,24},{8,5},{9,13},... | collective-permute-start | bytes 393224 | tf_op jit(solution)/shard_map/ppermute | solution.py:189
  289.1 2.6 collective-permute-done.18
  291.7 11.3 %collective-permute-done.19 = bf16[128,512]{0,1:T(8,128)(2,1)S(1)} collective-permute-done((bf16[128,512]{0,1:T(8,128)(2,1)S(1)}, bf16[128,512]{0,1:T(8,128)(2,1)S(1)}, u32[]{:S(2)}, u32[]{:S(2)}) %collective-permute-start.19) | collective-permute-done | bytes 131104 | tf_op jit(solution)/shard_map/ppermute | solution.py:189
  (86 shorter events, 28.0 us)
Async XLA Ops:
  10.3 21.9 %copy-start.1 = (bf16[256,3584]{1,0:T(8,128)(2,1)}, bf16[256,3584]{1,0:T(8,128)(2,1)S(1)}, u32[]{:S(2)}) copy-start(bf16[256,3584]{1,0:T(8,128)(2,1)S(1)} %fusion.12) | copy-start | bytes 5505028
  10.3 41.1 %collective-permute-start = (bf16[256,3584]{1,0:T(8,128)(2,1)S(1)}, bf16[256,3584]{1,0:T(8,128)(2,1)}, u32[]{:S(2)}, u32[]{:S(2)}) collective-permute-start(bf16[256,3584]{1,0:T(8,128)(2,1)S(1)} %fusion.12), channel_id=1, source_target_pairs={{0,8},{4,12},{8,0},{12,4},{16,24},{20,28},{24,16},{28,20},{1,9},{5... | collective-permute-start | bytes 5505032 | tf_op jit(solution)/shard_map/ppermute | solution.py:80
  10.4 41.1 %collective-permute-start.1 = (bf16[256,3584]{1,0:T(8,128)(2,1)S(1)}, bf16[256,3584]{1,0:T(8,128)(2,1)}, u32[]{:S(2)}, u32[]{:S(2)}) collective-permute-start(bf16[256,3584]{1,0:T(8,128)(2,1)S(1)} %fusion.12), channel_id=1, source_target_pairs={{0,16},{4,20},{8,24},{12,28},{16,0},{20,4},{24,8},{28,12},{1,17},{... | collective-permute-start | bytes 5505032 | tf_op jit(solution)/shard_map/ppermute | solution.py:80
  11.9 39.6 %collective-permute-start.2 = (bf16[256,3584]{1,0:T(8,128)(2,1)S(1)}, bf16[256,3584]{1,0:T(8,128)(2,1)}, u32[]{:S(2)}, u32[]{:S(2)}) collective-permute-start(bf16[256,3584]{1,0:T(8,128)(2,1)S(1)} %fusion.12), channel_id=1, source_target_pairs={{0,4},{4,0},{8,12},{12,8},{16,20},{20,16},{24,28},{28,24},{1,5},{5... | collective-permute-start | bytes 5505032 | tf_op jit(solution)/shard_map/ppermute | solution.py:80
  55.5 53.4 %all-to-all-start = ((bf16[8,512,256]{2,1,0:T(8,128)(2,1)}), bf16[8,512,256]{2,1,0:T(8,128)(2,1)S(1)}, u32[]{:S(2)}, u32[]{:S(2)}) async-start(bf16[8,512,256]{2,1,0:T(8,128)(2,1)} %bitcast.37), calls=%async_computation | async-start | bytes 4194304 | tf_op jit(solution)/shard_map/all_to_all | solution.py:134
  61.9 156.8 %all-gather.2.cloned.1.call-start = ((), (), s32[]{:S(2)}) async-start(), calls=%async_computation.3 | async-start | bytes 8257536 | tf_op jit(solution)/shard_map/all_gather | solution.py:161
  64.8 44.9 %collective-permute-start.3 = (bf16[256,3584]{1,0:T(8,128)(2,1)}, bf16[256,3584]{1,0:T(8,128)(2,1)}, u32[]{:S(2)}, u32[]{:S(2)}) collective-permute-start(bf16[256,3584]{1,0:T(8,128)(2,1)} %collective-permute-done), channel_id=1, source_target_pairs={{0,4},{4,0},{8,12},{12,8},{16,20},{20,16},{24,28},{28,24},{1,5},{5... | collective-permute-start | bytes 5505032 | tf_op jit(solution)/shard_map/ppermute | solution.py:80
  66.4 49.2 %collective-permute-start.4 = (bf16[256,3584]{1,0:T(8,128)(2,1)}, bf16[256,3584]{1,0:T(8,128)(2,1)}, u32[]{:S(2)}, u32[]{:S(2)}) collective-permute-start(bf16[256,3584]{1,0:T(8,128)(2,1)} %collective-permute-done.1), channel_id=1, source_target_pairs={{0,4},{4,0},{8,12},{12,8},{16,20},{20,16},{24,28},{28,24},{1,5},{5... | collective-permute-start | bytes 5505032 | tf_op jit(solution)/shard_map/ppermute | solution.py:80
  67.8 38.8 %collective-permute-start.5 = (bf16[128,3584]{1,0:T(8,128)(2,1)S(1)}, bf16[128,3584]{1,0:T(8,128)(2,1)S(1)}, u32[]{:S(2)}, u32[]{:S(2)}) collective-permute-start(bf16[128,3584]{1,0:T(8,128)(2,1)S(1)} %slice.25), channel_id=1, source_target_pairs={{0,16},{4,20},{8,24},{12,28},{16,0},{20,4},{24,8},{28,12},{1,17},{... | collective-permute-start | bytes 2752520 | tf_op jit(solution)/shard_map/ppermute | solution.py:80
  69.1 37.5 %collective-permute-start.6 = (bf16[128,3584]{1,0:T(8,128)(2,1)S(1)}, bf16[128,3584]{1,0:T(8,128)(2,1)S(1)}, u32[]{:S(2)}, u32[]{:S(2)}) collective-permute-start(bf16[128,3584]{1,0:T(8,128)(2,1)S(1)} %slice.26), channel_id=1, source_target_pairs={{0,8},{4,12},{8,0},{12,4},{16,24},{20,28},{24,16},{28,20},{1,9},{5... | collective-permute-start | bytes 2752520 | tf_op jit(solution)/shard_map/ppermute | solution.py:80
  108.5 12.0 %collective-permute-start.7 = (bf16[256,3584]{1,0:T(8,128)(2,1)}, bf16[256,3584]{1,0:T(8,128)(2,1)}, u32[]{:S(2)}, u32[]{:S(2)}) collective-permute-start(bf16[256,3584]{1,0:T(8,128)(2,1)} %pad_maximum_fusion), channel_id=1, source_target_pairs={{0,4},{4,0},{8,12},{12,8},{16,20},{20,16},{24,28},{28,24},{1,5},{5... | collective-permute-start | bytes 5505032 | tf_op jit(solution)/shard_map/ppermute | solution.py:80
  123.4 26.4 %collective-permute-start.8 = (bf16[128,3584]{1,0:T(8,128)(2,1)S(1)}, bf16[128,3584]{1,0:T(8,128)(2,1)S(1)}, u32[]{:S(2)}, u32[]{:S(2)}) collective-permute-start(bf16[128,3584]{1,0:T(8,128)(2,1)S(1)} %get-tuple-element.38), channel_id=1, source_target_pairs={{0,4},{4,0},{8,12},{12,8},{16,20},{20,16},{24,28},{28,24},{1,5},{5... | collective-permute-start | bytes 2752520 | tf_op jit(solution)/shard_map/ppermute | solution.py:80
  123.4 22.9 %collective-permute-start.9 = (bf16[128,3584]{1,0:T(8,128)(2,1)S(1)}, bf16[128,3584]{1,0:T(8,128)(2,1)S(1)}, u32[]{:S(2)}, u32[]{:S(2)}) collective-permute-start(bf16[128,3584]{1,0:T(8,128)(2,1)S(1)} %get-tuple-element.38), channel_id=1, source_target_pairs={{0,8},{4,12},{8,0},{12,4},{16,24},{20,28},{24,16},{28,20},{1,9},{5... | collective-permute-start | bytes 2752520 | tf_op jit(solution)/shard_map/ppermute | solution.py:80
  123.8 23.2 %collective-permute-start.11 = (bf16[128,3584]{1,0:T(8,128)(2,1)S(1)}, bf16[128,3584]{1,0:T(8,128)(2,1)S(1)}, u32[]{:S(2)}, u32[]{:S(2)}) collective-permute-start(bf16[128,3584]{1,0:T(8,128)(2,1)S(1)} %get-tuple-element.38), channel_id=1, source_target_pairs={{0,16},{4,20},{8,24},{12,28},{16,0},{20,4},{24,8},{28,12},{1,17},{... | collective-permute-start | bytes 2752520 | tf_op jit(solution)/shard_map/ppermute | solution.py:80
  146.4 11.0 %collective-permute-start.13 = (bf16[64,3584]{1,0:T(8,128)(2,1)S(1)}, bf16[64,3584]{1,0:T(8,128)(2,1)S(1)}, u32[]{:S(2)}, u32[]{:S(2)}) collective-permute-start(bf16[64,3584]{1,0:T(8,128)(2,1)S(1)} %slice.32), channel_id=1, source_target_pairs={{0,16},{4,20},{8,24},{12,28},{16,0},{20,4},{24,8},{28,12},{1,17},{... | collective-permute-start | bytes 1376264 | tf_op jit(solution)/shard_map/ppermute | solution.py:80
  147.0 10.8 %collective-permute-start.14 = (bf16[64,3584]{1,0:T(8,128)(2,1)S(1)}, bf16[64,3584]{1,0:T(8,128)(2,1)S(1)}, u32[]{:S(2)}, u32[]{:S(2)}) collective-permute-start(bf16[64,3584]{1,0:T(8,128)(2,1)S(1)} %slice.33), channel_id=1, source_target_pairs={{0,8},{4,12},{8,0},{12,4},{16,24},{20,28},{24,16},{28,20},{1,9},{5... | collective-permute-start | bytes 1376264 | tf_op jit(solution)/shard_map/ppermute | solution.py:80
  148.2 12.0 %collective-permute-start.10 = (bf16[128,3584]{1,0:T(8,128)(2,1)S(1)}, bf16[128,3584]{1,0:T(8,128)(2,1)S(1)}, u32[]{:S(2)}, u32[]{:S(2)}) collective-permute-start(bf16[128,3584]{1,0:T(8,128)(2,1)S(1)} %collective-permute-done.9), channel_id=1, source_target_pairs={{0,4},{4,0},{8,12},{12,8},{16,20},{20,16},{24,28},{28,24},{1,5},{5... | collective-permute-start | bytes 2752520 | tf_op jit(solution)/shard_map/ppermute | solution.py:80
  149.8 10.5 %collective-permute-start.12 = (bf16[128,3584]{1,0:T(8,128)(2,1)S(1)}, bf16[128,3584]{1,0:T(8,128)(2,1)S(1)}, u32[]{:S(2)}, u32[]{:S(2)}) collective-permute-start(bf16[128,3584]{1,0:T(8,128)(2,1)S(1)} %collective-permute-done.11), channel_id=1, source_target_pairs={{0,4},{4,0},{8,12},{12,8},{16,20},{20,16},{24,28},{28,24},{1,5},{5... | collective-permute-start | bytes 2752520 | tf_op jit(solution)/shard_map/ppermute | solution.py:80
  157.9 4.3 %collective-permute-start.15 = (bf16[128,3584]{1,0:T(8,128)(2,1)S(1)}, bf16[128,3584]{1,0:T(8,128)(2,1)S(1)}, u32[]{:S(2)}, u32[]{:S(2)}) collective-permute-start(bf16[128,3584]{1,0:T(8,128)(2,1)S(1)} %pad_maximum_fusion.1), channel_id=1, source_target_pairs={{0,4},{4,0},{8,12},{12,8},{16,20},{20,16},{24,28},{28,24},{1,5},{5... | collective-permute-start | bytes 2752520 | tf_op jit(solution)/shard_map/ppermute | solution.py:80
  166.3 108.5 %reduce-scatter.2.cloned.1.call-start = ((), (), s32[]{:S(2)}) async-start(), calls=%async_computation.4 | async-start | bytes 2621440 | tf_op jit(solution)/shard_map/reduce_scatter | solution.py:166
  228.5 60.6 %collective-permute-start.16 = (bf16[128,512]{0,1:T(8,128)(2,1)S(1)}, bf16[128,512]{0,1:T(8,128)(2,1)S(1)}, u32[]{:S(2)}, u32[]{:S(2)}) collective-permute-start(bf16[128,512]{0,1:T(8,128)(2,1)S(1)} %get-tuple-element.65), channel_id=1, source_target_pairs={{0,4},{1,12},{2,20},{3,28},{4,0},{5,8},{6,16},{7,24},{8,13},{9,5},... | collective-permute-start | bytes 393224 | tf_op jit(solution)/shard_map/ppermute | solution.py:189
  229.8 59.3 %collective-permute-start.17 = (bf16[128,512]{0,1:T(8,128)(2,1)S(1)}, bf16[128,512]{0,1:T(8,128)(2,1)S(1)}, u32[]{:S(2)}, u32[]{:S(2)}) collective-permute-start(bf16[128,512]{0,1:T(8,128)(2,1)S(1)} %get-tuple-element.64), channel_id=1, source_target_pairs={{0,0},{1,8},{2,16},{3,24},{4,4},{5,12},{6,20},{7,28},{8,9},{9,1},{... | collective-permute-start | bytes 393224 | tf_op jit(solution)/shard_map/ppermute | solution.py:189
  276.0 15.8 %collective-permute-start.18 = (bf16[128,512]{0,1:T(8,128)(2,1)S(1)}, bf16[128,512]{0,1:T(8,128)(2,1)S(1)}, u32[]{:S(2)}, u32[]{:S(2)}) collective-permute-start(bf16[128,512]{0,1:T(8,128)(2,1)S(1)} %get-tuple-element.69), channel_id=1, source_target_pairs={{0,4},{1,12},{2,20},{3,28},{4,0},{5,8},{6,16},{7,24},{8,5},{9,13},... | collective-permute-start | bytes 393224 | tf_op jit(solution)/shard_map/ppermute | solution.py:189
  287.2 15.9 %collective-permute-start.19 = (bf16[128,512]{0,1:T(8,128)(2,1)S(1)}, bf16[128,512]{0,1:T(8,128)(2,1)S(1)}, u32[]{:S(2)}, u32[]{:S(2)}) collective-permute-start(bf16[128,512]{0,1:T(8,128)(2,1)S(1)} %get-tuple-element.68), channel_id=1, source_target_pairs={{0,0},{1,8},{2,16},{3,24},{4,4},{5,12},{6,20},{7,28},{8,1},{9,9},{... | collective-permute-start | bytes 393224 | tf_op jit(solution)/shard_map/ppermute | solution.py:189
  (5 other events, 29.3 us)
Sparse Core Ops, SparseCore 0:
  166.5 50.9 all-gather.1
  228.4 46.3 reduce-scatter.1
